TPU v7x, 512 devices: a whole 4x4x16 slice. The times are simulated.
512 devices in a mesh: req: 128 (over y, z, core), tp: 4 (over x).
Axes of the slice: x: 4, y: 4, z: 16, core: 2. Of those that a mesh axis runs over, the one named last changes fastest.
Arguments:
- tokens: bfloat16 [131072, 3584], P('req', 'tp'), may hold values from -6 to 6
- key_value_weight: bfloat16 [3584, 1024], P('tp'), may hold values from -0.09375 to 0.09375
- adapter_down_maps: bfloat16 [128, 16, 3584], P('req', None, 'tp'), may hold values from -0.09375 to 0.09375
- adapter_up_maps: bfloat16 [128, 16, 1024], P('req', None, 'tp'), may hold values from -1.5 to 1.5
- block_adapter_ids: int32 [1024], P('req'), may hold values from 0 to 127, never falling along the last dimension, each value on 1 to 32 neighbouring positions
- block_live_rows: int32 [1024], P('req'), may hold values from 32 to 128
- adapter_storage_slot: int32 [128], replicated, may hold values from 0 to 127, each once
Outputs:
- keys_values: bfloat16 [131072, 1024], P('req', 'tp')
Inputs may be any that keep to these rules, and one draw needn't show every extreme that they name: `block_adapter_ids`: block ids never fall from one block to the next, every adapter id names at least one block, and one adapter names 32 blocks. `adapter_storage_slot`: each storage slot belongs to exactly one adapter.
All inputs are finite; a program needn't handle non-finite values.
Results may differ from a plain program's by a relative error of at most 0.003.
Values may be sent and summed in bfloat16 or wider, within the bound.
No kernel may reach another device: no remote copies, remote signals or barrier semaphores. Data moves between devices by JAX's collectives and lax.ppermute only.
A program may use at most 64 MiB of HBM per device.

v0:
```python
import jax
import jax.numpy as jnp
from jax import lax
from jax.sharding import PartitionSpec as P

adapter_scale = 0.5


def shards(
    tokens,
    key_value_weight,
    adapter_down_maps,
    adapter_up_maps,
    block_adapter_ids,
    block_live_rows,
    adapter_storage_slot,
):
    rows_dev, width_dev = tokens.shape
    blocks_dev = block_adapter_ids.shape[0]
    block_rows = rows_dev // blocks_dev
    local_columns = adapter_up_maps.shape[2]
    adapter_count = adapter_storage_slot.shape[0]
    matches = (
        block_adapter_ids[:, None] == jnp.arange(adapter_count, dtype=jnp.int32)[None, :]
    ).astype(jnp.int32)
    slot_ids = jnp.sum(matches * adapter_storage_slot[None, :], axis=1)
    pieces = (
        lax.all_gather(adapter_down_maps, "req", axis=0, tiled=True),
        lax.all_gather(adapter_up_maps, "req", axis=0, tiled=True),
    )
    piece_count = pieces[0].shape[0]
    chosen = (slot_ids[:, None] == jnp.arange(piece_count, dtype=jnp.int32)[None, :]).astype(
        jnp.bfloat16
    )
    a_part = jnp.einsum("bj,jrd->brd", chosen, pieces[0], preferred_element_type=jnp.float32)
    b_part = jnp.einsum("bj,jrc->brc", chosen, pieces[1], preferred_element_type=jnp.float32)
    chosen_down_maps = a_part.astype(jnp.bfloat16)
    chosen_up_maps = b_part.astype(jnp.bfloat16)
    features_all = lax.all_gather(tokens, "tp", axis=1, tiled=True)
    tp_index = lax.axis_index("tp")
    own_part = lax.dynamic_slice_in_dim(
        lax.all_gather(key_value_weight, "tp", axis=0, tiled=True),
        tp_index * local_columns,
        local_columns,
        1,
    )
    base_result = jnp.dot(features_all, own_part, preferred_element_type=jnp.float32)
    complete_down_maps = lax.all_gather(chosen_down_maps, "tp", axis=2, tiled=True)
    blocked_input = features_all.reshape(blocks_dev, block_rows, features_all.shape[1])
    rank_reduced = jnp.einsum(
        "qzo,qjo->qzj", blocked_input, complete_down_maps, preferred_element_type=jnp.float32
    )
    low_values = rank_reduced.astype(jnp.bfloat16)
    adapter_result = jnp.einsum(
        "bkr,brc->bkc", low_values, chosen_up_maps, preferred_element_type=jnp.float32
    ).reshape(rows_dev, local_columns)
    live_rows = (
        jnp.arange(block_rows, dtype=jnp.int32)[None, :] < block_live_rows[:, None]
    ).reshape(rows_dev, 1)
    adapted_output = base_result + adapter_scale * adapter_result
    return jnp.where(live_rows, adapted_output, jnp.zeros_like(adapted_output)).astype(jnp.bfloat16)


def solution(mesh):
    in_specs = (
        P("req", "tp"),
        P("tp", None),
        P("req", None, "tp"),
        P("req", None, "tp"),
        P("req"),
        P("req"),
        P(),
    )
    out_specs = P("req", "tp")
    return jax.shard_map(shards, mesh=mesh, in_specs=in_specs, out_specs=out_specs, check_vma=False)
```

profile of v0, /device:TPU:1, one launch (start us, length us, event | category | flops | bytes accessed | tf_op | source)
XLA Modules:
  0.0 465.4 jit_solution(3460865263811185851)
XLA Ops:
  6.5 0.0 all-gather.11.cloned.1.call-start
  6.5 0.7 all-gather.11.cloned.1.call-update
  7.3 0.0 all-gather.9.cloned.1.call-start
  7.3 0.7 all-gather.9.cloned.1.call-update
  8.0 0.0 all-gather.7.cloned.1.call-start
  8.1 0.7 all-gather.7.cloned.1.call-update
  8.7 0.0 all-gather.5.cloned.1.call-start
  8.8 0.5 all-gather.5.cloned.1.call-update
  9.3 0.9 select_reduce_fusion
  10.2 0.7 fusion.23
  10.9 136.2 %all-gather.11.cloned.1.call-done = bf16[128,16,256]{2,1,0:T(8,128)(2,1)} async-done(((bf16[1,16,256]{2,1,0:T(8,128)(2,1)}), bf16[128,16,256]{2,1,0:T(8,128)(2,1)}) %all-gather.11.cloned.1.call-update) | async-done | bytes 1048592 | tf_op jit(solution)/shard_map/all_gather | solution.py:29
  147.1 1.6 convolution_convert_fusion
  148.7 139.3 %all-gather.9.cloned.1.call-done = bf16[128,16,896]{2,1,0:T(8,128)(2,1)} async-done(((bf16[1,16,896]{2,1,0:T(8,128)(2,1)}), bf16[128,16,896]{2,1,0:T(8,128)(2,1)}) %all-gather.9.cloned.1.call-update) | async-done | bytes 3670032 | tf_op jit(solution)/shard_map/all_gather | solution.py:28
  287.9 3.0 fusion.16
  291.0 12.6 %all_gather.18 = bf16[8,16,3584]{2,0,1:T(8,128)(2,1)S(1)} all-gather(bf16[8,16,896]{2,0,1:T(8,128)(2,1)S(1)} %fusion.16), channel_id=1, replica_groups=mesh['req'=128,'tp'=4] {'tp'}, dimensions={2}, use_global_device_ids=true | all-gather | bytes 1146880 | tf_op jit(solution)/shard_map/all_gather | solution.py:48
  303.5 63.6 %all-gather.7.cloned.1.call-done = bf16[1024,3584]{1,0:T(8,128)(2,1)} async-done(((bf16[1024,896]{1,0:T(8,128)(2,1)}), bf16[1024,3584]{1,0:T(8,128)(2,1)}) %all-gather.7.cloned.1.call-update) | async-done | bytes 7340048 | tf_op jit(solution)/shard_map/all_gather | solution.py:39
  367.2 5.3 %convolution_multiply_fusion = f32[8,128,256]{2,1,0:T(8,128)S(1)} fusion(bf16[8,128,3584]{2,1,0:T(8,128)(2,1)} %bitcast.18, bf16[8,16,3584]{2,0,1:T(8,128)(2,1)S(1)} %all_gather.18, bf16[8,16,256]{2,0,1:T(8,128)(2,1)S(1)} %convolution_convert_fusion), kind=kOutput, calls=%fused_computation.5 | convolution fusion | flops 126107648 | bytes 9371648 | tf_op jit(solution)/shard_map/bkr,brc->bkc/dot_general | solution.py:54
  372.5 0.3 copy.18
  372.8 79.2 %all-gather.5.cloned.1.call-done = bf16[3584,1024]{1,0:T(8,128)(2,1)} async-done(((bf16[896,1024]{1,0:T(8,128)(2,1)}), bf16[3584,1024]{1,0:T(8,128)(2,1)}) %all-gather.5.cloned.1.call-update) | async-done | bytes 7340048 | tf_op jit(solution)/shard_map/all_gather | solution.py:42
  452.0 5.8 %fusion.13 = bf16[1024,256]{0,1:T(8,128)(2,1)S(1)} fusion(f32[1024,256]{0,1:T(8,128)S(1)} %copy.18, bf16[1024,3584]{1,0:T(8,128)(2,1)} %all-gather.7.cloned.1.call-done, bf16[3584,1024]{1,0:T(8,128)(2,1)} %all-gather.5.cloned.1.call-done, s32[]{:T(128)S(6)} %select_n.7, pred[1024]{0:T(1024)(128)(4,1)S(1)} %fusion.23), kind=kOutput, calls=%fused_computation.8 | convolution fusion | flops 1879834624 | bytes 10748932 | tf_op jit(solution)/shard_map/dot_general | solution.py:47
  457.8 1.0 copy.17
Async XLA Ops:
  6.5 140.5 %all-gather.11.cloned.1.call-start = ((), (), s32[]{:S(2)}) async-start(), calls=%async_computation.3 | async-start | bytes 1056768 | tf_op jit(solution)/shard_map/all_gather | solution.py:29
  7.3 280.7 %all-gather.9.cloned.1.call-start = ((), (), s32[]{:S(2)}) async-start(), calls=%async_computation.2 | async-start | bytes 3698688 | tf_op jit(solution)/shard_map/all_gather | solution.py:28
  8.0 359.1 %all-gather.7.cloned.1.call-start = ((), (), s32[]{:S(2)}) async-start(), calls=%async_computation.1 | async-start | bytes 9175040 | tf_op jit(solution)/shard_map/all_gather | solution.py:39
  8.7 443.3 %all-gather.5.cloned.1.call-start = ((), (), s32[]{:S(2)}) async-start(), calls=%async_computation | async-start | bytes 9175040 | tf_op jit(solution)/shard_map/all_gather | solution.py:42
Sparse Core Ops, SparseCore 0:
  10.3 136.7 all-gather.10
  150.1 137.7 all-gather.8
  290.1 77.0 all-gather.6
  369.1 82.8 all-gather.4
where the time goes:
time: 466 us; the launch traced here: 465 us
  waiting for transfers between devices  421 us (90%)
  matrix products  15.7 us (3%)
  between operations  13.2 us (3%)
  blocking collectives  12.6 us (3%)
    all_gather x1, waiting for transfers between devices, shards(): lax.all_gather(adapter_down_maps, 'req', axis=0, tiled=True)  139 us
    all_gather x1, waiting for transfers between devices, shards(): lax.all_gather(adapter_up_maps, 'req', axis=0, tiled=True)  136 us
    all_gather x1, waiting for transfers between devices, shards(): lax.all_gather(key_value_weight, 'tp', axis=0, tiled=True)  79.2 us
    all_gather x1, waiting for transfers between devices, shards(): features_all = lax.all_gather(tokens, 'tp', axis=1, tiled=True)  63.6 us
    all_gather x1, blocking collectives, shards(): lax.all_gather(chosen_down_maps, 'tp', axis=2, tiled=True)  12.6 us
  transfers between devices with their start and end apart: 4, of which 4 were waited for; matrix products, arithmetic and copies ran while one was open for 3% of the time, Pallas kernels for 0%

commit v1 on v0

v1 whole, which is shorter than its diff:
```python
import jax
import jax.numpy as jnp
from jax import lax
from jax.sharding import PartitionSpec as P

adapter_scale = 0.5


def shards(
    tokens,
    key_value_weight,
    adapter_down_maps,
    adapter_up_maps,
    block_adapter_ids,
    block_live_rows,
    adapter_storage_slot,
):
    rows_dev, width_dev = tokens.shape
    blocks_dev = block_adapter_ids.shape[0]
    block_rows = rows_dev // blocks_dev
    rank = adapter_down_maps.shape[1]
    local_columns = adapter_up_maps.shape[2]
    tp_size = key_value_weight.shape[1] // local_columns

    slot_ids = adapter_storage_slot[block_adapter_ids]

    both_maps = jnp.concatenate([adapter_down_maps, adapter_up_maps], axis=2)
    all_maps = lax.all_gather(both_maps, "req", axis=0, tiled=True)
    chosen_maps = all_maps[slot_ids]
    chosen_down_maps = chosen_maps[:, :, :width_dev]
    chosen_up_maps = chosen_maps[:, :, width_dev:]

    base_partial = jnp.dot(tokens, key_value_weight, preferred_element_type=jnp.float32)
    blocked_input = tokens.reshape(blocks_dev, block_rows, width_dev)
    shrunk_partial = jnp.einsum(
        "qzo,qjo->qzj", blocked_input, chosen_down_maps, preferred_element_type=jnp.float32
    ).reshape(rows_dev, rank)
    payload = jnp.concatenate(
        [
            base_partial.reshape(rows_dev, tp_size, local_columns).transpose(1, 0, 2),
            jnp.broadcast_to(shrunk_partial[None], (tp_size, rows_dev, rank)),
        ],
        axis=2,
    )
    summed = lax.psum_scatter(payload, "tp", scatter_dimension=0, tiled=False)
    base_result = summed[:, :local_columns]
    low_values = summed[:, local_columns:].astype(jnp.bfloat16)

    adapter_result = jnp.einsum(
        "bkr,brc->bkc",
        low_values.reshape(blocks_dev, block_rows, rank),
        chosen_up_maps,
        preferred_element_type=jnp.float32,
    ).reshape(rows_dev, local_columns)
    live_rows = (
        jnp.arange(block_rows, dtype=jnp.int32)[None, :] < block_live_rows[:, None]
    ).reshape(rows_dev, 1)
    adapted_output = base_result + adapter_scale * adapter_result
    return jnp.where(live_rows, adapted_output, jnp.zeros_like(adapted_output)).astype(jnp.bfloat16)


def solution(mesh):
    in_specs = (
        P("req", "tp"),
        P("tp", None),
        P("req", None, "tp"),
        P("req", None, "tp"),
        P("req"),
        P("req"),
        P(),
    )
    out_specs = P("req", "tp")
    return jax.shard_map(shards, mesh=mesh, in_specs=in_specs, out_specs=out_specs, check_vma=False)
```

time: 466 us -> 245 us (0.53)
  waiting for transfers between devices: 421 us -> 205 us
  blocking collectives: 12.6 us -> 0 us
  local copies, waits for them, and re-layouts: 1.33 us -> 11.3 us
  matrix products: 15.7 us -> 6.85 us
  other arithmetic: 1.58 us -> 7.95 us
    all_gather x4 -> x1, waiting for transfers between devices: 418 us -> 139 us  [shards(): all_maps = lax.all_gather(both_maps, 'req', axis=0, tiled=True)]
    reduce_scatter x0 -> x1, waiting for transfers between devices: none -> 66 us  [shards(): summed = lax.psum_scatter(payload, 'tp', scatter_dimension=0, tiled=False)]
    all_gather x1 -> x0, blocking collectives: 12.6 us -> none  [shards(): lax.all_gather(chosen_down_maps, 'tp', axis=2, tiled=True)]
    dot_general x4 -> x3, matrix products: 15.7 us -> 6.85 us  [the longest x1 5.94 us: shards(): jnp.dot(tokens, key_value_weight, preferred_element_type=jnp.float32)]
    concatenate x0 -> x2, other arithmetic: none -> 6.85 us  [the longest x1 5.33 us: shards(): jnp.concatenate([base_partial.reshape(rows_dev, tp_size, local_columns).t...]
    reshape x0 -> x1, local copies, waits for them, and re-layouts: none -> 5.42 us  [shards(): base_partial.reshape(rows_dev, tp_size, local_columns).transpose(1, 0, 2)]
  transfers between devices with their start and end apart: 4 -> 2, of which waited for: 4 -> 2; matrix products, arithmetic and copies ran while one was open for 3% -> 5% of each run, Pallas kernels for 0% -> 0%
where the time goes in v1:
time: 245 us; the launch traced here: 244 us
  waiting for transfers between devices  205 us (84%)
  between operations  13.5 us (6%)
  local copies, waits for them, and re-layouts  11.3 us (5%)
  other arithmetic  7.95 us (3%)
  matrix products  6.85 us (3%)
    all_gather x1, waiting for transfers between devices, shards(): all_maps = lax.all_gather(both_maps, 'req', axis=0, tiled=True)  139 us
    reduce_scatter x1, waiting for transfers between devices, shards(): summed = lax.psum_scatter(payload, 'tp', scatter_dimension=0, tiled=False)  66 us
    dot_general x1, matrix products, shards(): jnp.dot(tokens, key_value_weight, preferred_element_type=jnp.float32)  5.94 us
    reshape x1, local copies, waits for them, and re-layouts, shards(): base_partial.reshape(rows_dev, tp_size, local_columns).transpose(1, 0, 2)  5.42 us
    concatenate x1, other arithmetic, shards(): jnp.concatenate([base_partial.reshape(rows_dev, tp_size, local_columns).t...  5.33 us
  transfers between devices with their start and end apart: 2, of which 2 were waited for; matrix products, arithmetic and copies ran while one was open for 5% of the time, Pallas kernels for 0%

profile of v1, /device:TPU:1, one launch (start us, length us, event | category | flops | bytes accessed | tf_op | source)
XLA Modules:
  0.0 244.2 jit_solution(13733681826843781190)
XLA Ops:
  6.5 0.0 copy-start
  6.5 0.0 all-gather.2.cloned.1.call-start
  6.5 1.5 pad_maximum_fusion.1
  8.1 0.0 all-gather.2.cloned.1.call-update
  8.1 0.0 reduce-scatter.2.cloned.1.call-start
  8.1 0.0 copy-done
  8.1 5.9 %fusion.6 = f32[1024,1024]{0,1:T(8,128)} fusion(bf16[1024,896]{1,0:T(8,128)(2,1)S(1)} %copy-done, bf16[896,1024]{1,0:T(8,128)(2,1)} %param.8), kind=kOutput, calls=%fused_computation.19 | convolution fusion | flops 1879048192 | bytes 7864320 | tf_op jit(solution)/shard_map/dot_general | solution.py:33
  14.1 0.0 copy-start.3
  14.1 0.0 copy-start.1
  14.1 5.4 %copy.14 = f32[1024,4,256]{2,0,1:T(8,128)} copy(f32[1024,4,256]{0,2,1:T(8,128)} %bitcast.22) | data formatting | bytes 8388608 | tf_op jit(solution)/shard_map/reshape | solution.py:40
  19.5 0.0 copy-done.3
  19.5 0.0 copy-done.1
  19.5 0.6 gather_fusion
  20.2 138.6 %all-gather.2.cloned.1.call-done = bf16[128,16,1152]{2,1,0:T(8,128)(2,1)} async-done(((bf16[1,16,1152]{2,1,0:T(8,128)(2,1)}), bf16[128,16,1152]{2,1,0:T(8,128)(2,1)}) %all-gather.2.cloned.1.call-update) | async-done | bytes 4718608 | tf_op jit(solution)/shard_map/all_gather | solution.py:28
  158.8 2.9 %gather_fusion.1 = bf16[8,16,1152]{2,1,0:T(8,128)(2,1)S(1)} fusion(bf16[128,16,1152]{2,1,0:T(8,128)(2,1)} %all-gather.2.cloned.1.call-done, s32[1024]{0:T(1024)S(1)} %pad_clamp_fusion), kind=kCustom, calls=%fused_computation.1 | custom fusion | bytes 589856 | tf_op jit(solution)/shard_map/gather | solution.py:29
  161.7 0.6 convolution_bitcast_fusion
  162.3 0.2 copy.19
  162.6 0.1 broadcast_in_dim.27
  162.7 5.3 %pad_maximum_fusion = f32[4,1024,272]{2,1,0:T(8,128)} fusion(f32[4,1024,16]{2,1,0:T(8,128)S(1)} %broadcast_in_dim.27, f32[4,1024,256]{2,1,0:T(8,128)} %bitcast.21), kind=kLoop, calls=%fused_computation.2 | loop fusion | flops 1114112 | bytes 8912896 | tf_op jit(solution)/shard_map/concatenate | solution.py:38
  168.0 0.0 copy-start.4
  168.0 0.0 reduce-scatter.2.cloned.1.call-update
  168.1 0.6 copy-done.4
  168.7 0.1 fusion.4
  168.8 66.0 %reduce-scatter.2.cloned.1.call-done = f32[1,1024,272]{2,1,0:T(8,128)} async-done(((f32[4,1024,272]{2,1,0:T(8,128)}), f32[1,1024,272]{2,1,0:T(8,128)}) %reduce-scatter.2.cloned.1.call-update) | async-done | bytes 1114128 | tf_op jit(solution)/shard_map/reduce_scatter | solution.py:45
  234.8 0.0 copy-start.2
  234.8 1.2 slice.35
  236.0 0.3 convolution_multiply_fusion
  236.3 0.1 copy-done.2
  236.4 1.0 fusion.1
  (4 shorter events, 0.0 us)
Async XLA Ops:
  6.5 1.6 copy-start
  6.5 152.2 %all-gather.2.cloned.1.call-start = ((), (), s32[]{:S(2)}) async-start(), calls=%async_computation.1 | async-start | bytes 4755456 | tf_op jit(solution)/shard_map/all_gather | solution.py:28
  8.1 226.7 %reduce-scatter.2.cloned.1.call-start = ((), (), s32[]{:S(2)}) async-start(), calls=%async_computation.2 | async-start | bytes 7864320 | tf_op jit(solution)/shard_map/reduce_scatter | solution.py:45
  14.1 5.4 %copy-start.3 = (s32[8]{0:T(128)S(1)}, s32[8]{0:T(128)}, u32[]{:S(2)}) copy-start(s32[8]{0:T(128)} %param.11) | copy-start | bytes 100
  14.1 5.4 %copy-start.1 = (s32[128]{0:T(128)S(1)}, s32[128]{0:T(128)}, u32[]{:S(2)}) copy-start(s32[128]{0:T(128)} %param.13) | copy-start | bytes 1540
  168.0 0.7 copy-start.4
  234.8 1.6 copy-start.2
Sparse Core Ops, SparseCore 0:
  10.4 148.3 all-gather.1
  168.2 66.5 reduce-scatter.1

commit v2 on v1

v2 whole, which is shorter than its diff:
```python
import numpy as np

import jax
import jax.numpy as jnp
from jax import lax
from jax.sharding import Mesh
from jax.sharding import PartitionSpec as P

adapter_scale = 0.5
ROWS = ("y", "z", "c")


def pick_entries(table, wanted, own_row, per_row, per_column):
    row_of = wanted // per_row
    inside = wanted % per_row
    entries = table[inside % per_column, inside // per_column]
    keep = (row_of == own_row)[:, None, None]
    return jnp.where(keep, entries, jnp.zeros_like(entries))


def shards(
    tokens,
    key_value_weight,
    adapter_down_maps,
    adapter_up_maps,
    block_adapter_ids,
    block_live_rows,
    adapter_storage_slot,
):
    rows_dev, width_dev = tokens.shape
    blocks_dev = block_adapter_ids.shape[0]
    block_rows = rows_dev // blocks_dev
    rank = adapter_down_maps.shape[1]
    local_columns = adapter_up_maps.shape[2]
    tp_size = key_value_weight.shape[1] // local_columns
    y_size = lax.axis_size("y")
    per_column = lax.axis_size("c")
    per_row = lax.axis_size("z") * per_column

    slot_ids = adapter_storage_slot[block_adapter_ids]
    my_row = lax.axis_index("y")

    base_partial = jnp.dot(tokens, key_value_weight, preferred_element_type=jnp.float32)
    outgoing = base_partial.reshape(rows_dev, tp_size, local_columns).transpose(1, 0, 2)
    incoming = lax.all_to_all(outgoing, "tp", 0, 0, tiled=False)
    base_result = jnp.sum(incoming, axis=0)

    both_maps = jnp.concatenate([adapter_down_maps, adapter_up_maps], axis=2)
    column = lax.all_gather(both_maps, "z", axis=0, tiled=True)
    row_table = lax.all_gather(column, "c", axis=0, tiled=False)
    chosen_maps = pick_entries(row_table, slot_ids, my_row, per_row, per_column)
    for shift in range(1, y_size):
        their_ids = lax.ppermute(
            slot_ids, "y", [(i, (i - shift) % y_size) for i in range(y_size)]
        )
        sent = pick_entries(row_table, their_ids, my_row, per_row, per_column)
        chosen_maps = chosen_maps + lax.ppermute(
            sent, "y", [(i, (i + shift) % y_size) for i in range(y_size)]
        )
    chosen_down_maps = chosen_maps[:, :, :width_dev]
    chosen_up_maps = chosen_maps[:, :, width_dev:]

    blocked_input = tokens.reshape(blocks_dev, block_rows, width_dev)
    shrunk_partial = jnp.einsum(
        "qzo,qjo->qzj", blocked_input, chosen_down_maps, preferred_element_type=jnp.float32
    ).reshape(rows_dev, rank)
    shrunk = jnp.sum(lax.all_gather(shrunk_partial, "tp", axis=0, tiled=False), axis=0)
    low_values = shrunk.astype(jnp.bfloat16)

    adapter_result = jnp.einsum(
        "bkr,brc->bkc",
        low_values.reshape(blocks_dev, block_rows, rank),
        chosen_up_maps,
        preferred_element_type=jnp.float32,
    ).reshape(rows_dev, local_columns)
    live_rows = (
        jnp.arange(block_rows, dtype=jnp.int32)[None, :] < block_live_rows[:, None]
    ).reshape(rows_dev, 1)
    adapted_output = base_result + adapter_scale * adapter_result
    return jnp.where(live_rows, adapted_output, jnp.zeros_like(adapted_output)).astype(jnp.bfloat16)


def split_mesh(mesh):
    devices = np.asarray(mesh.devices)
    first = devices[:, 0]
    y_size = len({d.coords[1] for d in first})
    z_size = len({d.coords[2] for d in first})
    c_size = len({d.core_on_chip for d in first})
    split = devices.reshape(y_size, z_size, c_size, devices.shape[1])
    for (yi, zi, ci), d in np.ndenumerate(split[:, :, :, 0]):
        assert (d.coords[1], d.coords[2], d.core_on_chip) == (
            sorted({e.coords[1] for e in first})[yi],
            sorted({e.coords[2] for e in first})[zi],
            sorted({e.core_on_chip for e in first})[ci],
        )
    return Mesh(split, ROWS + ("tp",))


def solution(mesh):
    in_specs = (
        P(ROWS, "tp"),
        P("tp", None),
        P(ROWS, None, "tp"),
        P(ROWS, None, "tp"),
        P(ROWS),
        P(ROWS),
        P(),
    )
    out_specs = P(ROWS, "tp")
    return jax.shard_map(
        shards, mesh=split_mesh(mesh), in_specs=in_specs, out_specs=out_specs, check_vma=False
    )
```

time: 245 us -> 146 us (0.60)
  waiting for transfers between devices: 205 us -> 32.7 us
  blocking collectives: 0 us -> 46.1 us
  starting transfers between devices: 0.04 us -> 24.8 us
    all_gather x1, waiting for transfers between devices: 139 us -> 20.9 us  [shards(): row_table = lax.all_gather(column, 'c', axis=0, tiled=False)]
    reduce_scatter x1 -> x0, waiting for transfers between devices: 66 us -> none  [shards(): summed = lax.psum_scatter(payload, 'tp', scatter_dimension=0, tiled=False)]
    all_gather x0 -> x2, blocking collectives: none -> 46.1 us  [the longest x1 36 us: shards(): column = lax.all_gather(both_maps, 'z', axis=0, tiled=True)]
    ppermute x0 -> x6, starting transfers between devices: none -> 19.8 us  [the longest x3 11.5 us: shards(): lax.ppermute(slot_ids, 'y', [(i, (i - shift) % y_size) for i in range(y_s...]
    ppermute x0 -> x6, waiting for transfers between devices: none -> 11.9 us  [the longest x3 11.8 us: shards(): lax.ppermute(sent, 'y', [(i, (i + shift) % y_size) for i in range(y_size)])]
    reshape x1 -> x0, local copies, waits for them, and re-layouts: 5.42 us -> none  [shards(): base_partial.reshape(rows_dev, tp_size, local_columns).transpose(1, 0, 2)]
    concatenate x1 -> x4, other arithmetic: 5.33 us -> 0.09 us  [pick_entries(): entries = table[inside % per_column, inside // per_column]]
    all_to_all x0 -> x1, starting transfers between devices: none -> 4.97 us  [shards(): incoming = lax.all_to_all(outgoing, 'tp', 0, 0, tiled=False)]
  transfers between devices with their start and end apart: 2 -> 8, of which waited for: 2 -> 3; matrix products, arithmetic and copies ran while one was open for 5% -> 13% of each run, Pallas kernels for 0% -> 0%
where the time goes in v2:
time: 146 us; the launch traced here: 144 us
  blocking collectives  46.1 us (32%)
  waiting for transfers between devices  32.7 us (22%)
  starting transfers between devices  24.8 us (17%)
  between operations  13.6 us (9%)
  other arithmetic  9.95 us (7%)
  local copies, waits for them, and re-layouts  8.94 us (6%)
  matrix products  7.91 us (5%)
    all_gather x1, blocking collectives, shards(): column = lax.all_gather(both_maps, 'z', axis=0, tiled=True)  36 us
    all_gather x1, waiting for transfers between devices, shards(): row_table = lax.all_gather(column, 'c', axis=0, tiled=False)  20.9 us
    ppermute x3, waiting for transfers between devices, shards(): lax.ppermute(sent, 'y', [(i, (i + shift) % y_size) for i in range(y_size)])  11.8 us
    ppermute x3, starting transfers between devices, shards(): lax.ppermute(slot_ids, 'y', [(i, (i - shift) % y_size) for i in range(y_s...  11.5 us
    all_gather x1, blocking collectives, shards(): lax.all_gather(shrunk_partial, 'tp', axis=0, tiled=False)  10.1 us
    ppermute x3, starting transfers between devices, shards(): lax.ppermute(sent, 'y', [(i, (i + shift) % y_size) for i in range(y_size)])  8.29 us
    dot_general x1, matrix products, shards(): jnp.dot(tokens, key_value_weight, preferred_element_type=jnp.float32)  5.86 us
    gather x4, local copies, waits for them, and re-layouts, pick_entries(): entries = table[inside % per_column, inside // per_column]  5.02 us
  transfers between devices with their start and end apart: 8, of which 3 were waited for; matrix products, arithmetic and copies ran while one was open for 13% of the time, Pallas kernels for 0%

profile of v2, /device:TPU:1, one launch (start us, length us, event | category | flops | bytes accessed | tf_op | source)
XLA Modules:
  0.0 144.1 jit_solution(14350227295226438584)
XLA Ops:
  6.5 0.0 copy-start
  6.5 0.8 compare_select_fusion.8
  7.3 1.3 gather_fusion
  8.6 4.0 %collective-permute-start.4 = (s32[8]{0:T(128)S(1)}, s32[8]{0:T(128)S(1)}, u32[]{:S(2)}, u32[]{:S(2)}) collective-permute-start(s32[8]{0:T(128)S(1)} %gather_fusion), channel_id=1, source_target_pairs={{0,128},{128,256},{256,384},{384,0},{1,129},{129,257},{257,385},{3... | collective-permute-start | bytes 104 | tf_op jit(solution)/shard_map/ppermute | solution.py:53
  12.7 4.5 %collective-permute-start.2 = (s32[8]{0:T(128)S(1)}, s32[8]{0:T(128)S(1)}, u32[]{:S(2)}, u32[]{:S(2)}) collective-permute-start(s32[8]{0:T(128)S(1)} %gather_fusion), channel_id=1, source_target_pairs={{0,256},{128,384},{256,0},{384,128},{1,257},{129,385},{257,1},{385... | collective-permute-start | bytes 104 | tf_op jit(solution)/shard_map/ppermute | solution.py:53
  17.2 3.0 %collective-permute-start = (s32[8]{0:T(128)S(1)}, s32[8]{0:T(128)S(1)}, u32[]{:S(2)}, u32[]{:S(2)}) collective-permute-start(s32[8]{0:T(128)S(1)} %gather_fusion), channel_id=1, source_target_pairs={{0,384},{128,0},{256,128},{384,256},{1,385},{129,1},{257,129},{385... | collective-permute-start | bytes 104 | tf_op jit(solution)/shard_map/ppermute | solution.py:53
  20.2 0.0 copy-done
  20.2 5.9 %fusion.31 = f32[1024,1024]{0,1:T(8,128)} fusion(bf16[1024,896]{1,0:T(8,128)(2,1)S(1)} %copy-done, bf16[896,1024]{1,0:T(8,128)(2,1)} %param.8), kind=kOutput, calls=%fused_computation.98 | convolution fusion | flops 1879048192 | bytes 7864320 | tf_op jit(solution)/shard_map/dot_general | solution.py:43
  26.0 0.0 copy-start.2
  26.1 0.0 copy-start.3
  26.1 5.0 %all-to-all-start = ((f32[4,1024,256]{1,2,0:T(8,128)}), f32[4,1024,256]{1,2,0:T(8,128)}, u32[]{:S(2)}, u32[]{:S(2)}) async-start(f32[4,1024,256]{1,2,0:T(8,128)} %bitcast.31), calls=%async_computation | async-start | bytes 8388608 | tf_op jit(solution)/shard_map/all_to_all | solution.py:45
  31.0 0.0 all-gather.3.cloned.1.call-start
  31.1 0.0 copy-done.2
  31.1 0.0 copy-done.3
  31.1 36.0 %all_gather.12 = bf16[16,16,1152]{2,1,0:T(8,128)(2,1)} all-gather(bf16[1,16,1152]{2,1,0:T(8,128)(2,1)S(1)} %pad_maximum_fusion), channel_id=1, replica_groups=mesh['y'=4,'z'=16,'c'=2,'tp'=4] {'z'}, dimensions={0}, use_global_device_ids=true | all-gather | bytes 626688 | tf_op jit(solution)/shard_map/all_gather | solution.py:49
  67.1 0.0 all-gather.3.cloned.1.call-update
  67.1 0.0 copy-start.4
  67.2 0.0 collective-permute-done.4
  67.2 0.0 collective-permute-done.2
  67.3 0.0 collective-permute-done
  67.3 20.9 %all-gather.3.cloned.1.call-done = bf16[32,16,1152]{2,1,0:T(8,128)(2,1)} async-done(((bf16[16,16,1152]{2,1,0:T(8,128)(2,1)}), bf16[32,16,1152]{2,1,0:T(8,128)(2,1)}) %all-gather.3.cloned.1.call-update) | async-done | bytes 1179664 | tf_op jit(solution)/shard_map/all_gather | solution.py:50
  88.2 0.0 copy-start.1
  88.2 2.0 %gather_fusion.4 = bf16[8,16,1152]{2,1,0:T(8,128)(2,1)S(1)} fusion(bf16[2,16,16,1152]{3,2,1,0:T(8,128)(2,1)} %bitcast.33, s32[8]{0:T(128)S(1)} %fusion.23), kind=kCustom, calls=%fused_computation.4 | custom fusion | bytes 589888 | tf_op jit(solution)/shard_map/gather | solution.py:16
  90.2 0.8 broadcast_select_fusion
  91.0 3.4 %collective-permute-start.5 = (bf16[8,16,1152]{2,1,0:T(8,128)(2,1)}, bf16[8,16,1152]{2,1,0:T(8,128)(2,1)}, u32[]{:S(2)}, u32[]{:S(2)}) collective-permute-start(bf16[8,16,1152]{2,1,0:T(8,128)(2,1)} %broadcast_select_fusion), channel_id=1, source_target_pairs={{0,384},{128,0},{256,128},{384,256},{1,385},{129,1},{257,129},{385... | collective-permute-start | bytes 884744 | tf_op jit(solution)/shard_map/ppermute | solution.py:57
  94.4 1.9 %gather_fusion.3 = bf16[8,16,1152]{2,1,0:T(8,128)(2,1)S(1)} fusion(bf16[2,16,16,1152]{3,2,1,0:T(8,128)(2,1)} %bitcast.34, s32[8]{0:T(128)S(1)} %fusion.18), kind=kCustom, calls=%fused_computation.3 | custom fusion | bytes 589888 | tf_op jit(solution)/shard_map/gather | solution.py:16
  96.2 0.8 broadcast_select_fusion.1
  97.1 2.4 %collective-permute-start.3 = (bf16[8,16,1152]{2,1,0:T(8,128)(2,1)}, bf16[8,16,1152]{2,1,0:T(8,128)(2,1)}, u32[]{:S(2)}, u32[]{:S(2)}) collective-permute-start(bf16[8,16,1152]{2,1,0:T(8,128)(2,1)} %broadcast_select_fusion.1), channel_id=1, source_target_pairs={{0,256},{128,384},{256,0},{384,128},{1,257},{129,385},{257,1},{385... | collective-permute-start | bytes 884744 | tf_op jit(solution)/shard_map/ppermute | solution.py:57
  99.5 0.0 copy-done.1
  99.5 0.6 gather_fusion.2
  100.1 0.8 broadcast_select_fusion.2
  101.0 2.5 %collective-permute-start.1 = (bf16[8,16,1152]{2,1,0:T(8,128)(2,1)}, bf16[8,16,1152]{2,1,0:T(8,128)(2,1)}, u32[]{:S(2)}, u32[]{:S(2)}) collective-permute-start(bf16[8,16,1152]{2,1,0:T(8,128)(2,1)} %broadcast_select_fusion.2), channel_id=1, source_target_pairs={{0,128},{128,256},{256,384},{384,0},{1,129},{129,257},{257,385},{3... | collective-permute-start | bytes 884744 | tf_op jit(solution)/shard_map/ppermute | solution.py:57
  103.5 0.0 copy-done.4
  103.5 0.1 fusion.4
  103.6 0.6 gather_fusion.1
  104.2 0.0 collective-permute-done.5
  104.2 4.7 %collective-permute-done.3 = bf16[8,16,1152]{2,1,0:T(8,128)(2,1)} collective-permute-done((bf16[8,16,1152]{2,1,0:T(8,128)(2,1)}, bf16[8,16,1152]{2,1,0:T(8,128)(2,1)}, u32[]{:S(2)}, u32[]{:S(2)}) %collective-permute-start.3) | collective-permute-done | bytes 294944 | tf_op jit(solution)/shard_map/ppermute | solution.py:57
  108.9 7.1 %collective-permute-done.1 = bf16[8,16,1152]{2,1,0:T(8,128)(2,1)} collective-permute-done((bf16[8,16,1152]{2,1,0:T(8,128)(2,1)}, bf16[8,16,1152]{2,1,0:T(8,128)(2,1)}, u32[]{:S(2)}, u32[]{:S(2)}) %collective-permute-start.1) | collective-permute-done | bytes 294944 | tf_op jit(solution)/shard_map/ppermute | solution.py:57
  116.0 1.3 add_add_fusion
  117.3 0.6 convolution_bitcast_fusion
  118.0 10.1 %all_gather.15 = f32[4,1024,16]{1,2,0:T(8,128)S(1)} all-gather(f32[1,1024,16]{1,2,0:T(8,128)S(1)} %all_gather_reshape.3), channel_id=1, replica_groups=mesh['y'=4,'z'=16,'c'=2,'tp'=4] {'tp'}, dimensions={0}, use_global_device_ids=true | all-gather | bytes 327680 | tf_op jit(solution)/shard_map/all_gather | solution.py:67
  128.1 1.4 convolution_multiply_fusion
  129.5 1.6 %copy.12 = f32[1024,256]{0,1:T(8,128)S(1)} copy(f32[1024,256]{1,0:T(8,128)} %bitcast.32) | data formatting | bytes 2097152 | tf_op jit(solution)/shard_map/mul | solution.py:79
  131.1 0.0 all-to-all-done
  131.1 3.7 %reduce_sum.18 = f32[1024,256]{0,1:T(8,128)} reduce(f32[4,1024,256]{1,2,0:T(8,128)} %all-to-all-done, f32[]{:T(128)} %constant.123.clone.1), dimensions={0}, to_apply=%region_0.0 | reduce | flops 786432 | bytes 5242884 | tf_op jit(solution)/shard_map/reduce_sum | solution.py:46
  134.8 1.5 %select_convert_fusion = bf16[1024,256]{0,1:T(8,128)(2,1)S(1)} fusion(f32[1024,256]{0,1:T(8,128)} %reduce_sum.18, f32[1024,256]{0,1:T(8,128)S(1)} %copy.12, pred[1024]{0:T(1024)(128)(4,1)S(1)} %fusion.4), kind=kLoop, calls=%fused_computation.7 | loop fusion | flops 786432 | bytes 2622464 | tf_op jit(solution)/shard_map/convert_element_type | solution.py:80
  136.3 1.0 copy.13
  (13 shorter events, 0.2 us)
Async XLA Ops:
  6.5 13.6 %copy-start = (bf16[1024,896]{1,0:T(8,128)(2,1)S(1)}, bf16[1024,896]{1,0:T(8,128)(2,1)}, u32[]{:S(2)}) copy-start(bf16[1024,896]{1,0:T(8,128)(2,1)} %param.7) | copy-start | bytes 5505028
  8.6 58.5 %collective-permute-start.4 = (s32[8]{0:T(128)S(1)}, s32[8]{0:T(128)S(1)}, u32[]{:S(2)}, u32[]{:S(2)}) collective-permute-start(s32[8]{0:T(128)S(1)} %gather_fusion), channel_id=1, source_target_pairs={{0,128},{128,256},{256,384},{384,0},{1,129},{129,257},{257,385},{3... | collective-permute-start | bytes 104 | tf_op jit(solution)/shard_map/ppermute | solution.py:53
  12.7 54.6 %collective-permute-start.2 = (s32[8]{0:T(128)S(1)}, s32[8]{0:T(128)S(1)}, u32[]{:S(2)}, u32[]{:S(2)}) collective-permute-start(s32[8]{0:T(128)S(1)} %gather_fusion), channel_id=1, source_target_pairs={{0,256},{128,384},{256,0},{384,128},{1,257},{129,385},{257,1},{385... | collective-permute-start | bytes 104 | tf_op jit(solution)/shard_map/ppermute | solution.py:53
  17.2 50.1 %collective-permute-start = (s32[8]{0:T(128)S(1)}, s32[8]{0:T(128)S(1)}, u32[]{:S(2)}, u32[]{:S(2)}) collective-permute-start(s32[8]{0:T(128)S(1)} %gather_fusion), channel_id=1, source_target_pairs={{0,384},{128,0},{256,128},{384,256},{1,385},{129,1},{257,129},{385... | collective-permute-start | bytes 104 | tf_op jit(solution)/shard_map/ppermute | solution.py:53
  26.0 5.0 %copy-start.2 = (bf16[1,16,896]{2,1,0:T(8,128)(2,1)S(1)}, bf16[1,16,896]{2,1,0:T(8,128)(2,1)}, u32[]{:S(2)}) copy-start(bf16[1,16,896]{2,1,0:T(8,128)(2,1)} %param.9) | copy-start | bytes 86020
  26.1 5.0 %copy-start.3 = (bf16[1,16,256]{2,1,0:T(8,128)(2,1)S(1)}, bf16[1,16,256]{2,1,0:T(8,128)(2,1)}, u32[]{:S(2)}) copy-start(bf16[1,16,256]{2,1,0:T(8,128)(2,1)} %param.10) | copy-start | bytes 24580
  26.1 105.1 %all-to-all-start = ((f32[4,1024,256]{1,2,0:T(8,128)}), f32[4,1024,256]{1,2,0:T(8,128)}, u32[]{:S(2)}, u32[]{:S(2)}) async-start(f32[4,1024,256]{1,2,0:T(8,128)} %bitcast.31), calls=%async_computation | async-start | bytes 8388608 | tf_op jit(solution)/shard_map/all_to_all | solution.py:45
  31.0 57.2 %all-gather.3.cloned.1.call-start = ((), (), s32[]{:S(2)}) async-start(), calls=%async_computation.1 | async-start | bytes 1769472 | tf_op jit(solution)/shard_map/all_gather | solution.py:50
  67.1 36.3 %copy-start.4 = (s32[8]{0:T(128)S(1)}, s32[8]{0:T(128)}, u32[]{:S(2)}) copy-start(s32[8]{0:T(128)} %param.12) | copy-start | bytes 100
  88.2 11.3 %copy-start.1 = (bf16[32,16,1152]{2,1,0:T(8,128)(2,1)S(1)}, bf16[32,16,1152]{2,1,0:T(8,128)(2,1)}, u32[]{:S(2)}) copy-start(bf16[32,16,1152]{2,1,0:T(8,128)(2,1)} %all-gather.3.cloned.1.call-done) | copy-start | bytes 3538948
  91.0 13.2 %collective-permute-start.5 = (bf16[8,16,1152]{2,1,0:T(8,128)(2,1)}, bf16[8,16,1152]{2,1,0:T(8,128)(2,1)}, u32[]{:S(2)}, u32[]{:S(2)}) collective-permute-start(bf16[8,16,1152]{2,1,0:T(8,128)(2,1)} %broadcast_select_fusion), channel_id=1, source_target_pairs={{0,384},{128,0},{256,128},{384,256},{1,385},{129,1},{257,129},{385... | collective-permute-start | bytes 884744 | tf_op jit(solution)/shard_map/ppermute | solution.py:57
  97.1 11.8 %collective-permute-start.3 = (bf16[8,16,1152]{2,1,0:T(8,128)(2,1)}, bf16[8,16,1152]{2,1,0:T(8,128)(2,1)}, u32[]{:S(2)}, u32[]{:S(2)}) collective-permute-start(bf16[8,16,1152]{2,1,0:T(8,128)(2,1)} %broadcast_select_fusion.1), channel_id=1, source_target_pairs={{0,256},{128,384},{256,0},{384,128},{1,257},{129,385},{257,1},{385... | collective-permute-start | bytes 884744 | tf_op jit(solution)/shard_map/ppermute | solution.py:57
  101.0 15.1 %collective-permute-start.1 = (bf16[8,16,1152]{2,1,0:T(8,128)(2,1)}, bf16[8,16,1152]{2,1,0:T(8,128)(2,1)}, u32[]{:S(2)}, u32[]{:S(2)}) collective-permute-start(bf16[8,16,1152]{2,1,0:T(8,128)(2,1)} %broadcast_select_fusion.2), channel_id=1, source_target_pairs={{0,128},{128,256},{256,384},{384,0},{1,129},{129,257},{257,385},{3... | collective-permute-start | bytes 884744 | tf_op jit(solution)/shard_map/ppermute | solution.py:57
Sparse Core Ops, SparseCore 0:
  67.3 20.9 all-gather.2

commit v3 on v2

--- a/solution.py
+++ b/solution.py
@@ -40,23 +40,26 @@
     slot_ids = adapter_storage_slot[block_adapter_ids]
     my_row = lax.axis_index("y")
 
+    both_maps = jnp.concatenate([adapter_down_maps, adapter_up_maps], axis=2)
+    column = lax.all_gather(both_maps, "z", axis=0, tiled=True)
+    tokens, key_value_weight, slot_ids, column = lax.optimization_barrier(
+        (tokens, key_value_weight, slot_ids, column)
+    )
+    row_table = lax.all_gather(column, "c", axis=0, tiled=False)
+    row_ids = lax.all_to_all(
+        jnp.broadcast_to(slot_ids[None], (y_size, blocks_dev)), "y", 0, 0, tiled=False
+    )
+
     base_partial = jnp.dot(tokens, key_value_weight, preferred_element_type=jnp.float32)
     outgoing = base_partial.reshape(rows_dev, tp_size, local_columns).transpose(1, 0, 2)
     incoming = lax.all_to_all(outgoing, "tp", 0, 0, tiled=False)
     base_result = jnp.sum(incoming, axis=0)
 
-    both_maps = jnp.concatenate([adapter_down_maps, adapter_up_maps], axis=2)
-    column = lax.all_gather(both_maps, "z", axis=0, tiled=True)
-    row_table = lax.all_gather(column, "c", axis=0, tiled=False)
-    chosen_maps = pick_entries(row_table, slot_ids, my_row, per_row, per_column)
-    for shift in range(1, y_size):
-        their_ids = lax.ppermute(
-            slot_ids, "y", [(i, (i - shift) % y_size) for i in range(y_size)]
-        )
-        sent = pick_entries(row_table, their_ids, my_row, per_row, per_column)
-        chosen_maps = chosen_maps + lax.ppermute(
-            sent, "y", [(i, (i + shift) % y_size) for i in range(y_size)]
-        )
+    sent = pick_entries(row_table, row_ids.reshape(-1), my_row, per_row, per_column)
+    received = lax.all_to_all(
+        sent.reshape((y_size, blocks_dev) + sent.shape[1:]), "y", 0, 0, tiled=False
+    )
+    chosen_maps = jnp.sum(received, axis=0, dtype=received.dtype)
     chosen_down_maps = chosen_maps[:, :, :width_dev]
     chosen_up_maps = chosen_maps[:, :, width_dev:]
 

time: 146 us -> 167 us (1.14)
  blocking collectives: 46.1 us -> 86.6 us
  starting transfers between devices: 24.8 us -> 12.7 us
  waiting for transfers between devices: 32.7 us -> 28.8 us
  local copies, waits for them, and re-layouts: 8.94 us -> 7.09 us
    all_gather x1, blocking collectives: 10.1 us -> 51.6 us  [shards(): lax.all_gather(shrunk_partial, 'tp', axis=0, tiled=False)]
    ppermute x6 -> x0, starting transfers between devices: 19.8 us -> none  [the longest x3 11.5 us: shards(): lax.ppermute(slot_ids, 'y', [(i, (i - shift) % y_size) for i in range(y_s...]
    all_to_all x0 -> x2, waiting for transfers between devices: none -> 14.5 us  [the longest x1 10.5 us: shards(): lax.all_to_all(sent.reshape((y_size, blocks_dev) + sent.shape[1:]), 'y',...]
    ppermute x6 -> x0, waiting for transfers between devices: 11.9 us -> none  [the longest x3 11.8 us: shards(): lax.ppermute(sent, 'y', [(i, (i + shift) % y_size) for i in range(y_size)])]
    all_to_all x0 -> x2, starting transfers between devices: none -> 7.71 us  [the longest x1 4.18 us: shards(): lax.all_to_all(jnp.broadcast_to(slot_ids[None], (y_size, blocks_dev)), 'y...]
    all_gather x1, waiting for transfers between devices: 20.9 us -> 14.2 us  [shards(): row_table = lax.all_gather(column, 'c', axis=0, tiled=False)]
    gather x4 -> x1, local copies, waits for them, and re-layouts: 5.02 us -> 2 us  [pick_entries(): entries = table[inside % per_column, inside // per_column]]
  transfers between devices with their start and end apart: 8 -> 4, of which waited for: 3 -> 3; matrix products, arithmetic and copies ran while one was open for 13% -> 7% of each run, Pallas kernels for 0% -> 0%
where the time goes in v3:
time: 167 us; the launch traced here: 165 us
  blocking collectives  86.6 us (52%)
  waiting for transfers between devices  28.8 us (17%)
  between operations  13.5 us (8%)
  starting transfers between devices  12.7 us (8%)
  other arithmetic  8.86 us (5%)
  matrix products  7.91 us (5%)
  local copies, waits for them, and re-layouts  7.09 us (4%)
    all_gather x1, blocking collectives, shards(): lax.all_gather(shrunk_partial, 'tp', axis=0, tiled=False)  51.6 us
    all_gather x1, blocking collectives, shards(): column = lax.all_gather(both_maps, 'z', axis=0, tiled=True)  35 us
    all_gather x1, waiting for transfers between devices, shards(): row_table = lax.all_gather(column, 'c', axis=0, tiled=False)  14.2 us
    all_to_all x1, waiting for transfers between devices, shards(): lax.all_to_all(sent.reshape((y_size, blocks_dev) + sent.shape[1:]), 'y',...  10.5 us
    dot_general x1, matrix products, shards(): jnp.dot(tokens, key_value_weight, preferred_element_type=jnp.float32)  5.86 us
    all_to_all x1, starting transfers between devices, shards(): incoming = lax.all_to_all(outgoing, 'tp', 0, 0, tiled=False)  4.99 us
    all_to_all x1, starting transfers between devices, shards(): lax.all_to_all(jnp.broadcast_to(slot_ids[None], (y_size, blocks_dev)), 'y...  4.18 us
    all_to_all x1, waiting for transfers between devices, shards(): lax.all_to_all(jnp.broadcast_to(slot_ids[None], (y_size, blocks_dev)), 'y...  4.06 us
  transfers between devices with their start and end apart: 4, of which 3 were waited for; matrix products, arithmetic and copies ran while one was open for 7% of the time, Pallas kernels for 0%

profile of v3, /device:TPU:1, one launch (start us, length us, event | category | flops | bytes accessed | tf_op | source)
XLA Modules:
  0.0 165.4 jit_solution(11173040780300092218)
XLA Ops:
  6.5 0.0 copy-start
  6.5 0.0 all-gather.3.cloned.1.call-start
  6.5 0.8 compare_select_fusion.2
  7.3 0.8 pad_maximum_fusion
  8.1 35.0 %all_gather.12 = bf16[16,16,1152]{2,1,0:T(8,128)(2,1)} all-gather(bf16[1,16,1152]{2,1,0:T(8,128)(2,1)S(1)} %pad_maximum_fusion), channel_id=1, replica_groups=mesh['y'=4,'z'=16,'c'=2,'tp'=4] {'z'}, dimensions={0}, use_global_device_ids=true | all-gather | bytes 626688 | tf_op jit(solution)/shard_map/all_gather | solution.py:44
  43.1 1.3 gather_fusion
  44.4 0.0 all-gather.3.cloned.1.call-update
  44.4 0.6 broadcast_in_dim.38
  45.0 4.2 %all-to-all-start.1 = ((s32[4,1,8]{2,1,0:T(1,128)}), s32[4,1,8]{2,1,0:T(1,128)S(1)}, u32[]{:S(2)}, u32[]{:S(2)}) async-start(s32[4,1,8]{2,1,0:T(1,128)} %broadcast_in_dim.38), calls=%async_computation.1 | async-start | bytes 4096 | tf_op jit(solution)/shard_map/all_to_all | solution.py:49
  49.2 4.1 %all-to-all-done.1 = s32[4,1,8]{2,1,0:T(1,128)S(1)} async-done(((s32[4,1,8]{2,1,0:T(1,128)}), s32[4,1,8]{2,1,0:T(1,128)S(1)}, u32[]{:S(2)}, u32[]{:S(2)}) %all-to-all-start.1) | async-done | bytes 160 | tf_op jit(solution)/shard_map/all_to_all | solution.py:49
  53.2 0.5 broadcast.250
  53.8 0.7 reduce.3
  54.4 0.1 reshape.222
  54.6 14.2 %all-gather.3.cloned.1.call-done = bf16[32,16,1152]{2,1,0:T(8,128)(2,1)} async-done(((bf16[16,16,1152]{2,1,0:T(8,128)(2,1)}), bf16[32,16,1152]{2,1,0:T(8,128)(2,1)}) %all-gather.3.cloned.1.call-update) | async-done | bytes 1179664 | tf_op jit(solution)/shard_map/all_gather | solution.py:48
  68.8 2.0 %gather_fusion.1 = bf16[32,16,1152]{2,1,0:T(8,128)(2,1)S(1)} fusion(bf16[2,16,16,1152]{3,2,1,0:T(8,128)(2,1)} %bitcast.30, s32[32]{0:T(128)S(1)} %fusion.15), kind=kCustom, calls=%fused_computation.1 | custom fusion | bytes 2359552 | tf_op jit(solution)/shard_map/gather | solution.py:16
  70.8 1.2 broadcast_select_fusion
  72.0 3.5 %all-to-all-start.2 = ((bf16[4,8,16,1152]{3,2,1,0:T(8,128)(2,1)}), bf16[4,8,16,1152]{3,2,1,0:T(8,128)(2,1)S(1)}, u32[]{:S(2)}, u32[]{:S(2)}) async-start(bf16[4,8,16,1152]{3,2,1,0:T(8,128)(2,1)} %broadcast_select_fusion), calls=%async_computation.2 | async-start | bytes 2359296 | tf_op jit(solution)/shard_map/all_to_all | solution.py:59
  75.5 0.0 copy-done
  75.5 5.9 %fusion.16 = f32[1024,1024]{0,1:T(8,128)} fusion(bf16[1024,896]{1,0:T(8,128)(2,1)S(1)} %copy-done, bf16[896,1024]{1,0:T(8,128)(2,1)} %param.8), kind=kOutput, calls=%fused_computation.41 | convolution fusion | flops 1879048192 | bytes 7864320 | tf_op jit(solution)/shard_map/dot_general | solution.py:53
  81.4 10.5 %all-to-all-done.2 = bf16[4,8,16,1152]{3,2,1,0:T(8,128)(2,1)S(1)} async-done(((bf16[4,8,16,1152]{3,2,1,0:T(8,128)(2,1)}), bf16[4,8,16,1152]{3,2,1,0:T(8,128)(2,1)S(1)}, u32[]{:S(2)}, u32[]{:S(2)}) %all-to-all-start.2) | async-done | bytes 1179680 | tf_op jit(solution)/shard_map/all_to_all | solution.py:59
  91.9 0.0 copy-start.1
  91.9 5.0 %all-to-all-start = ((f32[4,1024,256]{1,2,0:T(8,128)}), f32[4,1024,256]{1,2,0:T(8,128)}, u32[]{:S(2)}, u32[]{:S(2)}) async-start(f32[4,1024,256]{1,2,0:T(8,128)} %bitcast.28), calls=%async_computation | async-start | bytes 8388608 | tf_op jit(solution)/shard_map/all_to_all | solution.py:55
  96.9 0.0 copy-done.1
  96.9 0.1 fusion.5
  96.9 0.2 reduce_sum.28
  97.1 0.6 fusion
  97.8 51.6 %all_gather.15 = f32[4,1024,16]{1,2,0:T(8,128)S(1)} all-gather(f32[1,1024,16]{1,2,0:T(8,128)S(1)} %all_gather_reshape.3), channel_id=1, replica_groups=mesh['y'=4,'z'=16,'c'=2,'tp'=4] {'tp'}, dimensions={0}, use_global_device_ids=true | all-gather | bytes 327680 | tf_op jit(solution)/shard_map/all_gather | solution.py:70
  149.5 1.4 convolution_multiply_fusion
  150.9 1.6 copy.12
  152.5 0.0 all-to-all-done
  152.5 3.7 %reduce_sum.27 = f32[1024,256]{0,1:T(8,128)} reduce(f32[4,1024,256]{1,2,0:T(8,128)} %all-to-all-done, f32[]{:T(128)} %constant.55.clone.1), dimensions={0}, to_apply=%region_0.0 | reduce | flops 786432 | bytes 5242884 | tf_op jit(solution)/shard_map/reduce_sum | solution.py:56
  156.2 1.4 select_convert_fusion
  157.6 1.0 copy.13
  (6 shorter events, 0.1 us)
Async XLA Ops:
  6.5 69.0 %copy-start = (bf16[1024,896]{1,0:T(8,128)(2,1)S(1)}, bf16[1024,896]{1,0:T(8,128)(2,1)}, u32[]{:S(2)}) copy-start(bf16[1024,896]{1,0:T(8,128)(2,1)} %param.7) | copy-start | bytes 5505028
  6.5 62.2 %all-gather.3.cloned.1.call-start = ((), (), s32[]{:S(2)}) async-start(), calls=%async_computation.3 | async-start | bytes 1769472 | tf_op jit(solution)/shard_map/all_gather | solution.py:48
  45.0 8.2 %all-to-all-start.1 = ((s32[4,1,8]{2,1,0:T(1,128)}), s32[4,1,8]{2,1,0:T(1,128)S(1)}, u32[]{:S(2)}, u32[]{:S(2)}) async-start(s32[4,1,8]{2,1,0:T(1,128)} %broadcast_in_dim.38), calls=%async_computation.1 | async-start | bytes 4096 | tf_op jit(solution)/shard_map/all_to_all | solution.py:49
  72.0 19.9 %all-to-all-start.2 = ((bf16[4,8,16,1152]{3,2,1,0:T(8,128)(2,1)}), bf16[4,8,16,1152]{3,2,1,0:T(8,128)(2,1)S(1)}, u32[]{:S(2)}, u32[]{:S(2)}) async-start(bf16[4,8,16,1152]{3,2,1,0:T(8,128)(2,1)} %broadcast_select_fusion), calls=%async_computation.2 | async-start | bytes 2359296 | tf_op jit(solution)/shard_map/all_to_all | solution.py:59
  91.9 5.0 %copy-start.1 = (s32[8]{0:T(128)S(1)}, s32[8]{0:T(128)}, u32[]{:S(2)}) copy-start(s32[8]{0:T(128)} %param.12) | copy-start | bytes 100
  91.9 60.6 %all-to-all-start = ((f32[4,1024,256]{1,2,0:T(8,128)}), f32[4,1024,256]{1,2,0:T(8,128)}, u32[]{:S(2)}, u32[]{:S(2)}) async-start(f32[4,1024,256]{1,2,0:T(8,128)} %bitcast.28), calls=%async_computation | async-start | bytes 8388608 | tf_op jit(solution)/shard_map/all_to_all | solution.py:55
Sparse Core Ops, SparseCore 0:
  44.5 24.1 all-gather.2

commit v4 on v3

--- a/solution.py
+++ b/solution.py
@@ -40,20 +40,24 @@
     slot_ids = adapter_storage_slot[block_adapter_ids]
     my_row = lax.axis_index("y")
 
-    both_maps = jnp.concatenate([adapter_down_maps, adapter_up_maps], axis=2)
-    column = lax.all_gather(both_maps, "z", axis=0, tiled=True)
-    tokens, key_value_weight, slot_ids, column = lax.optimization_barrier(
-        (tokens, key_value_weight, slot_ids, column)
-    )
-    row_table = lax.all_gather(column, "c", axis=0, tiled=False)
-    row_ids = lax.all_to_all(
-        jnp.broadcast_to(slot_ids[None], (y_size, blocks_dev)), "y", 0, 0, tiled=False
-    )
-
     base_partial = jnp.dot(tokens, key_value_weight, preferred_element_type=jnp.float32)
     outgoing = base_partial.reshape(rows_dev, tp_size, local_columns).transpose(1, 0, 2)
     incoming = lax.all_to_all(outgoing, "tp", 0, 0, tiled=False)
     base_result = jnp.sum(incoming, axis=0)
+
+    both_maps = jnp.concatenate([adapter_down_maps, adapter_up_maps], axis=2)
+    both_maps, outgoing = lax.optimization_barrier((both_maps, outgoing))
+    column = lax.all_gather(both_maps, "z", axis=0, tiled=True)
+    row_table = lax.all_gather(column, "c", axis=0, tiled=False)
+    row_ids = jnp.stack(
+        [slot_ids]
+        + [
+            lax.ppermute(slot_ids, "y", [(i, (i - shift) % y_size) for i in range(y_size)])
+            for shift in range(1, y_size)
+        ]
+    )
+    row_ids = jnp.roll(row_ids, my_row, axis=0)
+    row_table, base_result = lax.optimization_barrier((row_table, base_result))
 
     sent = pick_entries(row_table, row_ids.reshape(-1), my_row, per_row, per_column)
     received = lax.all_to_all(

time: 167 us -> 127 us (0.76)
  the two profiles are of different devices: /device:TPU:1 before, /device:TPU:32 now
where the time goes in v4:
time: 127 us; the launch traced here: 126 us
  blocking collectives  51.8 us (41%)
  waiting for transfers between devices  19.7 us (16%)
  starting transfers between devices  19.5 us (15%)
  between operations  13.6 us (11%)
  matrix products  7.82 us (6%)
  local copies, waits for them, and re-layouts  6.88 us (5%)
  other arithmetic  6.87 us (5%)
    all_gather x1, blocking collectives, shards(): column = lax.all_gather(both_maps, 'z', axis=0, tiled=True)  39 us
    all_to_all x1, waiting for transfers between devices, shards(): lax.all_to_all(sent.reshape((y_size, blocks_dev) + sent.shape[1:]), 'y',...  15.9 us
    all_gather x1, blocking collectives, shards(): lax.all_gather(shrunk_partial, 'tp', axis=0, tiled=False)  12.9 us
    ppermute x3, starting transfers between devices, shards(): lax.ppermute(slot_ids, 'y', [(i, (i - shift) % y_size) for i in range(y_s...  10.9 us
    dot_general x1, matrix products, shards(): jnp.dot(tokens, key_value_weight, preferred_element_type=jnp.float32)  5.86 us
    all_to_all x1, starting transfers between devices, shards(): incoming = lax.all_to_all(outgoing, 'tp', 0, 0, tiled=False)  4.98 us
    reduce_sum x1, other arithmetic, shards(): base_result = jnp.sum(incoming, axis=0)  3.88 us
    ppermute x3, waiting for transfers between devices, shards(): lax.ppermute(slot_ids, 'y', [(i, (i - shift) % y_size) for i in range(y_s...  3.75 us
  transfers between devices with their start and end apart: 6, of which 2 were waited for; matrix products, arithmetic and copies ran while one was open for 4% of the time, Pallas kernels for 0%

profile of v4, /device:TPU:32, one launch (start us, length us, event | category | flops | bytes accessed | tf_op | source)
XLA Modules:
  0.0 126.2 jit_solution(3222475951654883003)
XLA Ops:
  6.5 0.0 copy-start
  6.5 1.5 %copy-done = bf16[1024,896]{1,0:T(8,128)(2,1)S(1)} copy-done((bf16[1024,896]{1,0:T(8,128)(2,1)S(1)}, bf16[1024,896]{1,0:T(8,128)(2,1)}, u32[]{:S(2)}) %copy-start) | copy-done | bytes 1835032
  8.0 5.9 %fusion.15 = f32[1024,1024]{0,1:T(8,128)} fusion(bf16[1024,896]{1,0:T(8,128)(2,1)S(1)} %copy-done, bf16[896,1024]{1,0:T(8,128)(2,1)} %param.8), kind=kOutput, calls=%fused_computation.42 | convolution fusion | flops 1879048192 | bytes 7864320 | tf_op jit(solution)/shard_map/dot_general | solution.py:43
  13.9 0.0 copy-start.2
  13.9 0.0 copy-start.3
  13.9 0.0 copy-start.4
  13.9 0.0 copy-start.1
  13.9 5.0 %all-to-all-start = ((f32[4,1024,256]{1,2,0:T(8,128)}), f32[4,1024,256]{1,2,0:T(8,128)}, u32[]{:S(2)}, u32[]{:S(2)}) async-start(f32[4,1024,256]{1,2,0:T(8,128)} %bitcast.33), calls=%async_computation | async-start | bytes 8388608 | tf_op jit(solution)/shard_map/all_to_all | solution.py:45
  18.9 0.0 all-gather.3.cloned.1.call-start
  18.9 0.0 copy-done.2
  19.0 0.0 copy-done.3
  19.0 39.0 %all_gather.12 = bf16[16,16,1152]{2,1,0:T(8,128)(2,1)} all-gather(bf16[1,16,1152]{2,1,0:T(8,128)(2,1)S(1)} %pad_maximum_fusion), channel_id=1, replica_groups=mesh['y'=4,'z'=16,'c'=2,'tp'=4] {'z'}, dimensions={0}, use_global_device_ids=true | all-gather | bytes 626688 | tf_op jit(solution)/shard_map/all_gather | solution.py:50
  57.9 0.0 all-gather.3.cloned.1.call-update
  58.0 0.0 copy-done.4
  58.0 0.0 copy-done.1
  58.0 0.6 gather_fusion
  58.7 5.1 %collective-permute-start.1 = (s32[8]{0:T(128)S(1)}, s32[8]{0:T(128)S(1)}, u32[]{:S(2)}, u32[]{:S(2)}) collective-permute-start(s32[8]{0:T(128)S(1)} %gather_fusion), channel_id=1, source_target_pairs={{0,256},{128,384},{256,0},{384,128},{1,257},{129,385},{257,1},{385... | collective-permute-start | bytes 104 | tf_op jit(solution)/shard_map/ppermute | solution.py:55
  63.8 3.0 %collective-permute-start = (s32[8]{0:T(128)S(1)}, s32[8]{0:T(128)S(1)}, u32[]{:S(2)}, u32[]{:S(2)}) collective-permute-start(s32[8]{0:T(128)S(1)} %gather_fusion), channel_id=1, source_target_pairs={{0,384},{128,0},{256,128},{384,256},{1,385},{129,1},{257,129},{385... | collective-permute-start | bytes 104 | tf_op jit(solution)/shard_map/ppermute | solution.py:55
  66.7 2.9 %collective-permute-start.2 = (s32[8]{0:T(128)S(1)}, s32[8]{0:T(128)S(1)}, u32[]{:S(2)}, u32[]{:S(2)}) collective-permute-start(s32[8]{0:T(128)S(1)} %gather_fusion), channel_id=1, source_target_pairs={{0,128},{128,256},{256,384},{384,0},{1,129},{129,257},{257,385},{3... | collective-permute-start | bytes 104 | tf_op jit(solution)/shard_map/ppermute | solution.py:55
  69.6 0.0 collective-permute-done.1
  69.6 0.0 collective-permute-done
  69.7 3.7 %collective-permute-done.2 = s32[8]{0:T(128)S(1)} collective-permute-done((s32[8]{0:T(128)S(1)}, s32[8]{0:T(128)S(1)}, u32[]{:S(2)}, u32[]{:S(2)}) %collective-permute-start.2) | collective-permute-done | bytes 64 | tf_op jit(solution)/shard_map/ppermute | solution.py:55
  73.5 0.1 reshape.205
  73.6 0.0 all-to-all-done
  73.6 3.9 %reduce_sum.27 = f32[1024,256]{0,1:T(8,128)} reduce(f32[4,1024,256]{1,2,0:T(8,128)} %all-to-all-done, f32[]{:T(128)} %constant.71.clone.1), dimensions={0}, to_apply=%region_0.0 | reduce | flops 786432 | bytes 5242884 | tf_op jit(solution)/shard_map/reduce_sum | solution.py:46
  77.5 0.0 all-gather.3.cloned.1.call-done
  77.5 2.0 %gather_fusion.1 = bf16[32,16,1152]{2,1,0:T(8,128)(2,1)S(1)} fusion(bf16[2,16,16,1152]{3,2,1,0:T(8,128)(2,1)} %bitcast.35, s32[32]{0:T(128)S(1)} %fusion.14), kind=kCustom, calls=%fused_computation.1 | custom fusion | bytes 2359552 | tf_op jit(solution)/shard_map/gather | solution.py:16
  79.5 0.0 copy-start.5
  79.5 1.2 broadcast_select_fusion
  80.7 3.5 %all-to-all-start.1 = ((bf16[4,8,16,1152]{3,2,1,0:T(8,128)(2,1)}), bf16[4,8,16,1152]{3,2,1,0:T(8,128)(2,1)S(1)}, u32[]{:S(2)}, u32[]{:S(2)}) async-start(bf16[4,8,16,1152]{3,2,1,0:T(8,128)(2,1)} %broadcast_select_fusion), calls=%async_computation.1 | async-start | bytes 2359296 | tf_op jit(solution)/shard_map/all_to_all | solution.py:63
  84.2 0.0 copy-done.5
  84.2 0.1 fusion.4
  84.3 15.9 %all-to-all-done.1 = bf16[4,8,16,1152]{3,2,1,0:T(8,128)(2,1)S(1)} async-done(((bf16[4,8,16,1152]{3,2,1,0:T(8,128)(2,1)}), bf16[4,8,16,1152]{3,2,1,0:T(8,128)(2,1)S(1)}, u32[]{:S(2)}, u32[]{:S(2)}) %all-to-all-start.1) | async-done | bytes 1179680 | tf_op jit(solution)/shard_map/all_to_all | solution.py:63
  100.2 0.2 reduce_sum.28
  100.4 0.6 convolution_bitcast_fusion
  101.1 12.9 %all_gather.15 = f32[4,1024,16]{1,2,0:T(8,128)S(1)} all-gather(f32[1,1024,16]{1,2,0:T(8,128)S(1)} %all_gather_reshape.3), channel_id=1, replica_groups=mesh['y'=4,'z'=16,'c'=2,'tp'=4] {'tp'}, dimensions={0}, use_global_device_ids=true | all-gather | bytes 327680 | tf_op jit(solution)/shard_map/all_gather | solution.py:74
  114.0 1.3 %convolution_multiply_fusion = f32[8,128,256]{2,1,0:T(8,128)} fusion(bf16[8,16,1152]{2,1,0:T(8,128)(2,1)S(1)} %reduce_sum.28, bf16[1024,16]{0,1:T(8,128)(2,1)S(1)} %reduce_sum.29), kind=kOutput, calls=%fused_computation.2 | convolution fusion | flops 8650752 | bytes 1146880 | tf_op jit(solution)/shard_map/bkr,brc->bkc/dot_general | solution.py:77
  115.3 1.6 %copy.12 = f32[1024,256]{0,1:T(8,128)S(1)} copy(f32[1024,256]{1,0:T(8,128)} %bitcast.34) | data formatting | bytes 2097152 | tf_op jit(solution)/shard_map/mul | solution.py:86
  116.9 1.4 %select_convert_fusion = bf16[1024,256]{0,1:T(8,128)(2,1)S(1)} fusion(f32[1024,256]{0,1:T(8,128)} %reduce_sum.27, f32[1024,256]{0,1:T(8,128)S(1)} %copy.12, pred[1024]{0:T(1024)(128)(4,1)S(1)} %fusion.4), kind=kLoop, calls=%fused_computation.5 | loop fusion | flops 786432 | bytes 2622464 | tf_op jit(solution)/shard_map/convert_element_type | solution.py:87
  118.3 1.0 copy.13
  (9 shorter events, 0.2 us)
Async XLA Ops:
  6.5 1.5 %copy-start = (bf16[1024,896]{1,0:T(8,128)(2,1)S(1)}, bf16[1024,896]{1,0:T(8,128)(2,1)}, u32[]{:S(2)}) copy-start(bf16[1024,896]{1,0:T(8,128)(2,1)} %param.7) | copy-start | bytes 5505028
  13.9 5.0 %copy-start.2 = (bf16[1,16,896]{2,1,0:T(8,128)(2,1)S(1)}, bf16[1,16,896]{2,1,0:T(8,128)(2,1)}, u32[]{:S(2)}) copy-start(bf16[1,16,896]{2,1,0:T(8,128)(2,1)} %param.9) | copy-start | bytes 86020
  13.9 5.1 %copy-start.3 = (bf16[1,16,256]{2,1,0:T(8,128)(2,1)S(1)}, bf16[1,16,256]{2,1,0:T(8,128)(2,1)}, u32[]{:S(2)}) copy-start(bf16[1,16,256]{2,1,0:T(8,128)(2,1)} %param.10) | copy-start | bytes 24580
  13.9 44.1 %copy-start.4 = (s32[8]{0:T(128)S(1)}, s32[8]{0:T(128)}, u32[]{:S(2)}) copy-start(s32[8]{0:T(128)} %param.11) | copy-start | bytes 100
  13.9 44.1 %copy-start.1 = (s32[128]{0:T(128)S(1)}, s32[128]{0:T(128)}, u32[]{:S(2)}) copy-start(s32[128]{0:T(128)} %param.13) | copy-start | bytes 1540
  13.9 59.7 %all-to-all-start = ((f32[4,1024,256]{1,2,0:T(8,128)}), f32[4,1024,256]{1,2,0:T(8,128)}, u32[]{:S(2)}, u32[]{:S(2)}) async-start(f32[4,1024,256]{1,2,0:T(8,128)} %bitcast.33), calls=%async_computation | async-start | bytes 8388608 | tf_op jit(solution)/shard_map/all_to_all | solution.py:45
  18.9 58.6 %all-gather.3.cloned.1.call-start = ((), (), s32[]{:S(2)}) async-start(), calls=%async_computation.2 | async-start | bytes 1769472 | tf_op jit(solution)/shard_map/all_gather | solution.py:51
  58.7 11.0 %collective-permute-start.1 = (s32[8]{0:T(128)S(1)}, s32[8]{0:T(128)S(1)}, u32[]{:S(2)}, u32[]{:S(2)}) collective-permute-start(s32[8]{0:T(128)S(1)} %gather_fusion), channel_id=1, source_target_pairs={{0,256},{128,384},{256,0},{384,128},{1,257},{129,385},{257,1},{385... | collective-permute-start | bytes 104 | tf_op jit(solution)/shard_map/ppermute | solution.py:55
  63.8 5.9 %collective-permute-start = (s32[8]{0:T(128)S(1)}, s32[8]{0:T(128)S(1)}, u32[]{:S(2)}, u32[]{:S(2)}) collective-permute-start(s32[8]{0:T(128)S(1)} %gather_fusion), channel_id=1, source_target_pairs={{0,384},{128,0},{256,128},{384,256},{1,385},{129,1},{257,129},{385... | collective-permute-start | bytes 104 | tf_op jit(solution)/shard_map/ppermute | solution.py:55
  66.7 6.7 %collective-permute-start.2 = (s32[8]{0:T(128)S(1)}, s32[8]{0:T(128)S(1)}, u32[]{:S(2)}, u32[]{:S(2)}) collective-permute-start(s32[8]{0:T(128)S(1)} %gather_fusion), channel_id=1, source_target_pairs={{0,128},{128,256},{256,384},{384,0},{1,129},{129,257},{257,385},{3... | collective-permute-start | bytes 104 | tf_op jit(solution)/shard_map/ppermute | solution.py:55
  79.5 4.8 %copy-start.5 = (s32[8]{0:T(128)S(1)}, s32[8]{0:T(128)}, u32[]{:S(2)}) copy-start(s32[8]{0:T(128)} %param.12) | copy-start | bytes 100
  80.7 19.5 %all-to-all-start.1 = ((bf16[4,8,16,1152]{3,2,1,0:T(8,128)(2,1)}), bf16[4,8,16,1152]{3,2,1,0:T(8,128)(2,1)S(1)}, u32[]{:S(2)}, u32[]{:S(2)}) async-start(bf16[4,8,16,1152]{3,2,1,0:T(8,128)(2,1)} %broadcast_select_fusion), calls=%async_computation.1 | async-start | bytes 2359296 | tf_op jit(solution)/shard_map/all_to_all | solution.py:63
Sparse Core Ops, SparseCore 0:
  58.1 17.6 all-gather.2

commit v5 on v4

--- a/solution.py
+++ b/solution.py
@@ -43,7 +43,6 @@
     base_partial = jnp.dot(tokens, key_value_weight, preferred_element_type=jnp.float32)
     outgoing = base_partial.reshape(rows_dev, tp_size, local_columns).transpose(1, 0, 2)
     incoming = lax.all_to_all(outgoing, "tp", 0, 0, tiled=False)
-    base_result = jnp.sum(incoming, axis=0)
 
     both_maps = jnp.concatenate([adapter_down_maps, adapter_up_maps], axis=2)
     both_maps, outgoing = lax.optimization_barrier((both_maps, outgoing))
@@ -57,7 +56,9 @@
         ]
     )
     row_ids = jnp.roll(row_ids, my_row, axis=0)
-    row_table, base_result = lax.optimization_barrier((row_table, base_result))
+    row_table, incoming = lax.optimization_barrier((row_table, incoming))
+
+    base_result = jnp.sum(incoming, axis=0)
 
     sent = pick_entries(row_table, row_ids.reshape(-1), my_row, per_row, per_column)
     received = lax.all_to_all(

time: 127 us -> 127 us (level)
  the two profiles are of different devices: /device:TPU:32 before, /device:TPU:1 now
where the time goes in v5:
time: 127 us; the launch traced here: 125 us
  blocking collectives  46.9 us (37%)
  waiting for transfers between devices  24.2 us (19%)
  starting transfers between devices  18.6 us (15%)
  between operations  13.6 us (11%)
  matrix products  7.82 us (6%)
  local copies, waits for them, and re-layouts  6.88 us (5%)
  other arithmetic  6.7 us (5%)
    all_gather x1, blocking collectives, shards(): column = lax.all_gather(both_maps, 'z', axis=0, tiled=True)  36.7 us
    all_to_all x1, waiting for transfers between devices, shards(): lax.all_to_all(sent.reshape((y_size, blocks_dev) + sent.shape[1:]), 'y',...  12.5 us
    all_gather x1, blocking collectives, shards(): lax.all_gather(shrunk_partial, 'tp', axis=0, tiled=False)  10.2 us
    ppermute x3, starting transfers between devices, shards(): lax.ppermute(slot_ids, 'y', [(i, (i - shift) % y_size) for i in range(y_s...  10.1 us
    all_gather x1, waiting for transfers between devices, shards(): row_table = lax.all_gather(column, 'c', axis=0, tiled=False)  8.75 us
    dot_general x1, matrix products, shards(): jnp.dot(tokens, key_value_weight, preferred_element_type=jnp.float32)  5.86 us
    all_to_all x1, starting transfers between devices, shards(): incoming = lax.all_to_all(outgoing, 'tp', 0, 0, tiled=False)  4.98 us
    reduce_sum x1, other arithmetic, shards(): base_result = jnp.sum(incoming, axis=0)  3.73 us
  transfers between devices with their start and end apart: 6, of which 3 were waited for; matrix products, arithmetic and copies ran while one was open for 4% of the time, Pallas kernels for 0%

profile of v5, /device:TPU:1, one launch (start us, length us, event | category | flops | bytes accessed | tf_op | source)
XLA Modules:
  0.0 124.7 jit_solution(6618405726440724371)
XLA Ops:
  6.5 0.0 copy-start
  6.5 1.5 %copy-done = bf16[1024,896]{1,0:T(8,128)(2,1)S(1)} copy-done((bf16[1024,896]{1,0:T(8,128)(2,1)S(1)}, bf16[1024,896]{1,0:T(8,128)(2,1)}, u32[]{:S(2)}) %copy-start) | copy-done | bytes 1835032
  8.0 5.9 %fusion.15 = f32[1024,1024]{0,1:T(8,128)} fusion(bf16[1024,896]{1,0:T(8,128)(2,1)S(1)} %copy-done, bf16[896,1024]{1,0:T(8,128)(2,1)} %param.8), kind=kOutput, calls=%fused_computation.42 | convolution fusion | flops 1879048192 | bytes 7864320 | tf_op jit(solution)/shard_map/dot_general | solution.py:43
  13.9 0.0 copy-start.2
  13.9 0.0 copy-start.3
  13.9 0.0 copy-start.4
  13.9 0.0 copy-start.1
  13.9 5.0 %all-to-all-start = ((f32[4,1024,256]{1,2,0:T(8,128)}), f32[4,1024,256]{1,2,0:T(8,128)}, u32[]{:S(2)}, u32[]{:S(2)}) async-start(f32[4,1024,256]{1,2,0:T(8,128)} %bitcast.33), calls=%async_computation | async-start | bytes 8388608 | tf_op jit(solution)/shard_map/all_to_all | solution.py:45
  18.9 0.0 all-gather.3.cloned.1.call-start
  18.9 0.0 copy-done.2
  19.0 0.0 copy-done.3
  19.0 36.7 %all_gather.12 = bf16[16,16,1152]{2,1,0:T(8,128)(2,1)} all-gather(bf16[1,16,1152]{2,1,0:T(8,128)(2,1)S(1)} %pad_maximum_fusion), channel_id=1, replica_groups=mesh['y'=4,'z'=16,'c'=2,'tp'=4] {'z'}, dimensions={0}, use_global_device_ids=true | all-gather | bytes 626688 | tf_op jit(solution)/shard_map/all_gather | solution.py:49
  55.7 0.0 all-gather.3.cloned.1.call-update
  55.7 0.0 copy-done.4
  55.8 0.0 copy-done.1
  55.8 0.6 gather_fusion
  56.4 4.8 %collective-permute-start.1 = (s32[8]{0:T(128)S(1)}, s32[8]{0:T(128)S(1)}, u32[]{:S(2)}, u32[]{:S(2)}) collective-permute-start(s32[8]{0:T(128)S(1)} %gather_fusion), channel_id=1, source_target_pairs={{0,256},{128,384},{256,0},{384,128},{1,257},{129,385},{257,1},{385... | collective-permute-start | bytes 104 | tf_op jit(solution)/shard_map/ppermute | solution.py:54
  61.2 2.7 %collective-permute-start = (s32[8]{0:T(128)S(1)}, s32[8]{0:T(128)S(1)}, u32[]{:S(2)}, u32[]{:S(2)}) collective-permute-start(s32[8]{0:T(128)S(1)} %gather_fusion), channel_id=1, source_target_pairs={{0,384},{128,0},{256,128},{384,256},{1,385},{129,1},{257,129},{385... | collective-permute-start | bytes 104 | tf_op jit(solution)/shard_map/ppermute | solution.py:54
  63.9 2.6 %collective-permute-start.2 = (s32[8]{0:T(128)S(1)}, s32[8]{0:T(128)S(1)}, u32[]{:S(2)}, u32[]{:S(2)}) collective-permute-start(s32[8]{0:T(128)S(1)} %gather_fusion), channel_id=1, source_target_pairs={{0,128},{128,256},{256,384},{384,0},{1,129},{129,257},{257,385},{3... | collective-permute-start | bytes 104 | tf_op jit(solution)/shard_map/ppermute | solution.py:54
  66.6 0.0 collective-permute-done.1
  66.6 0.0 collective-permute-done
  66.6 2.9 %collective-permute-done.2 = s32[8]{0:T(128)S(1)} collective-permute-done((s32[8]{0:T(128)S(1)}, s32[8]{0:T(128)S(1)}, u32[]{:S(2)}, u32[]{:S(2)}) %collective-permute-start.2) | collective-permute-done | bytes 64 | tf_op jit(solution)/shard_map/ppermute | solution.py:54
  69.5 0.1 reshape.205
  69.6 8.8 %all-gather.3.cloned.1.call-done = bf16[32,16,1152]{2,1,0:T(8,128)(2,1)} async-done(((bf16[16,16,1152]{2,1,0:T(8,128)(2,1)}), bf16[32,16,1152]{2,1,0:T(8,128)(2,1)}) %all-gather.3.cloned.1.call-update) | async-done | bytes 1179664 | tf_op jit(solution)/shard_map/all_gather | solution.py:50
  78.4 0.0 all-to-all-done
  78.4 2.0 %gather_fusion.1 = bf16[32,16,1152]{2,1,0:T(8,128)(2,1)S(1)} fusion(bf16[2,16,16,1152]{3,2,1,0:T(8,128)(2,1)} %bitcast.35, s32[32]{0:T(128)S(1)} %fusion.14), kind=kCustom, calls=%fused_computation.1 | custom fusion | bytes 2359552 | tf_op jit(solution)/shard_map/gather | solution.py:16
  80.4 0.0 copy-start.5
  80.4 1.2 broadcast_select_fusion
  81.6 3.5 %all-to-all-start.1 = ((bf16[4,8,16,1152]{3,2,1,0:T(8,128)(2,1)}), bf16[4,8,16,1152]{3,2,1,0:T(8,128)(2,1)S(1)}, u32[]{:S(2)}, u32[]{:S(2)}) async-start(bf16[4,8,16,1152]{3,2,1,0:T(8,128)(2,1)} %broadcast_select_fusion), calls=%async_computation.1 | async-start | bytes 2359296 | tf_op jit(solution)/shard_map/all_to_all | solution.py:64
  85.1 0.0 copy-done.5
  85.2 0.1 fusion.4
  85.2 3.7 %reduce_sum.27 = f32[1024,256]{0,1:T(8,128)} reduce(f32[4,1024,256]{1,2,0:T(8,128)} %all-to-all-done, f32[]{:T(128)} %constant.71.clone.1), dimensions={0}, to_apply=%region_0.1 | reduce | flops 786432 | bytes 5242884 | tf_op jit(solution)/shard_map/reduce_sum | solution.py:61
  89.0 12.5 %all-to-all-done.1 = bf16[4,8,16,1152]{3,2,1,0:T(8,128)(2,1)S(1)} async-done(((bf16[4,8,16,1152]{3,2,1,0:T(8,128)(2,1)}), bf16[4,8,16,1152]{3,2,1,0:T(8,128)(2,1)S(1)}, u32[]{:S(2)}, u32[]{:S(2)}) %all-to-all-start.1) | async-done | bytes 1179680 | tf_op jit(solution)/shard_map/all_to_all | solution.py:64
  101.5 0.2 reduce_sum.28
  101.7 0.6 convolution_bitcast_fusion
  102.4 10.2 %all_gather.15 = f32[4,1024,16]{1,2,0:T(8,128)S(1)} all-gather(f32[1,1024,16]{1,2,0:T(8,128)S(1)} %all_gather_reshape.3), channel_id=1, replica_groups=mesh['y'=4,'z'=16,'c'=2,'tp'=4] {'tp'}, dimensions={0}, use_global_device_ids=true | all-gather | bytes 327680 | tf_op jit(solution)/shard_map/all_gather | solution.py:75
  112.6 1.3 %convolution_multiply_fusion = f32[8,128,256]{2,1,0:T(8,128)} fusion(bf16[8,16,1152]{2,1,0:T(8,128)(2,1)S(1)} %reduce_sum.28, bf16[1024,16]{0,1:T(8,128)(2,1)S(1)} %reduce_sum.29), kind=kOutput, calls=%fused_computation.2 | convolution fusion | flops 8650752 | bytes 1146880 | tf_op jit(solution)/shard_map/bkr,brc->bkc/dot_general | solution.py:78
  113.9 1.6 %copy.12 = f32[1024,256]{0,1:T(8,128)S(1)} copy(f32[1024,256]{1,0:T(8,128)} %bitcast.34) | data formatting | bytes 2097152 | tf_op jit(solution)/shard_map/mul | solution.py:87
  115.4 1.4 %select_convert_fusion = bf16[1024,256]{0,1:T(8,128)(2,1)S(1)} fusion(f32[1024,256]{0,1:T(8,128)} %reduce_sum.27, f32[1024,256]{0,1:T(8,128)S(1)} %copy.12, pred[1024]{0:T(1024)(128)(4,1)S(1)} %fusion.4), kind=kLoop, calls=%fused_computation.5 | loop fusion | flops 786432 | bytes 2622464 | tf_op jit(solution)/shard_map/convert_element_type | solution.py:88
  116.9 1.0 copy.13
  (9 shorter events, 0.2 us)
Async XLA Ops:
  6.5 1.5 %copy-start = (bf16[1024,896]{1,0:T(8,128)(2,1)S(1)}, bf16[1024,896]{1,0:T(8,128)(2,1)}, u32[]{:S(2)}) copy-start(bf16[1024,896]{1,0:T(8,128)(2,1)} %param.7) | copy-start | bytes 5505028
  13.9 5.0 %copy-start.2 = (bf16[1,16,896]{2,1,0:T(8,128)(2,1)S(1)}, bf16[1,16,896]{2,1,0:T(8,128)(2,1)}, u32[]{:S(2)}) copy-start(bf16[1,16,896]{2,1,0:T(8,128)(2,1)} %param.9) | copy-start | bytes 86020
  13.9 5.1 %copy-start.3 = (bf16[1,16,256]{2,1,0:T(8,128)(2,1)S(1)}, bf16[1,16,256]{2,1,0:T(8,128)(2,1)}, u32[]{:S(2)}) copy-start(bf16[1,16,256]{2,1,0:T(8,128)(2,1)} %param.10) | copy-start | bytes 24580
  13.9 41.8 %copy-start.4 = (s32[8]{0:T(128)S(1)}, s32[8]{0:T(128)}, u32[]{:S(2)}) copy-start(s32[8]{0:T(128)} %param.11) | copy-start | bytes 100
  13.9 41.9 %copy-start.1 = (s32[128]{0:T(128)S(1)}, s32[128]{0:T(128)}, u32[]{:S(2)}) copy-start(s32[128]{0:T(128)} %param.13) | copy-start | bytes 1540
  13.9 64.5 %all-to-all-start = ((f32[4,1024,256]{1,2,0:T(8,128)}), f32[4,1024,256]{1,2,0:T(8,128)}, u32[]{:S(2)}, u32[]{:S(2)}) async-start(f32[4,1024,256]{1,2,0:T(8,128)} %bitcast.33), calls=%async_computation | async-start | bytes 8388608 | tf_op jit(solution)/shard_map/all_to_all | solution.py:45
  18.9 59.5 %all-gather.3.cloned.1.call-start = ((), (), s32[]{:S(2)}) async-start(), calls=%async_computation.2 | async-start | bytes 1769472 | tf_op jit(solution)/shard_map/all_gather | solution.py:50
  56.4 10.1 %collective-permute-start.1 = (s32[8]{0:T(128)S(1)}, s32[8]{0:T(128)S(1)}, u32[]{:S(2)}, u32[]{:S(2)}) collective-permute-start(s32[8]{0:T(128)S(1)} %gather_fusion), channel_id=1, source_target_pairs={{0,256},{128,384},{256,0},{384,128},{1,257},{129,385},{257,1},{385... | collective-permute-start | bytes 104 | tf_op jit(solution)/shard_map/ppermute | solution.py:54
  61.2 5.3 %collective-permute-start = (s32[8]{0:T(128)S(1)}, s32[8]{0:T(128)S(1)}, u32[]{:S(2)}, u32[]{:S(2)}) collective-permute-start(s32[8]{0:T(128)S(1)} %gather_fusion), channel_id=1, source_target_pairs={{0,384},{128,0},{256,128},{384,256},{1,385},{129,1},{257,129},{385... | collective-permute-start | bytes 104 | tf_op jit(solution)/shard_map/ppermute | solution.py:54
  63.9 5.5 %collective-permute-start.2 = (s32[8]{0:T(128)S(1)}, s32[8]{0:T(128)S(1)}, u32[]{:S(2)}, u32[]{:S(2)}) collective-permute-start(s32[8]{0:T(128)S(1)} %gather_fusion), channel_id=1, source_target_pairs={{0,128},{128,256},{256,384},{384,0},{1,129},{129,257},{257,385},{3... | collective-permute-start | bytes 104 | tf_op jit(solution)/shard_map/ppermute | solution.py:54
  80.4 4.8 %copy-start.5 = (s32[8]{0:T(128)S(1)}, s32[8]{0:T(128)}, u32[]{:S(2)}) copy-start(s32[8]{0:T(128)} %param.12) | copy-start | bytes 100
  81.6 19.9 %all-to-all-start.1 = ((bf16[4,8,16,1152]{3,2,1,0:T(8,128)(2,1)}), bf16[4,8,16,1152]{3,2,1,0:T(8,128)(2,1)S(1)}, u32[]{:S(2)}, u32[]{:S(2)}) async-start(bf16[4,8,16,1152]{3,2,1,0:T(8,128)(2,1)} %broadcast_select_fusion), calls=%async_computation.1 | async-start | bytes 2359296 | tf_op jit(solution)/shard_map/all_to_all | solution.py:64
Sparse Core Ops, SparseCore 0:
  55.9 22.4 all-gather.2

commit v6 on v5

--- a/solution.py
+++ b/solution.py
@@ -47,7 +47,18 @@
     both_maps = jnp.concatenate([adapter_down_maps, adapter_up_maps], axis=2)
     both_maps, outgoing = lax.optimization_barrier((both_maps, outgoing))
     column = lax.all_gather(both_maps, "z", axis=0, tiled=True)
-    row_table = lax.all_gather(column, "c", axis=0, tiled=False)
+    c_size = lax.axis_size("c")
+    row_table = jnp.roll(
+        jnp.stack(
+            [column]
+            + [
+                lax.ppermute(column, "c", [(i, (i + shift) % c_size) for i in range(c_size)])
+                for shift in range(1, c_size)
+            ]
+        ),
+        lax.axis_index("c"),
+        axis=0,
+    )
     row_ids = jnp.stack(
         [slot_ids]
         + [

time: 127 us -> 115 us (0.906)
  the two profiles are of different devices: /device:TPU:1 before, /device:TPU:2 now
where the time goes in v6:
time: 115 us; the launch traced here: 114 us
  blocking collectives  45.8 us (40%)
  starting transfers between devices  27.2 us (24%)
  waiting for transfers between devices  15.6 us (14%)
  other arithmetic  10.3 us (9%)
  matrix products  7.82 us (7%)
  local copies, waits for them, and re-layouts  7.42 us (6%)
    all_gather x1, blocking collectives, shards(): column = lax.all_gather(both_maps, 'z', axis=0, tiled=True)  33.6 us
    all_gather x1, blocking collectives, shards(): lax.all_gather(shrunk_partial, 'tp', axis=0, tiled=False)  12.2 us
    all_to_all x1, waiting for transfers between devices, shards(): lax.all_to_all(sent.reshape((y_size, blocks_dev) + sent.shape[1:]), 'y',...  11.9 us
    ppermute x3, starting transfers between devices, shards(): lax.ppermute(slot_ids, 'y', [(i, (i - shift) % y_size) for i in range(y_s...  10.9 us
    all_to_all x1, starting transfers between devices, shards(): incoming = lax.all_to_all(outgoing, 'tp', 0, 0, tiled=False)  10.8 us
    dot_general x1, matrix products, shards(): jnp.dot(tokens, key_value_weight, preferred_element_type=jnp.float32)  5.86 us
    ppermute x3, waiting for transfers between devices, shards(): lax.ppermute(slot_ids, 'y', [(i, (i - shift) % y_size) for i in range(y_s...  3.74 us
    reduce_sum x1, other arithmetic, shards(): base_result = jnp.sum(incoming, axis=0)  3.73 us
  transfers between devices with their start and end apart: 6, of which 2 were waited for; matrix products, arithmetic and copies ran while one was open for 6% of the time, Pallas kernels for 0%

profile of v6, /device:TPU:2, one launch (start us, length us, event | category | flops | bytes accessed | tf_op | source)
XLA Modules:
  0.0 114.4 jit_solution(475071603168108477)
XLA Ops:
  0.0 0.0 copy-start
  0.0 1.5 %copy-done = bf16[1024,896]{1,0:T(8,128)(2,1)S(1)} copy-done((bf16[1024,896]{1,0:T(8,128)(2,1)S(1)}, bf16[1024,896]{1,0:T(8,128)(2,1)}, u32[]{:S(2)}) %copy-start) | copy-done | bytes 1835032
  1.5 5.9 %fusion.18 = f32[1024,1024]{0,1:T(8,128)} fusion(bf16[1024,896]{1,0:T(8,128)(2,1)S(1)} %copy-done, bf16[896,1024]{1,0:T(8,128)(2,1)} %param.8), kind=kOutput, calls=%fused_computation.49 | convolution fusion | flops 1879048192 | bytes 7864320 | tf_op jit(solution)/shard_map/dot_general | solution.py:43
  7.4 0.0 copy-start.4
  7.4 0.0 copy-start.5
  7.4 0.0 copy-start.6
  7.4 0.0 copy-start.1
  7.4 10.8 %all-to-all-start = ((f32[4,1024,256]{1,2,0:T(8,128)}), f32[4,1024,256]{1,2,0:T(8,128)}, u32[]{:S(2)}, u32[]{:S(2)}) async-start(f32[4,1024,256]{1,2,0:T(8,128)} %bitcast.34), calls=%async_computation | async-start | bytes 8388608 | tf_op jit(solution)/shard_map/all_to_all | solution.py:45
  18.2 0.0 copy-done.4
  18.2 0.0 copy-done.5
  18.2 33.6 %all_gather.6 = bf16[16,16,1152]{2,1,0:T(8,128)(2,1)S(1)} all-gather(bf16[1,16,1152]{2,1,0:T(8,128)(2,1)S(1)} %pad_maximum_fusion), channel_id=1, replica_groups=mesh['y'=4,'z'=16,'c'=2,'tp'=4] {'z'}, dimensions={0}, use_global_device_ids=true | all-gather | bytes 626688 | tf_op jit(solution)/shard_map/all_gather | solution.py:49
  51.8 0.0 copy-start.2
  51.8 1.9 %collective-permute-start = (bf16[16,16,1152]{2,1,0:T(8,128)(2,1)S(1)}, bf16[16,16,1152]{2,1,0:T(8,128)(2,1)S(1)}, u32[]{:S(2)}, u32[]{:S(2)}) collective-permute-start(bf16[16,16,1152]{2,1,0:T(8,128)(2,1)S(1)} %all_gather.6), channel_id=1, source_target_pairs={{0,4},{4,0},{1,5},{5,1},{2,6},{6,2},{3,7},{7,3},{8,12},{12,8},{9,1... | collective-permute-start | bytes 1769480 | tf_op jit(solution)/shard_map/ppermute | solution.py:55
  53.7 0.0 copy-done.6
  53.8 0.0 copy-done.1
  53.8 0.6 gather_fusion
  54.4 5.1 %collective-permute-start.2 = (s32[8]{0:T(128)S(1)}, s32[8]{0:T(128)S(1)}, u32[]{:S(2)}, u32[]{:S(2)}) collective-permute-start(s32[8]{0:T(128)S(1)} %gather_fusion), channel_id=1, source_target_pairs={{0,256},{128,384},{256,0},{384,128},{1,257},{129,385},{257,1},{385... | collective-permute-start | bytes 104 | tf_op jit(solution)/shard_map/ppermute | solution.py:65
  59.5 3.0 %collective-permute-start.1 = (s32[8]{0:T(128)S(1)}, s32[8]{0:T(128)S(1)}, u32[]{:S(2)}, u32[]{:S(2)}) collective-permute-start(s32[8]{0:T(128)S(1)} %gather_fusion), channel_id=1, source_target_pairs={{0,384},{128,0},{256,128},{384,256},{1,385},{129,1},{257,129},{385... | collective-permute-start | bytes 104 | tf_op jit(solution)/shard_map/ppermute | solution.py:65
  62.5 2.9 %collective-permute-start.3 = (s32[8]{0:T(128)S(1)}, s32[8]{0:T(128)S(1)}, u32[]{:S(2)}, u32[]{:S(2)}) collective-permute-start(s32[8]{0:T(128)S(1)} %gather_fusion), channel_id=1, source_target_pairs={{0,128},{128,256},{256,384},{384,0},{1,129},{129,257},{257,385},{3... | collective-permute-start | bytes 104 | tf_op jit(solution)/shard_map/ppermute | solution.py:65
  65.4 0.0 collective-permute-done.2
  65.4 0.0 collective-permute-done.1
  65.4 3.7 %collective-permute-done.3 = s32[8]{0:T(128)S(1)} collective-permute-done((s32[8]{0:T(128)S(1)}, s32[8]{0:T(128)S(1)}, u32[]{:S(2)}, u32[]{:S(2)}) %collective-permute-start.3) | collective-permute-done | bytes 64 | tf_op jit(solution)/shard_map/ppermute | solution.py:65
  69.2 0.1 reshape.205
  69.3 0.0 collective-permute-done
  69.3 0.0 copy-start.3
  69.3 0.0 copy-done.2
  69.4 0.8 copy-done.3
  70.2 2.3 %fusion.2 = bf16[2,16,16,1152]{3,2,1,0:T(8,128)(2,1)S(1)} fusion(s32[]{:T(128)S(6)} %select_n.103, bf16[1,16,16,1152]{3,2,1,0:T(8,128)(2,1)} %bitcast.36, bf16[1,16,16,1152]{3,2,1,0:T(8,128)(2,1)} %bitcast.37), kind=kLoop, calls=%fused_computation.9 | loop fusion | flops 1769472 | bytes 2359300 | tf_op jit(solution)/shard_map/jit(_roll_dynamic)/concatenate | solution.py:51
  72.5 0.0 all-to-all-done
  72.5 1.7 %gather_fusion.1 = bf16[32,16,1152]{2,1,0:T(8,128)(2,1)} fusion(bf16[2,16,16,1152]{3,2,1,0:T(8,128)(2,1)S(1)} %fusion.2, s32[32]{0:T(128)S(1)} %fusion.17), kind=kCustom, calls=%fused_computation.1 | custom fusion | bytes 2359552 | tf_op jit(solution)/shard_map/gather | solution.py:16
  74.3 0.0 copy-start.7
  74.3 2.5 %broadcast_select_fusion = bf16[4,8,16,1152]{3,2,1,0:T(8,128)(2,1)} fusion(bf16[4,8,16,1152]{3,2,1,0:T(8,128)(2,1)} %bitcast.33, pred[4,8]{1,0:T(4,128)(4,1)S(1)} %get-tuple-element.11), kind=kLoop, calls=%fused_computation.10 | loop fusion | flops 589824 | bytes 2359328 | tf_op jit(solution)/shard_map/jit(_where)/select_n | solution.py:18
  76.7 3.5 %all-to-all-start.1 = ((bf16[4,8,16,1152]{3,2,1,0:T(8,128)(2,1)}), bf16[4,8,16,1152]{3,2,1,0:T(8,128)(2,1)S(1)}, u32[]{:S(2)}, u32[]{:S(2)}) async-start(bf16[4,8,16,1152]{3,2,1,0:T(8,128)(2,1)} %broadcast_select_fusion), calls=%async_computation.1 | async-start | bytes 2359296 | tf_op jit(solution)/shard_map/all_to_all | solution.py:75
  80.3 0.0 copy-done.7
  80.3 0.1 fusion.7
  80.4 3.7 %reduce_sum.27 = f32[1024,256]{0,1:T(8,128)} reduce(f32[4,1024,256]{1,2,0:T(8,128)} %all-to-all-done, f32[]{:T(128)} %constant.93.clone.1), dimensions={0}, to_apply=%region_0.1 | reduce | flops 786432 | bytes 5242884 | tf_op jit(solution)/shard_map/reduce_sum | solution.py:72
  84.1 11.9 %all-to-all-done.1 = bf16[4,8,16,1152]{3,2,1,0:T(8,128)(2,1)S(1)} async-done(((bf16[4,8,16,1152]{3,2,1,0:T(8,128)(2,1)}), bf16[4,8,16,1152]{3,2,1,0:T(8,128)(2,1)S(1)}, u32[]{:S(2)}, u32[]{:S(2)}) %all-to-all-start.1) | async-done | bytes 1179680 | tf_op jit(solution)/shard_map/all_to_all | solution.py:75
  96.0 0.2 reduce_sum.28
  96.2 0.6 convolution_bitcast_fusion
  96.9 12.2 %all_gather.7 = f32[4,1024,16]{1,2,0:T(8,128)S(1)} all-gather(f32[1,1024,16]{1,2,0:T(8,128)S(1)} %all_gather_reshape.3), channel_id=1, replica_groups=mesh['y'=4,'z'=16,'c'=2,'tp'=4] {'tp'}, dimensions={0}, use_global_device_ids=true | all-gather | bytes 327680 | tf_op jit(solution)/shard_map/all_gather | solution.py:86
  109.1 1.3 %convolution_multiply_fusion = f32[8,128,256]{2,1,0:T(8,128)} fusion(bf16[8,16,1152]{2,1,0:T(8,128)(2,1)S(1)} %reduce_sum.28, bf16[1024,16]{0,1:T(8,128)(2,1)S(1)} %reduce_sum.29), kind=kOutput, calls=%fused_computation.6 | convolution fusion | flops 8650752 | bytes 1146880 | tf_op jit(solution)/shard_map/bkr,brc->bkc/dot_general | solution.py:89
  110.4 1.6 %copy.12 = f32[1024,256]{0,1:T(8,128)S(1)} copy(f32[1024,256]{1,0:T(8,128)} %bitcast.35) | data formatting | bytes 2097152 | tf_op jit(solution)/shard_map/mul | solution.py:98
  111.9 1.4 %select_convert_fusion = bf16[1024,256]{0,1:T(8,128)(2,1)S(1)} fusion(f32[1024,256]{0,1:T(8,128)} %reduce_sum.27, f32[1024,256]{0,1:T(8,128)S(1)} %copy.12, pred[1024]{0:T(1024)(128)(4,1)S(1)} %fusion.7), kind=kLoop, calls=%fused_computation.12 | loop fusion | flops 786432 | bytes 2622464 | tf_op jit(solution)/shard_map/convert_element_type | solution.py:99
  113.4 1.0 copy.13
  (9 shorter events, 0.2 us)
Async XLA Ops:
  0.0 1.5 %copy-start = (bf16[1024,896]{1,0:T(8,128)(2,1)S(1)}, bf16[1024,896]{1,0:T(8,128)(2,1)}, u32[]{:S(2)}) copy-start(bf16[1024,896]{1,0:T(8,128)(2,1)} %param.7) | copy-start | bytes 5505028
  7.4 10.8 %copy-start.4 = (bf16[1,16,896]{2,1,0:T(8,128)(2,1)S(1)}, bf16[1,16,896]{2,1,0:T(8,128)(2,1)}, u32[]{:S(2)}) copy-start(bf16[1,16,896]{2,1,0:T(8,128)(2,1)} %param.9) | copy-start | bytes 86020
  7.4 10.8 %copy-start.5 = (bf16[1,16,256]{2,1,0:T(8,128)(2,1)S(1)}, bf16[1,16,256]{2,1,0:T(8,128)(2,1)}, u32[]{:S(2)}) copy-start(bf16[1,16,256]{2,1,0:T(8,128)(2,1)} %param.10) | copy-start | bytes 24580
  7.4 46.4 %copy-start.6 = (s32[8]{0:T(128)S(1)}, s32[8]{0:T(128)}, u32[]{:S(2)}) copy-start(s32[8]{0:T(128)} %param.11) | copy-start | bytes 100
  7.4 46.4 %copy-start.1 = (s32[128]{0:T(128)S(1)}, s32[128]{0:T(128)}, u32[]{:S(2)}) copy-start(s32[128]{0:T(128)} %param.13) | copy-start | bytes 1540
  7.4 65.2 %all-to-all-start = ((f32[4,1024,256]{1,2,0:T(8,128)}), f32[4,1024,256]{1,2,0:T(8,128)}, u32[]{:S(2)}, u32[]{:S(2)}) async-start(f32[4,1024,256]{1,2,0:T(8,128)} %bitcast.34), calls=%async_computation | async-start | bytes 8388608 | tf_op jit(solution)/shard_map/all_to_all | solution.py:45
  51.8 17.5 %copy-start.2 = (bf16[16,16,1152]{2,1,0:T(8,128)(2,1)}, bf16[16,16,1152]{2,1,0:T(8,128)(2,1)S(1)}, u32[]{:S(2)}) copy-start(bf16[16,16,1152]{2,1,0:T(8,128)(2,1)S(1)} %all_gather.6) | copy-start | bytes 1769476
  51.8 17.5 %collective-permute-start = (bf16[16,16,1152]{2,1,0:T(8,128)(2,1)S(1)}, bf16[16,16,1152]{2,1,0:T(8,128)(2,1)S(1)}, u32[]{:S(2)}, u32[]{:S(2)}) collective-permute-start(bf16[16,16,1152]{2,1,0:T(8,128)(2,1)S(1)} %all_gather.6), channel_id=1, source_target_pairs={{0,4},{4,0},{1,5},{5,1},{2,6},{6,2},{3,7},{7,3},{8,12},{12,8},{9,1... | collective-permute-start | bytes 1769480 | tf_op jit(solution)/shard_map/ppermute | solution.py:55
  54.4 11.0 %collective-permute-start.2 = (s32[8]{0:T(128)S(1)}, s32[8]{0:T(128)S(1)}, u32[]{:S(2)}, u32[]{:S(2)}) collective-permute-start(s32[8]{0:T(128)S(1)} %gather_fusion), channel_id=1, source_target_pairs={{0,256},{128,384},{256,0},{384,128},{1,257},{129,385},{257,1},{385... | collective-permute-start | bytes 104 | tf_op jit(solution)/shard_map/ppermute | solution.py:65
  59.5 5.9 %collective-permute-start.1 = (s32[8]{0:T(128)S(1)}, s32[8]{0:T(128)S(1)}, u32[]{:S(2)}, u32[]{:S(2)}) collective-permute-start(s32[8]{0:T(128)S(1)} %gather_fusion), channel_id=1, source_target_pairs={{0,384},{128,0},{256,128},{384,256},{1,385},{129,1},{257,129},{385... | collective-permute-start | bytes 104 | tf_op jit(solution)/shard_map/ppermute | solution.py:65
  62.5 6.7 %collective-permute-start.3 = (s32[8]{0:T(128)S(1)}, s32[8]{0:T(128)S(1)}, u32[]{:S(2)}, u32[]{:S(2)}) collective-permute-start(s32[8]{0:T(128)S(1)} %gather_fusion), channel_id=1, source_target_pairs={{0,128},{128,256},{256,384},{384,0},{1,129},{129,257},{257,385},{3... | collective-permute-start | bytes 104 | tf_op jit(solution)/shard_map/ppermute | solution.py:65
  69.3 0.8 copy-start.3
  74.3 6.0 %copy-start.7 = (s32[8]{0:T(128)S(1)}, s32[8]{0:T(128)}, u32[]{:S(2)}) copy-start(s32[8]{0:T(128)} %param.12) | copy-start | bytes 100
  76.7 19.2 %all-to-all-start.1 = ((bf16[4,8,16,1152]{3,2,1,0:T(8,128)(2,1)}), bf16[4,8,16,1152]{3,2,1,0:T(8,128)(2,1)S(1)}, u32[]{:S(2)}, u32[]{:S(2)}) async-start(bf16[4,8,16,1152]{3,2,1,0:T(8,128)(2,1)} %broadcast_select_fusion), calls=%async_computation.1 | async-start | bytes 2359296 | tf_op jit(solution)/shard_map/all_to_all | solution.py:75

commit v7 on v6

--- a/solution.py
+++ b/solution.py
@@ -7,7 +7,7 @@
 from jax.sharding import PartitionSpec as P
 
 adapter_scale = 0.5
-ROWS = ("y", "z", "c")
+ROWS = ("y", "zh", "zl", "c")
 
 
 def pick_entries(table, wanted, own_row, per_row, per_column):
@@ -35,7 +35,7 @@
     tp_size = key_value_weight.shape[1] // local_columns
     y_size = lax.axis_size("y")
     per_column = lax.axis_size("c")
-    per_row = lax.axis_size("z") * per_column
+    per_row = lax.axis_size("zh") * lax.axis_size("zl") * per_column
 
     slot_ids = adapter_storage_slot[block_adapter_ids]
     my_row = lax.axis_index("y")
@@ -46,7 +46,8 @@
 
     both_maps = jnp.concatenate([adapter_down_maps, adapter_up_maps], axis=2)
     both_maps, outgoing = lax.optimization_barrier((both_maps, outgoing))
-    column = lax.all_gather(both_maps, "z", axis=0, tiled=True)
+    column = lax.all_gather(both_maps, "zl", axis=0, tiled=True)
+    column = lax.all_gather(column, "zh", axis=0, tiled=True)
     c_size = lax.axis_size("c")
     row_table = jnp.roll(
         jnp.stack(
@@ -112,6 +113,8 @@
             sorted({e.coords[2] for e in first})[zi],
             sorted({e.core_on_chip for e in first})[ci],
         )
+    zl_size = 4 if z_size % 4 == 0 else z_size
+    split = split.reshape(y_size, z_size // zl_size, zl_size, c_size, devices.shape[1])
     return Mesh(split, ROWS + ("tp",))
 
 

time: 115 us -> 124 us (1.078)
  blocking collectives: 45.8 us -> 55 us
    all_gather x1 -> x2, blocking collectives: 33.6 us -> 43 us  [the longest x1 29.5 us: shards(): column = lax.all_gather(column, 'zh', axis=0, tiled=True)]
where the time goes in v7:
time: 124 us
  blocking collectives  55 us (44%)
  starting transfers between devices  27.2 us (22%)
  waiting for transfers between devices  15.7 us (13%)
  other arithmetic  10.3 us (8%)
  matrix products  7.82 us (6%)
  local copies, waits for them, and re-layouts  7.42 us (6%)
    all_gather x1, blocking collectives, shards(): column = lax.all_gather(column, 'zh', axis=0, tiled=True)  29.5 us
    all_gather x1, blocking collectives, shards(): column = lax.all_gather(both_maps, 'zl', axis=0, tiled=True)  13.5 us
    all_gather x1, blocking collectives, shards(): lax.all_gather(shrunk_partial, 'tp', axis=0, tiled=False)  12 us
    all_to_all x1, waiting for transfers between devices, shards(): lax.all_to_all(sent.reshape((y_size, blocks_dev) + sent.shape[1:]), 'y',...  11.9 us
    ppermute x3, starting transfers between devices, shards(): lax.ppermute(slot_ids, 'y', [(i, (i - shift) % y_size) for i in range(y_s...  11 us
    all_to_all x1, starting transfers between devices, shards(): incoming = lax.all_to_all(outgoing, 'tp', 0, 0, tiled=False)  10.8 us
    dot_general x1, matrix products, shards(): jnp.dot(tokens, key_value_weight, preferred_element_type=jnp.float32)  5.86 us
    ppermute x3, waiting for transfers between devices, shards(): lax.ppermute(slot_ids, 'y', [(i, (i - shift) % y_size) for i in range(y_s...  3.77 us
  transfers between devices with their start and end apart: 6, of which 2 were waited for; matrix products, arithmetic and copies ran while one was open for 6% of the time, Pallas kernels for 0%

profile of v7, /device:TPU:2, one launch (start us, length us, event | category | flops | bytes accessed | tf_op | source)
XLA Modules:
  0.0 123.7 jit_solution(9751928729986445351)
XLA Ops:
  0.0 0.0 copy-start
  0.0 1.5 %copy-done = bf16[1024,896]{1,0:T(8,128)(2,1)S(1)} copy-done((bf16[1024,896]{1,0:T(8,128)(2,1)S(1)}, bf16[1024,896]{1,0:T(8,128)(2,1)}, u32[]{:S(2)}) %copy-start) | copy-done | bytes 1835032
  1.5 5.9 %fusion.18 = f32[1024,1024]{0,1:T(8,128)} fusion(bf16[1024,896]{1,0:T(8,128)(2,1)S(1)} %copy-done, bf16[896,1024]{1,0:T(8,128)(2,1)} %param.8), kind=kOutput, calls=%fused_computation.49 | convolution fusion | flops 1879048192 | bytes 7864320 | tf_op jit(solution)/shard_map/dot_general | solution.py:43
  7.4 0.0 copy-start.4
  7.4 0.0 copy-start.5
  7.4 0.0 copy-start.6
  7.4 0.0 copy-start.1
  7.4 10.8 %all-to-all-start = ((f32[4,1024,256]{1,2,0:T(8,128)}), f32[4,1024,256]{1,2,0:T(8,128)}, u32[]{:S(2)}, u32[]{:S(2)}) async-start(f32[4,1024,256]{1,2,0:T(8,128)} %bitcast.34), calls=%async_computation | async-start | bytes 8388608 | tf_op jit(solution)/shard_map/all_to_all | solution.py:45
  18.2 0.0 copy-done.4
  18.2 0.0 copy-done.5
  18.2 13.5 %all_gather.9 = bf16[4,16,1152]{2,1,0:T(8,128)(2,1)S(1)} all-gather(bf16[1,16,1152]{2,1,0:T(8,128)(2,1)S(1)} %pad_maximum_fusion), channel_id=1, replica_groups=mesh['y'=4,'zh'=4,'zl'=4,'c'=2,'tp'=4] {'zl'}, dimensions={0}, use_global_device_ids=true | all-gather | bytes 184320 | tf_op jit(solution)/shard_map/all_gather | solution.py:49
  31.7 29.5 %all_gather.10 = bf16[16,16,1152]{2,1,0:T(8,128)(2,1)S(1)} all-gather(bf16[4,16,1152]{2,1,0:T(8,128)(2,1)S(1)} %all_gather.9), channel_id=1, replica_groups=mesh['y'=4,'zh'=4,'zl'=4,'c'=2,'tp'=4] {'zh'}, dimensions={0}, use_global_device_ids=true | all-gather | bytes 737280 | tf_op jit(solution)/shard_map/all_gather | solution.py:50
  61.2 0.0 copy-start.2
  61.2 1.9 %collective-permute-start = (bf16[16,16,1152]{2,1,0:T(8,128)(2,1)S(1)}, bf16[16,16,1152]{2,1,0:T(8,128)(2,1)S(1)}, u32[]{:S(2)}, u32[]{:S(2)}) collective-permute-start(bf16[16,16,1152]{2,1,0:T(8,128)(2,1)S(1)} %all_gather.10), channel_id=1, source_target_pairs={{0,4},{4,0},{1,5},{5,1},{2,6},{6,2},{3,7},{7,3},{8,12},{12,8},{9,1... | collective-permute-start | bytes 1769480 | tf_op jit(solution)/shard_map/ppermute | solution.py:56
  63.2 0.0 copy-done.6
  63.2 0.0 copy-done.1
  63.2 0.6 gather_fusion
  63.9 5.1 %collective-permute-start.2 = (s32[8]{0:T(128)S(1)}, s32[8]{0:T(128)S(1)}, u32[]{:S(2)}, u32[]{:S(2)}) collective-permute-start(s32[8]{0:T(128)S(1)} %gather_fusion), channel_id=1, source_target_pairs={{0,256},{128,384},{256,0},{384,128},{1,257},{129,385},{257,1},{385... | collective-permute-start | bytes 104 | tf_op jit(solution)/shard_map/ppermute | solution.py:66
  69.0 3.0 %collective-permute-start.1 = (s32[8]{0:T(128)S(1)}, s32[8]{0:T(128)S(1)}, u32[]{:S(2)}, u32[]{:S(2)}) collective-permute-start(s32[8]{0:T(128)S(1)} %gather_fusion), channel_id=1, source_target_pairs={{0,384},{128,0},{256,128},{384,256},{1,385},{129,1},{257,129},{385... | collective-permute-start | bytes 104 | tf_op jit(solution)/shard_map/ppermute | solution.py:66
  72.0 2.9 %collective-permute-start.3 = (s32[8]{0:T(128)S(1)}, s32[8]{0:T(128)S(1)}, u32[]{:S(2)}, u32[]{:S(2)}) collective-permute-start(s32[8]{0:T(128)S(1)} %gather_fusion), channel_id=1, source_target_pairs={{0,128},{128,256},{256,384},{384,0},{1,129},{129,257},{257,385},{3... | collective-permute-start | bytes 104 | tf_op jit(solution)/shard_map/ppermute | solution.py:66
  74.9 0.0 collective-permute-done.2
  74.9 0.0 collective-permute-done.1
  74.9 3.8 %collective-permute-done.3 = s32[8]{0:T(128)S(1)} collective-permute-done((s32[8]{0:T(128)S(1)}, s32[8]{0:T(128)S(1)}, u32[]{:S(2)}, u32[]{:S(2)}) %collective-permute-start.3) | collective-permute-done | bytes 64 | tf_op jit(solution)/shard_map/ppermute | solution.py:66
  78.7 0.1 reshape.205
  78.8 0.0 collective-permute-done
  78.8 0.0 copy-start.3
  78.8 0.0 copy-done.2
  78.8 0.8 copy-done.3
  79.7 2.3 %fusion.2 = bf16[2,16,16,1152]{3,2,1,0:T(8,128)(2,1)S(1)} fusion(s32[]{:T(128)S(6)} %select_n.103, bf16[1,16,16,1152]{3,2,1,0:T(8,128)(2,1)} %bitcast.36, bf16[1,16,16,1152]{3,2,1,0:T(8,128)(2,1)} %bitcast.37), kind=kLoop, calls=%fused_computation.9 | loop fusion | flops 1769472 | bytes 2359300 | tf_op jit(solution)/shard_map/jit(_roll_dynamic)/concatenate | solution.py:52
  82.0 0.0 all-to-all-done
  82.0 1.7 %gather_fusion.1 = bf16[32,16,1152]{2,1,0:T(8,128)(2,1)} fusion(bf16[2,16,16,1152]{3,2,1,0:T(8,128)(2,1)S(1)} %fusion.2, s32[32]{0:T(128)S(1)} %fusion.17), kind=kCustom, calls=%fused_computation.1 | custom fusion | bytes 2359552 | tf_op jit(solution)/shard_map/gather | solution.py:16
  83.7 0.0 copy-start.7
  83.7 2.5 %broadcast_select_fusion = bf16[4,8,16,1152]{3,2,1,0:T(8,128)(2,1)} fusion(bf16[4,8,16,1152]{3,2,1,0:T(8,128)(2,1)} %bitcast.33, pred[4,8]{1,0:T(4,128)(4,1)S(1)} %get-tuple-element.11), kind=kLoop, calls=%fused_computation.10 | loop fusion | flops 589824 | bytes 2359328 | tf_op jit(solution)/shard_map/jit(_where)/select_n | solution.py:18
  86.2 3.5 %all-to-all-start.1 = ((bf16[4,8,16,1152]{3,2,1,0:T(8,128)(2,1)}), bf16[4,8,16,1152]{3,2,1,0:T(8,128)(2,1)S(1)}, u32[]{:S(2)}, u32[]{:S(2)}) async-start(bf16[4,8,16,1152]{3,2,1,0:T(8,128)(2,1)} %broadcast_select_fusion), calls=%async_computation.1 | async-start | bytes 2359296 | tf_op jit(solution)/shard_map/all_to_all | solution.py:76
  89.8 0.0 copy-done.7
  89.8 0.1 fusion.7
  89.9 3.7 %reduce_sum.27 = f32[1024,256]{0,1:T(8,128)} reduce(f32[4,1024,256]{1,2,0:T(8,128)} %all-to-all-done, f32[]{:T(128)} %constant.93.clone.1), dimensions={0}, to_apply=%region_0.1 | reduce | flops 786432 | bytes 5242884 | tf_op jit(solution)/shard_map/reduce_sum | solution.py:73
  93.6 11.9 %all-to-all-done.1 = bf16[4,8,16,1152]{3,2,1,0:T(8,128)(2,1)S(1)} async-done(((bf16[4,8,16,1152]{3,2,1,0:T(8,128)(2,1)}), bf16[4,8,16,1152]{3,2,1,0:T(8,128)(2,1)S(1)}, u32[]{:S(2)}, u32[]{:S(2)}) %all-to-all-start.1) | async-done | bytes 1179680 | tf_op jit(solution)/shard_map/all_to_all | solution.py:76
  105.5 0.2 reduce_sum.28
  105.7 0.6 convolution_bitcast_fusion
  106.4 12.0 %all_gather.11 = f32[4,1024,16]{1,2,0:T(8,128)S(1)} all-gather(f32[1,1024,16]{1,2,0:T(8,128)S(1)} %all_gather_reshape.3), channel_id=1, replica_groups=mesh['y'=4,'zh'=4,'zl'=4,'c'=2,'tp'=4] {'tp'}, dimensions={0}, use_global_device_ids=true | all-gather | bytes 327680 | tf_op jit(solution)/shard_map/all_gather | solution.py:87
  118.4 1.3 %convolution_multiply_fusion = f32[8,128,256]{2,1,0:T(8,128)} fusion(bf16[8,16,1152]{2,1,0:T(8,128)(2,1)S(1)} %reduce_sum.28, bf16[1024,16]{0,1:T(8,128)(2,1)S(1)} %reduce_sum.29), kind=kOutput, calls=%fused_computation.6 | convolution fusion | flops 8650752 | bytes 1146880 | tf_op jit(solution)/shard_map/bkr,brc->bkc/dot_general | solution.py:90
  119.7 1.6 %copy.12 = f32[1024,256]{0,1:T(8,128)S(1)} copy(f32[1024,256]{1,0:T(8,128)} %bitcast.35) | data formatting | bytes 2097152 | tf_op jit(solution)/shard_map/mul | solution.py:99
  121.3 1.4 %select_convert_fusion = bf16[1024,256]{0,1:T(8,128)(2,1)S(1)} fusion(f32[1024,256]{0,1:T(8,128)} %reduce_sum.27, f32[1024,256]{0,1:T(8,128)S(1)} %copy.12, pred[1024]{0:T(1024)(128)(4,1)S(1)} %fusion.7), kind=kLoop, calls=%fused_computation.12 | loop fusion | flops 786432 | bytes 2622464 | tf_op jit(solution)/shard_map/convert_element_type | solution.py:100
  122.7 1.0 copy.13
  (9 shorter events, 0.2 us)
Async XLA Ops:
  0.0 1.5 %copy-start = (bf16[1024,896]{1,0:T(8,128)(2,1)S(1)}, bf16[1024,896]{1,0:T(8,128)(2,1)}, u32[]{:S(2)}) copy-start(bf16[1024,896]{1,0:T(8,128)(2,1)} %param.7) | copy-start | bytes 5505028
  7.4 10.8 %copy-start.4 = (bf16[1,16,896]{2,1,0:T(8,128)(2,1)S(1)}, bf16[1,16,896]{2,1,0:T(8,128)(2,1)}, u32[]{:S(2)}) copy-start(bf16[1,16,896]{2,1,0:T(8,128)(2,1)} %param.9) | copy-start | bytes 86020
  7.4 10.8 %copy-start.5 = (bf16[1,16,256]{2,1,0:T(8,128)(2,1)S(1)}, bf16[1,16,256]{2,1,0:T(8,128)(2,1)}, u32[]{:S(2)}) copy-start(bf16[1,16,256]{2,1,0:T(8,128)(2,1)} %param.10) | copy-start | bytes 24580
  7.4 55.8 %copy-start.6 = (s32[8]{0:T(128)S(1)}, s32[8]{0:T(128)}, u32[]{:S(2)}) copy-start(s32[8]{0:T(128)} %param.11) | copy-start | bytes 100
  7.4 55.8 %copy-start.1 = (s32[128]{0:T(128)S(1)}, s32[128]{0:T(128)}, u32[]{:S(2)}) copy-start(s32[128]{0:T(128)} %param.13) | copy-start | bytes 1540
  7.4 74.6 %all-to-all-start = ((f32[4,1024,256]{1,2,0:T(8,128)}), f32[4,1024,256]{1,2,0:T(8,128)}, u32[]{:S(2)}, u32[]{:S(2)}) async-start(f32[4,1024,256]{1,2,0:T(8,128)} %bitcast.34), calls=%async_computation | async-start | bytes 8388608 | tf_op jit(solution)/shard_map/all_to_all | solution.py:45
  61.2 17.6 %copy-start.2 = (bf16[16,16,1152]{2,1,0:T(8,128)(2,1)}, bf16[16,16,1152]{2,1,0:T(8,128)(2,1)S(1)}, u32[]{:S(2)}) copy-start(bf16[16,16,1152]{2,1,0:T(8,128)(2,1)S(1)} %all_gather.10) | copy-start | bytes 1769476
  61.2 17.6 %collective-permute-start = (bf16[16,16,1152]{2,1,0:T(8,128)(2,1)S(1)}, bf16[16,16,1152]{2,1,0:T(8,128)(2,1)S(1)}, u32[]{:S(2)}, u32[]{:S(2)}) collective-permute-start(bf16[16,16,1152]{2,1,0:T(8,128)(2,1)S(1)} %all_gather.10), channel_id=1, source_target_pairs={{0,4},{4,0},{1,5},{5,1},{2,6},{6,2},{3,7},{7,3},{8,12},{12,8},{9,1... | collective-permute-start | bytes 1769480 | tf_op jit(solution)/shard_map/ppermute | solution.py:56
  63.9 11.0 %collective-permute-start.2 = (s32[8]{0:T(128)S(1)}, s32[8]{0:T(128)S(1)}, u32[]{:S(2)}, u32[]{:S(2)}) collective-permute-start(s32[8]{0:T(128)S(1)} %gather_fusion), channel_id=1, source_target_pairs={{0,256},{128,384},{256,0},{384,128},{1,257},{129,385},{257,1},{385... | collective-permute-start | bytes 104 | tf_op jit(solution)/shard_map/ppermute | solution.py:66
  69.0 5.9 %collective-permute-start.1 = (s32[8]{0:T(128)S(1)}, s32[8]{0:T(128)S(1)}, u32[]{:S(2)}, u32[]{:S(2)}) collective-permute-start(s32[8]{0:T(128)S(1)} %gather_fusion), channel_id=1, source_target_pairs={{0,384},{128,0},{256,128},{384,256},{1,385},{129,1},{257,129},{385... | collective-permute-start | bytes 104 | tf_op jit(solution)/shard_map/ppermute | solution.py:66
  72.0 6.7 %collective-permute-start.3 = (s32[8]{0:T(128)S(1)}, s32[8]{0:T(128)S(1)}, u32[]{:S(2)}, u32[]{:S(2)}) collective-permute-start(s32[8]{0:T(128)S(1)} %gather_fusion), channel_id=1, source_target_pairs={{0,128},{128,256},{256,384},{384,0},{1,129},{129,257},{257,385},{3... | collective-permute-start | bytes 104 | tf_op jit(solution)/shard_map/ppermute | solution.py:66
  78.8 0.8 copy-start.3
  83.7 6.0 %copy-start.7 = (s32[8]{0:T(128)S(1)}, s32[8]{0:T(128)}, u32[]{:S(2)}) copy-start(s32[8]{0:T(128)} %param.12) | copy-start | bytes 100
  86.2 19.2 %all-to-all-start.1 = ((bf16[4,8,16,1152]{3,2,1,0:T(8,128)(2,1)}), bf16[4,8,16,1152]{3,2,1,0:T(8,128)(2,1)S(1)}, u32[]{:S(2)}, u32[]{:S(2)}) async-start(bf16[4,8,16,1152]{3,2,1,0:T(8,128)(2,1)} %broadcast_select_fusion), calls=%async_computation.1 | async-start | bytes 2359296 | tf_op jit(solution)/shard_map/all_to_all | solution.py:76

commit v8 on v6

--- a/solution.py
+++ b/solution.py
@@ -59,14 +59,9 @@
         lax.axis_index("c"),
         axis=0,
     )
-    row_ids = jnp.stack(
-        [slot_ids]
-        + [
-            lax.ppermute(slot_ids, "y", [(i, (i - shift) % y_size) for i in range(y_size)])
-            for shift in range(1, y_size)
-        ]
+    row_ids = lax.all_to_all(
+        jnp.broadcast_to(slot_ids[None], (y_size, blocks_dev)), "y", 0, 0, tiled=False
     )
-    row_ids = jnp.roll(row_ids, my_row, axis=0)
     row_table, incoming = lax.optimization_barrier((row_table, incoming))
 
     base_result = jnp.sum(incoming, axis=0)
@@ -83,7 +78,13 @@
     shrunk_partial = jnp.einsum(
         "qzo,qjo->qzj", blocked_input, chosen_down_maps, preferred_element_type=jnp.float32
     ).reshape(rows_dev, rank)
-    shrunk = jnp.sum(lax.all_gather(shrunk_partial, "tp", axis=0, tiled=False), axis=0)
+    shrunk = jnp.sum(
+        lax.all_to_all(
+            jnp.broadcast_to(shrunk_partial[None], (tp_size,) + shrunk_partial.shape),
+            "tp", 0, 0, tiled=False,
+        ),
+        axis=0,
+    )
     low_values = shrunk.astype(jnp.bfloat16)
 
     adapter_result = jnp.einsum(

time: 115 us -> 107 us (0.930)
  the two profiles are of different devices: /device:TPU:2 before, /device:TPU:1 now
where the time goes in v8:
time: 107 us; the launch traced here: 106 us
  blocking collectives  52.3 us (49%)
  starting transfers between devices  24.2 us (23%)
  other arithmetic  10.8 us (10%)
  local copies, waits for them, and re-layouts  8.34 us (8%)
  matrix products  7.81 us (7%)
  waiting for transfers between devices  2.06 us (2%)
    all_gather x1, blocking collectives, shards(): column = lax.all_gather(both_maps, 'z', axis=0, tiled=True)  34.5 us
    all_to_all x1, blocking collectives, shards(): lax.all_to_all(sent.reshape((y_size, blocks_dev) + sent.shape[1:]), 'y',...  17.8 us
    ppermute x1, starting transfers between devices, shards(): lax.ppermute(column, 'c', [(i, (i + shift) % c_size) for i in range(c_siz...  7.21 us
    all_to_all x1, starting transfers between devices, shards(): lax.all_to_all(jnp.broadcast_to(shrunk_partial[None], (tp_size,) + shrunk...  6.96 us
    dot_general x1, matrix products, shards(): jnp.dot(tokens, key_value_weight, preferred_element_type=jnp.float32)  5.84 us
    all_to_all x1, starting transfers between devices, shards(): lax.all_to_all(jnp.broadcast_to(slot_ids[None], (y_size, blocks_dev)), 'y...  5 us
    all_to_all x1, starting transfers between devices, shards(): incoming = lax.all_to_all(outgoing, 'tp', 0, 0, tiled=False)  4.98 us
    reduce_sum x1, other arithmetic, shards(): base_result = jnp.sum(incoming, axis=0)  3.68 us
  transfers between devices with their start and end apart: 4, of which 2 were waited for; matrix products, arithmetic and copies ran while one was open for 13% of the time, Pallas kernels for 0%

profile of v8, /device:TPU:1, one launch (start us, length us, event | category | flops | bytes accessed | tf_op | source)
XLA Modules:
  0.0 105.5 jit_solution(2896902000734672946)
XLA Ops:
  0.0 0.0 copy-start
  0.0 0.8 compare_select_fusion.2
  0.8 1.3 %gather_fusion = s32[8]{0:T(128)S(1)} fusion(s32[128]{0:T(128)} %param.13, s32[1024]{0:T(1024)S(1)} %pad_clamp_fusion), kind=kCustom, calls=%fused_computation | custom fusion | bytes 96 | tf_op jit(solution)/shard_map/gather | solution.py:40
  2.1 0.6 broadcast_in_dim.45
  2.7 5.0 %all-to-all-start.1 = ((s32[4,1,8]{2,1,0:T(1,128)}), s32[4,1,8]{2,1,0:T(1,128)S(1)}, u32[]{:S(2)}, u32[]{:S(2)}) async-start(s32[4,1,8]{2,1,0:T(1,128)} %broadcast_in_dim.45), calls=%async_computation.1 | async-start | bytes 4096 | tf_op jit(solution)/shard_map/all_to_all | solution.py:62
  7.7 0.0 copy-done
  7.7 5.8 %fusion.18 = f32[1024,1024]{0,1:T(8,128)} fusion(bf16[1024,896]{1,0:T(8,128)(2,1)S(1)} %copy-done, bf16[896,1024]{1,0:T(8,128)(2,1)} %param.8), kind=kOutput, calls=%fused_computation.49 | convolution fusion | flops 1879048192 | bytes 7864320 | tf_op jit(solution)/shard_map/dot_general | solution.py:43
  13.5 0.0 all-to-all-done.1
  13.5 0.0 copy-start.3
  13.5 0.0 copy-start.4
  13.5 5.0 %all-to-all-start = ((f32[4,1024,256]{1,2,0:T(8,128)}), f32[4,1024,256]{1,2,0:T(8,128)}, u32[]{:S(2)}, u32[]{:S(2)}) async-start(f32[4,1024,256]{1,2,0:T(8,128)} %bitcast.33), calls=%async_computation | async-start | bytes 8388608 | tf_op jit(solution)/shard_map/all_to_all | solution.py:45
  18.5 0.0 copy-done.3
  18.5 0.0 copy-done.4
  18.6 34.5 %all_gather.3 = bf16[16,16,1152]{2,1,0:T(8,128)(2,1)S(1)} all-gather(bf16[1,16,1152]{2,1,0:T(8,128)(2,1)S(1)} %pad_maximum_fusion), channel_id=1, replica_groups=mesh['y'=4,'z'=16,'c'=2,'tp'=4] {'z'}, dimensions={0}, use_global_device_ids=true | all-gather | bytes 626688 | tf_op jit(solution)/shard_map/all_gather | solution.py:49
  53.1 0.0 copy-start.1
  53.1 7.2 %collective-permute-start = (bf16[16,16,1152]{2,1,0:T(8,128)(2,1)S(1)}, bf16[16,16,1152]{2,1,0:T(8,128)(2,1)S(1)}, u32[]{:S(2)}, u32[]{:S(2)}) collective-permute-start(bf16[16,16,1152]{2,1,0:T(8,128)(2,1)S(1)} %all_gather.3), channel_id=1, source_target_pairs={{0,4},{4,0},{1,5},{5,1},{2,6},{6,2},{3,7},{7,3},{8,12},{12,8},{9,1... | collective-permute-start | bytes 1769480 | tf_op jit(solution)/shard_map/ppermute | solution.py:55
  60.3 0.5 broadcast.251
  60.8 0.7 reduce.3
  61.5 0.1 reshape.222
  61.6 0.3 collective-permute-done
  61.9 0.0 copy-start.2
  61.9 0.0 copy-done.1
  61.9 0.9 copy-done.2
  62.8 2.4 %fusion.2 = bf16[2,16,16,1152]{3,2,1,0:T(8,128)(2,1)S(1)} fusion(s32[]{:T(128)S(6)} %select_n.93, bf16[1,16,16,1152]{3,2,1,0:T(8,128)(2,1)} %bitcast.35, bf16[1,16,16,1152]{3,2,1,0:T(8,128)(2,1)} %bitcast.36), kind=kLoop, calls=%fused_computation.9 | loop fusion | flops 1769472 | bytes 2359300 | tf_op jit(solution)/shard_map/jit(_roll_dynamic)/concatenate | solution.py:51
  65.2 0.0 all-to-all-done
  65.2 1.7 %gather_fusion.1 = bf16[32,16,1152]{2,1,0:T(8,128)(2,1)} fusion(bf16[2,16,16,1152]{3,2,1,0:T(8,128)(2,1)S(1)} %fusion.2, s32[32]{0:T(128)S(1)} %fusion.17), kind=kCustom, calls=%fused_computation.1 | custom fusion | bytes 2359552 | tf_op jit(solution)/shard_map/gather | solution.py:16
  66.9 1.4 %broadcast_select_fusion = bf16[4,8,16,1152]{3,2,1,0:T(8,128)(2,1)S(1)} fusion(bf16[4,8,16,1152]{3,2,1,0:T(8,128)(2,1)} %bitcast.32, pred[4,8]{1,0:T(4,128)(4,1)S(1)} %fusion.9), kind=kLoop, calls=%fused_computation.10 | loop fusion | flops 589824 | bytes 2359328 | tf_op jit(solution)/shard_map/jit(_where)/select_n | solution.py:18
  68.3 17.8 %all_to_all.21 = bf16[4,8,16,1152]{3,2,1,0:T(8,128)(2,1)S(1)} all-to-all(bf16[4,8,16,1152]{3,2,1,0:T(8,128)(2,1)S(1)} %broadcast_select_fusion), channel_id=1, replica_groups=mesh['y'=4,'z'=16,'c'=2,'tp'=4] {'y'}, dimensions={0} | all-to-all | bytes 2359296 | tf_op jit(solution)/shard_map/all_to_all | solution.py:70
  86.1 0.2 reduce_sum.28
  86.3 0.0 copy-start.5
  86.3 0.6 convolution_bitcast_fusion
  87.0 0.7 broadcast_in_dim.49
  87.7 7.0 %all-to-all-start.3 = ((f32[4,1024,16]{1,2,0:T(8,128)}), f32[4,1024,16]{1,2,0:T(8,128)S(1)}, u32[]{:S(2)}, u32[]{:S(2)}) async-start(f32[4,1024,16]{1,2,0:T(8,128)} %broadcast_in_dim.49), calls=%async_computation.3 | async-start | bytes 524288 | tf_op jit(solution)/shard_map/all_to_all | solution.py:82
  94.7 0.0 copy-done.5
  94.7 0.1 fusion.7
  94.7 3.7 %reduce_sum.27 = f32[1024,256]{0,1:T(8,128)} reduce(f32[4,1024,256]{1,2,0:T(8,128)} %all-to-all-done, f32[]{:T(128)} %constant.77.clone.1), dimensions={0}, to_apply=%region_0.1 | reduce | flops 786432 | bytes 5242884 | tf_op jit(solution)/shard_map/reduce_sum | solution.py:67
  98.4 1.8 %all-to-all-done.3 = f32[4,1024,16]{1,2,0:T(8,128)S(1)} async-done(((f32[4,1024,16]{1,2,0:T(8,128)}), f32[4,1024,16]{1,2,0:T(8,128)S(1)}, u32[]{:S(2)}, u32[]{:S(2)}) %all-to-all-start.3) | async-done | bytes 262176 | tf_op jit(solution)/shard_map/all_to_all | solution.py:82
  100.2 1.3 %convolution_multiply_fusion = f32[8,128,256]{2,1,0:T(8,128)} fusion(bf16[8,16,1152]{2,1,0:T(8,128)(2,1)S(1)} %reduce_sum.28, bf16[1024,16]{0,1:T(8,128)(2,1)S(1)} %reduce_sum.29), kind=kOutput, calls=%fused_computation.6 | convolution fusion | flops 8650752 | bytes 1146880 | tf_op jit(solution)/shard_map/bkr,brc->bkc/dot_general | solution.py:90
  101.5 1.6 %copy.13 = f32[1024,256]{0,1:T(8,128)S(1)} copy(f32[1024,256]{1,0:T(8,128)} %bitcast.34) | data formatting | bytes 2097152 | tf_op jit(solution)/shard_map/mul | solution.py:99
  103.1 1.4 %select_convert_fusion = bf16[1024,256]{0,1:T(8,128)(2,1)S(1)} fusion(f32[1024,256]{0,1:T(8,128)} %reduce_sum.27, f32[1024,256]{0,1:T(8,128)S(1)} %copy.13, pred[1024]{0:T(1024)(128)(4,1)S(1)} %fusion.7), kind=kLoop, calls=%fused_computation.12 | loop fusion | flops 786432 | bytes 2622464 | tf_op jit(solution)/shard_map/convert_element_type | solution.py:100
  104.5 1.0 copy.14
  (6 shorter events, 0.1 us)
Async XLA Ops:
  0.0 7.7 %copy-start = (bf16[1024,896]{1,0:T(8,128)(2,1)S(1)}, bf16[1024,896]{1,0:T(8,128)(2,1)}, u32[]{:S(2)}) copy-start(bf16[1024,896]{1,0:T(8,128)(2,1)} %param.7) | copy-start | bytes 5505028
  2.7 10.9 %all-to-all-start.1 = ((s32[4,1,8]{2,1,0:T(1,128)}), s32[4,1,8]{2,1,0:T(1,128)S(1)}, u32[]{:S(2)}, u32[]{:S(2)}) async-start(s32[4,1,8]{2,1,0:T(1,128)} %broadcast_in_dim.45), calls=%async_computation.1 | async-start | bytes 4096 | tf_op jit(solution)/shard_map/all_to_all | solution.py:62
  13.5 5.0 %copy-start.3 = (bf16[1,16,896]{2,1,0:T(8,128)(2,1)S(1)}, bf16[1,16,896]{2,1,0:T(8,128)(2,1)}, u32[]{:S(2)}) copy-start(bf16[1,16,896]{2,1,0:T(8,128)(2,1)} %param.9) | copy-start | bytes 86020
  13.5 5.0 %copy-start.4 = (bf16[1,16,256]{2,1,0:T(8,128)(2,1)S(1)}, bf16[1,16,256]{2,1,0:T(8,128)(2,1)}, u32[]{:S(2)}) copy-start(bf16[1,16,256]{2,1,0:T(8,128)(2,1)} %param.10) | copy-start | bytes 24580
  13.5 51.7 %all-to-all-start = ((f32[4,1024,256]{1,2,0:T(8,128)}), f32[4,1024,256]{1,2,0:T(8,128)}, u32[]{:S(2)}, u32[]{:S(2)}) async-start(f32[4,1024,256]{1,2,0:T(8,128)} %bitcast.33), calls=%async_computation | async-start | bytes 8388608 | tf_op jit(solution)/shard_map/all_to_all | solution.py:45
  53.1 8.8 %copy-start.1 = (bf16[16,16,1152]{2,1,0:T(8,128)(2,1)}, bf16[16,16,1152]{2,1,0:T(8,128)(2,1)S(1)}, u32[]{:S(2)}) copy-start(bf16[16,16,1152]{2,1,0:T(8,128)(2,1)S(1)} %all_gather.3) | copy-start | bytes 1769476
  53.1 8.8 %collective-permute-start = (bf16[16,16,1152]{2,1,0:T(8,128)(2,1)S(1)}, bf16[16,16,1152]{2,1,0:T(8,128)(2,1)S(1)}, u32[]{:S(2)}, u32[]{:S(2)}) collective-permute-start(bf16[16,16,1152]{2,1,0:T(8,128)(2,1)S(1)} %all_gather.3), channel_id=1, source_target_pairs={{0,4},{4,0},{1,5},{5,1},{2,6},{6,2},{3,7},{7,3},{8,12},{12,8},{9,1... | collective-permute-start | bytes 1769480 | tf_op jit(solution)/shard_map/ppermute | solution.py:55
  61.9 0.9 copy-start.2
  86.3 8.4 %copy-start.5 = (s32[8]{0:T(128)S(1)}, s32[8]{0:T(128)}, u32[]{:S(2)}) copy-start(s32[8]{0:T(128)} %param.12) | copy-start | bytes 100
  87.7 12.5 %all-to-all-start.3 = ((f32[4,1024,16]{1,2,0:T(8,128)}), f32[4,1024,16]{1,2,0:T(8,128)S(1)}, u32[]{:S(2)}, u32[]{:S(2)}) async-start(f32[4,1024,16]{1,2,0:T(8,128)} %broadcast_in_dim.49), calls=%async_computation.3 | async-start | bytes 524288 | tf_op jit(solution)/shard_map/all_to_all | solution.py:82

commit v9 on v8

--- a/solution.py
+++ b/solution.py
@@ -41,7 +41,16 @@
     my_row = lax.axis_index("y")
 
     base_partial = jnp.dot(tokens, key_value_weight, preferred_element_type=jnp.float32)
-    outgoing = base_partial.reshape(rows_dev, tp_size, local_columns).transpose(1, 0, 2)
+    peak = jnp.max(jnp.abs(base_partial))
+    exponent = jnp.clip(jnp.floor(jnp.log2(jnp.maximum(peak, 1e-30))), -100.0, 100.0)
+    scaled = (base_partial * jnp.exp2(13.0 - exponent)).astype(jnp.float16)
+    outgoing = jnp.concatenate(
+        [
+            scaled.reshape(rows_dev, tp_size, local_columns).transpose(1, 0, 2),
+            jnp.broadcast_to(exponent.astype(jnp.float16), (tp_size, 16, local_columns)),
+        ],
+        axis=1,
+    )
     incoming = lax.all_to_all(outgoing, "tp", 0, 0, tiled=False)
 
     both_maps = jnp.concatenate([adapter_down_maps, adapter_up_maps], axis=2)
@@ -64,7 +73,10 @@
     )
     row_table, incoming = lax.optimization_barrier((row_table, incoming))
 
-    base_result = jnp.sum(incoming, axis=0)
+    unscale = jnp.exp2(incoming[:, rows_dev, 0].astype(jnp.float32) - 13.0)
+    base_result = jnp.sum(
+        incoming[:, :rows_dev].astype(jnp.float32) * unscale[:, None, None], axis=0
+    )
 
     sent = pick_entries(row_table, row_ids.reshape(-1), my_row, per_row, per_column)
     received = lax.all_to_all(

time: 107 us -> 118 us (1.10)
  blocking collectives: 52.3 us -> 33.4 us
  waiting for transfers between devices: 2.06 us -> 18.7 us
  local copies, waits for them, and re-layouts: 8.34 us -> 13.4 us
  other arithmetic: 10.8 us -> 15.8 us
  starting transfers between devices: 24.2 us -> 27.2 us
    all_to_all x1 -> x0, blocking collectives: 17.8 us -> none  [shards(): lax.all_to_all(sent.reshape((y_size, blocks_dev) + sent.shape[1:]), 'y',...]
    all_to_all x0 -> x1, waiting for transfers between devices: none -> 15.1 us  [shards(): lax.all_to_all(sent.reshape((y_size, blocks_dev) + sent.shape[1:]), 'y',...]
    all_to_all x0 -> x1, starting transfers between devices: none -> 4.52 us  [shards(): lax.all_to_all(sent.reshape((y_size, blocks_dev) + sent.shape[1:]), 'y',...]
    reshape x0 -> x1, local copies, waits for them, and re-layouts: none -> 4.25 us  [shards(): scaled.reshape(rows_dev, tp_size, local_columns).transpose(1, 0, 2)]
    convert_element_type x0 -> x1, other arithmetic: none -> 4.13 us  [shards(): scaled = (base_partial * jnp.exp2(13.0 - exponent)).astype(jnp.float16)]
    concatenate x0 -> x1, local copies, waits for them, and re-layouts: none -> 3.37 us  [shards(): jnp.concatenate([scaled.reshape(rows_dev, tp_size, local_columns).transpo...]
    all_to_all x1, starting transfers between devices: 6.96 us -> 4.71 us  [shards(): lax.all_to_all(jnp.broadcast_to(shrunk_partial[None], (tp_size,) + shrunk...]
    all_to_all x1, waiting for transfers between devices: 1.77 us -> 3.39 us  [shards(): lax.all_to_all(jnp.broadcast_to(shrunk_partial[None], (tp_size,) + shrunk...]
  transfers between devices with their start and end apart: 4 -> 5, of which waited for: 2 -> 3; matrix products, arithmetic and copies ran while one was open for 13% -> 21% of each run, Pallas kernels for 0% -> 0%
where the time goes in v9:
time: 118 us; the launch traced here: 117 us
  blocking collectives  33.4 us (28%)
  starting transfers between devices  27.2 us (23%)
  waiting for transfers between devices  18.7 us (16%)
  other arithmetic  15.8 us (13%)
  local copies, waits for them, and re-layouts  13.4 us (11%)
  matrix products  7.4 us (6%)
    all_gather x1, blocking collectives, shards(): column = lax.all_gather(both_maps, 'z', axis=0, tiled=True)  33.4 us
    all_to_all x1, waiting for transfers between devices, shards(): lax.all_to_all(sent.reshape((y_size, blocks_dev) + sent.shape[1:]), 'y',...  15.1 us
    ppermute x1, starting transfers between devices, shards(): lax.ppermute(column, 'c', [(i, (i + shift) % c_size) for i in range(c_siz...  8.34 us
    dot_general x1, matrix products, shards(): jnp.dot(tokens, key_value_weight, preferred_element_type=jnp.float32)  6.42 us
    all_to_all x1, starting transfers between devices, shards(): lax.all_to_all(jnp.broadcast_to(slot_ids[None], (y_size, blocks_dev)), 'y...  5 us
    all_to_all x1, starting transfers between devices, shards(): lax.all_to_all(jnp.broadcast_to(shrunk_partial[None], (tp_size,) + shrunk...  4.71 us
    all_to_all x1, starting transfers between devices, shards(): incoming = lax.all_to_all(outgoing, 'tp', 0, 0, tiled=False)  4.58 us
    all_to_all x1, starting transfers between devices, shards(): lax.all_to_all(sent.reshape((y_size, blocks_dev) + sent.shape[1:]), 'y',...  4.52 us
  transfers between devices with their start and end apart: 5, of which 3 were waited for; matrix products, arithmetic and copies ran while one was open for 21% of the time, Pallas kernels for 0%

profile of v9, /device:TPU:1, one launch (start us, length us, event | category | flops | bytes accessed | tf_op | source)
XLA Modules:
  0.0 116.7 jit_solution(18367493793132872518)
XLA Ops:
  0.0 0.0 copy-start
  0.0 0.8 compare_select_fusion.2
  0.8 1.3 %gather_fusion = s32[8]{0:T(128)S(1)} fusion(s32[128]{0:T(128)} %param.13, s32[1024]{0:T(1024)S(1)} %pad_clamp_fusion), kind=kCustom, calls=%fused_computation | custom fusion | bytes 96 | tf_op jit(solution)/shard_map/gather | solution.py:40
  2.1 0.6 broadcast_in_dim.47
  2.7 5.0 %all-to-all-start.1 = ((s32[4,1,8]{2,1,0:T(1,128)}), s32[4,1,8]{2,1,0:T(1,128)S(1)}, u32[]{:S(2)}, u32[]{:S(2)}) async-start(s32[4,1,8]{2,1,0:T(1,128)} %broadcast_in_dim.47), calls=%async_computation.1 | async-start | bytes 4096 | tf_op jit(solution)/shard_map/all_to_all | solution.py:71
  7.7 0.0 copy-done
  7.7 6.4 %abs_reduce_fusion = (f32[]{:T(128)}, f32[1024,1024]{0,1:T(8,128)}) fusion(bf16[1024,896]{1,0:T(8,128)(2,1)S(1)} %copy-done, bf16[896,1024]{1,0:T(8,128)(2,1)} %param.8), kind=kOutput, calls=%fused_computation.4 | convolution fusion | flops 1881145344 | bytes 7864324 | tf_op jit(solution)/shard_map/dot_general | solution.py:43
  14.8 4.1 %multiply_convert_fusion = f16[1024,1024]{0,1:T(8,128)(2,1)} fusion(f32[1024,1024]{0,1:T(8,128)} %get-tuple-element.12, f32[]{:T(128)S(6)} %exp2.15), kind=kLoop, calls=%fused_computation.3 | loop fusion | flops 2097152 | bytes 6291460 | tf_op jit(solution)/shard_map/convert_element_type | solution.py:46
  19.0 4.2 %copy.16 = f16[1024,4,256]{2,0,1:T(8,128)(2,1)} copy(f16[1024,4,256]{0,2,1:T(8,128)(2,1)} %bitcast.36) | data formatting | bytes 4194304 | tf_op jit(solution)/shard_map/reshape | solution.py:49
  23.2 3.4 %concatenate.15 = f16[4,1040,256]{2,1,0:T(8,128)(2,1)} pad(f16[4,1024,256]{2,1,0:T(8,128)(2,1)} %bitcast.37, f16[]{:T(256)S(6)} %convert_element_type.24), padding=0_0x0_16x0_0 | pad | bytes 4227074 | tf_op jit(solution)/shard_map/concatenate | solution.py:47
  26.6 0.0 copy-start.3
  26.6 0.0 copy-start.4
  26.6 0.0 all-to-all-done.1
  26.6 4.6 %all-to-all-start = ((f16[4,1040,256]{2,1,0:T(8,128)(2,1)}), f16[4,1040,256]{2,1,0:T(8,128)(2,1)}, u32[]{:S(2)}, u32[]{:S(2)}) async-start(f16[4,1040,256]{2,1,0:T(8,128)(2,1)} %concatenate.15), calls=%async_computation | async-start | bytes 4259840 | tf_op jit(solution)/shard_map/all_to_all | solution.py:54
  31.2 0.0 copy-done.3
  31.2 0.0 copy-done.4
  31.2 33.4 %all_gather.3 = bf16[16,16,1152]{2,1,0:T(8,128)(2,1)S(1)} all-gather(bf16[1,16,1152]{2,1,0:T(8,128)(2,1)S(1)} %pad_maximum_fusion), channel_id=1, replica_groups=mesh['y'=4,'z'=16,'c'=2,'tp'=4] {'z'}, dimensions={0}, use_global_device_ids=true | all-gather | bytes 626688 | tf_op jit(solution)/shard_map/all_gather | solution.py:58
  64.6 0.0 copy-start.1
  64.6 8.3 %collective-permute-start = (bf16[16,16,1152]{2,1,0:T(8,128)(2,1)S(1)}, bf16[16,16,1152]{2,1,0:T(8,128)(2,1)S(1)}, u32[]{:S(2)}, u32[]{:S(2)}) collective-permute-start(bf16[16,16,1152]{2,1,0:T(8,128)(2,1)S(1)} %all_gather.3), channel_id=1, source_target_pairs={{0,4},{4,0},{1,5},{5,1},{2,6},{6,2},{3,7},{7,3},{8,12},{12,8},{9,1... | collective-permute-start | bytes 1769480 | tf_op jit(solution)/shard_map/ppermute | solution.py:64
  73.0 0.5 broadcast.267
  73.5 0.7 reduce.5
  74.1 0.1 reshape.222
  74.3 0.3 collective-permute-done
  74.6 0.0 copy-start.2
  74.6 0.0 copy-done.1
  74.6 0.8 copy-done.2
  75.4 2.3 %fusion.2 = bf16[2,16,16,1152]{3,2,1,0:T(8,128)(2,1)S(1)} fusion(s32[]{:T(128)S(6)} %select_n.93, bf16[1,16,16,1152]{3,2,1,0:T(8,128)(2,1)} %bitcast.39, bf16[1,16,16,1152]{3,2,1,0:T(8,128)(2,1)} %bitcast.40), kind=kLoop, calls=%fused_computation.12 | loop fusion | flops 1769472 | bytes 2359300 | tf_op jit(solution)/shard_map/jit(_roll_dynamic)/concatenate | solution.py:60
  77.7 0.0 all-to-all-done
  77.7 1.7 %gather_fusion.1 = bf16[32,16,1152]{2,1,0:T(8,128)(2,1)} fusion(bf16[2,16,16,1152]{3,2,1,0:T(8,128)(2,1)S(1)} %fusion.2, s32[32]{0:T(128)S(1)} %fusion.19), kind=kCustom, calls=%fused_computation.1 | custom fusion | bytes 2359552 | tf_op jit(solution)/shard_map/gather | solution.py:16
  79.4 0.0 copy-start.5
  79.4 2.5 %broadcast_select_fusion = bf16[4,8,16,1152]{3,2,1,0:T(8,128)(2,1)} fusion(bf16[4,8,16,1152]{3,2,1,0:T(8,128)(2,1)} %bitcast.38, pred[4,8]{1,0:T(4,128)(4,1)S(1)} %fusion.11), kind=kLoop, calls=%fused_computation.13 | loop fusion | flops 589824 | bytes 2359328 | tf_op jit(solution)/shard_map/jit(_where)/select_n | solution.py:18
  81.9 4.5 %all-to-all-start.2 = ((bf16[4,8,16,1152]{3,2,1,0:T(8,128)(2,1)}), bf16[4,8,16,1152]{3,2,1,0:T(8,128)(2,1)S(1)}, u32[]{:S(2)}, u32[]{:S(2)}) async-start(bf16[4,8,16,1152]{3,2,1,0:T(8,128)(2,1)} %broadcast_select_fusion), calls=%async_computation.2 | async-start | bytes 2359296 | tf_op jit(solution)/shard_map/all_to_all | solution.py:82
  86.5 0.0 copy-done.5
  86.5 0.1 fusion.9
  86.5 0.8 exponential_reduce_fusion
  87.4 15.1 %all-to-all-done.2 = bf16[4,8,16,1152]{3,2,1,0:T(8,128)(2,1)S(1)} async-done(((bf16[4,8,16,1152]{3,2,1,0:T(8,128)(2,1)}), bf16[4,8,16,1152]{3,2,1,0:T(8,128)(2,1)S(1)}, u32[]{:S(2)}, u32[]{:S(2)}) %all-to-all-start.2) | async-done | bytes 1179680 | tf_op jit(solution)/shard_map/all_to_all | solution.py:82
  102.4 0.2 reduce_sum.28
  102.6 0.6 convolution_bitcast_fusion
  103.2 0.7 broadcast_in_dim.51
  104.0 4.7 %all-to-all-start.3 = ((f32[4,1024,16]{1,2,0:T(8,128)}), f32[4,1024,16]{1,2,0:T(8,128)}, u32[]{:S(2)}, u32[]{:S(2)}) async-start(f32[4,1024,16]{1,2,0:T(8,128)} %broadcast_in_dim.51), calls=%async_computation.3 | async-start | bytes 524288 | tf_op jit(solution)/shard_map/all_to_all | solution.py:94
  108.7 2.2 %multiply_reduce_fusion = f32[1024,256]{1,0:T(8,128)S(1)} fusion(f32[4]{0:T(128)S(1)} %exponential_reduce_fusion, f16[4,1040,256]{2,1,0:T(8,128)(2,1)} %all-to-all-done), kind=kLoop, calls=%fused_computation.2 | loop fusion | flops 2883584 | bytes 3145744 | tf_op jit(solution)/shard_map/reduce_sum | solution.py:77
  110.9 3.4 %all-to-all-done.3 = f32[4,1024,16]{1,2,0:T(8,128)} async-done(((f32[4,1024,16]{1,2,0:T(8,128)}), f32[4,1024,16]{1,2,0:T(8,128)}, u32[]{:S(2)}, u32[]{:S(2)}) %all-to-all-start.3) | async-done | bytes 262176 | tf_op jit(solution)/shard_map/all_to_all | solution.py:94
  114.3 1.0 reduce_sum.29
  115.3 0.3 convolution_multiply_fusion
  115.6 1.0 fusion.4
  (5 shorter events, 0.1 us)
Async XLA Ops:
  0.0 7.7 %copy-start = (bf16[1024,896]{1,0:T(8,128)(2,1)S(1)}, bf16[1024,896]{1,0:T(8,128)(2,1)}, u32[]{:S(2)}) copy-start(bf16[1024,896]{1,0:T(8,128)(2,1)} %param.7) | copy-start | bytes 5505028
  2.7 23.9 %all-to-all-start.1 = ((s32[4,1,8]{2,1,0:T(1,128)}), s32[4,1,8]{2,1,0:T(1,128)S(1)}, u32[]{:S(2)}, u32[]{:S(2)}) async-start(s32[4,1,8]{2,1,0:T(1,128)} %broadcast_in_dim.47), calls=%async_computation.1 | async-start | bytes 4096 | tf_op jit(solution)/shard_map/all_to_all | solution.py:71
  26.6 4.6 %copy-start.3 = (bf16[1,16,896]{2,1,0:T(8,128)(2,1)S(1)}, bf16[1,16,896]{2,1,0:T(8,128)(2,1)}, u32[]{:S(2)}) copy-start(bf16[1,16,896]{2,1,0:T(8,128)(2,1)} %param.9) | copy-start | bytes 86020
  26.6 4.6 %copy-start.4 = (bf16[1,16,256]{2,1,0:T(8,128)(2,1)S(1)}, bf16[1,16,256]{2,1,0:T(8,128)(2,1)}, u32[]{:S(2)}) copy-start(bf16[1,16,256]{2,1,0:T(8,128)(2,1)} %param.10) | copy-start | bytes 24580
  26.6 51.1 %all-to-all-start = ((f16[4,1040,256]{2,1,0:T(8,128)(2,1)}), f16[4,1040,256]{2,1,0:T(8,128)(2,1)}, u32[]{:S(2)}, u32[]{:S(2)}) async-start(f16[4,1040,256]{2,1,0:T(8,128)(2,1)} %concatenate.15), calls=%async_computation | async-start | bytes 4259840 | tf_op jit(solution)/shard_map/all_to_all | solution.py:54
  64.6 10.0 %copy-start.1 = (bf16[16,16,1152]{2,1,0:T(8,128)(2,1)}, bf16[16,16,1152]{2,1,0:T(8,128)(2,1)S(1)}, u32[]{:S(2)}) copy-start(bf16[16,16,1152]{2,1,0:T(8,128)(2,1)S(1)} %all_gather.3) | copy-start | bytes 1769476
  64.6 10.0 %collective-permute-start = (bf16[16,16,1152]{2,1,0:T(8,128)(2,1)S(1)}, bf16[16,16,1152]{2,1,0:T(8,128)(2,1)S(1)}, u32[]{:S(2)}, u32[]{:S(2)}) collective-permute-start(bf16[16,16,1152]{2,1,0:T(8,128)(2,1)S(1)} %all_gather.3), channel_id=1, source_target_pairs={{0,4},{4,0},{1,5},{5,1},{2,6},{6,2},{3,7},{7,3},{8,12},{12,8},{9,1... | collective-permute-start | bytes 1769480 | tf_op jit(solution)/shard_map/ppermute | solution.py:64
  74.6 0.8 copy-start.2
  79.4 7.0 %copy-start.5 = (s32[8]{0:T(128)S(1)}, s32[8]{0:T(128)}, u32[]{:S(2)}) copy-start(s32[8]{0:T(128)} %param.12) | copy-start | bytes 100
  81.9 20.5 %all-to-all-start.2 = ((bf16[4,8,16,1152]{3,2,1,0:T(8,128)(2,1)}), bf16[4,8,16,1152]{3,2,1,0:T(8,128)(2,1)S(1)}, u32[]{:S(2)}, u32[]{:S(2)}) async-start(bf16[4,8,16,1152]{3,2,1,0:T(8,128)(2,1)} %broadcast_select_fusion), calls=%async_computation.2 | async-start | bytes 2359296 | tf_op jit(solution)/shard_map/all_to_all | solution.py:82
  104.0 10.3 %all-to-all-start.3 = ((f32[4,1024,16]{1,2,0:T(8,128)}), f32[4,1024,16]{1,2,0:T(8,128)}, u32[]{:S(2)}, u32[]{:S(2)}) async-start(f32[4,1024,16]{1,2,0:T(8,128)} %broadcast_in_dim.51), calls=%async_computation.3 | async-start | bytes 524288 | tf_op jit(solution)/shard_map/all_to_all | solution.py:94

commit v10 on v8

--- a/solution.py
+++ b/solution.py
@@ -10,10 +10,10 @@
 ROWS = ("y", "z", "c")
 
 
-def pick_entries(table, wanted, own_row, per_row, per_column):
+def pick_entries(table, wanted, own_row, own_column, per_row, per_column):
     row_of = wanted // per_row
     inside = wanted % per_row
-    entries = table[inside % per_column, inside // per_column]
+    entries = table[(own_column - inside % per_column) % per_column, inside // per_column]
     keep = (row_of == own_row)[:, None, None]
     return jnp.where(keep, entries, jnp.zeros_like(entries))
 
@@ -48,16 +48,12 @@
     both_maps, outgoing = lax.optimization_barrier((both_maps, outgoing))
     column = lax.all_gather(both_maps, "z", axis=0, tiled=True)
     c_size = lax.axis_size("c")
-    row_table = jnp.roll(
-        jnp.stack(
-            [column]
-            + [
-                lax.ppermute(column, "c", [(i, (i + shift) % c_size) for i in range(c_size)])
-                for shift in range(1, c_size)
-            ]
-        ),
-        lax.axis_index("c"),
-        axis=0,
+    row_table = jnp.stack(
+        [column]
+        + [
+            lax.ppermute(column, "c", [(i, (i + shift) % c_size) for i in range(c_size)])
+            for shift in range(1, c_size)
+        ]
     )
     row_ids = lax.all_to_all(
         jnp.broadcast_to(slot_ids[None], (y_size, blocks_dev)), "y", 0, 0, tiled=False
@@ -66,7 +62,9 @@
 
     base_result = jnp.sum(incoming, axis=0)
 
-    sent = pick_entries(row_table, row_ids.reshape(-1), my_row, per_row, per_column)
+    sent = pick_entries(
+        row_table, row_ids.reshape(-1), my_row, lax.axis_index("c"), per_row, per_column
+    )
     received = lax.all_to_all(
         sent.reshape((y_size, blocks_dev) + sent.shape[1:]), "y", 0, 0, tiled=False
     )

time: 107 us -> 106 us (level)
  the two profiles are of different devices: /device:TPU:1 before, /device:TPU:480 now
where the time goes in v10:
time: 106 us; the launch traced here: 105 us
  blocking collectives  48.6 us (46%)
  waiting for transfers between devices  18 us (17%)
  starting transfers between devices  14.8 us (14%)
  other arithmetic  8.32 us (8%)
  matrix products  7.84 us (7%)
  local copies, waits for them, and re-layouts  7.8 us (7%)
    all_gather x1, blocking collectives, shards(): column = lax.all_gather(both_maps, 'z', axis=0, tiled=True)  29.2 us
    all_to_all x1, blocking collectives, shards(): lax.all_to_all(sent.reshape((y_size, blocks_dev) + sent.shape[1:]), 'y',...  19.4 us
    all_to_all x1, waiting for transfers between devices, shards(): incoming = lax.all_to_all(outgoing, 'tp', 0, 0, tiled=False)  14.5 us
    dot_general x1, matrix products, shards(): jnp.dot(tokens, key_value_weight, preferred_element_type=jnp.float32)  5.85 us
    all_to_all x1, starting transfers between devices, shards(): incoming = lax.all_to_all(outgoing, 'tp', 0, 0, tiled=False)  5 us
    all_to_all x1, starting transfers between devices, shards(): lax.all_to_all(jnp.broadcast_to(slot_ids[None], (y_size, blocks_dev)), 'y...  4.46 us
    reduce_sum x1, other arithmetic, shards(): base_result = jnp.sum(incoming, axis=0)  3.69 us
    all_to_all x1, starting transfers between devices, shards(): lax.all_to_all(jnp.broadcast_to(shrunk_partial[None], (tp_size,) + shrunk...  3.41 us
  transfers between devices with their start and end apart: 4, of which 3 were waited for; matrix products, arithmetic and copies ran while one was open for 12% of the time, Pallas kernels for 0%

profile of v10, /device:TPU:480, one launch (start us, length us, event | category | flops | bytes accessed | tf_op | source)
XLA Modules:
  0.0 105.5 jit_solution(2866849495335677633)
XLA Ops:
  0.0 0.0 copy-start
  0.0 0.8 compare_select_fusion.2
  0.8 1.3 %gather_fusion = s32[8]{0:T(128)S(1)} fusion(s32[128]{0:T(128)} %param.13, s32[1024]{0:T(1024)S(1)} %pad_clamp_fusion), kind=kCustom, calls=%fused_computation | custom fusion | bytes 96 | tf_op jit(solution)/shard_map/gather | solution.py:40
  2.1 0.6 broadcast_in_dim.45
  2.7 4.5 %all-to-all-start.1 = ((s32[4,1,8]{2,1,0:T(1,128)}), s32[4,1,8]{2,1,0:T(1,128)S(1)}, u32[]{:S(2)}, u32[]{:S(2)}) async-start(s32[4,1,8]{2,1,0:T(1,128)} %broadcast_in_dim.45), calls=%async_computation.1 | async-start | bytes 4096 | tf_op jit(solution)/shard_map/all_to_all | solution.py:58
  7.2 0.0 copy-done
  7.2 5.9 %fusion.17 = f32[1024,1024]{0,1:T(8,128)} fusion(bf16[1024,896]{1,0:T(8,128)(2,1)S(1)} %copy-done, bf16[896,1024]{1,0:T(8,128)(2,1)} %param.8), kind=kOutput, calls=%fused_computation.48 | convolution fusion | flops 1879048192 | bytes 7864320 | tf_op jit(solution)/shard_map/dot_general | solution.py:43
  13.0 0.0 all-to-all-done.1
  13.0 0.0 copy-start.1
  13.0 0.0 copy-start.2
  13.0 5.0 %all-to-all-start = ((f32[4,1024,256]{1,2,0:T(8,128)}), f32[4,1024,256]{1,2,0:T(8,128)}, u32[]{:S(2)}, u32[]{:S(2)}) async-start(f32[4,1024,256]{1,2,0:T(8,128)} %bitcast.33), calls=%async_computation | async-start | bytes 8388608 | tf_op jit(solution)/shard_map/all_to_all | solution.py:45
  18.0 0.0 copy-done.1
  18.0 0.0 copy-done.2
  18.1 29.2 %all_gather.3 = bf16[16,16,1152]{2,1,0:T(8,128)(2,1)S(1)} all-gather(bf16[1,16,1152]{2,1,0:T(8,128)(2,1)S(1)} %pad_maximum_fusion.1), channel_id=1, replica_groups=mesh['y'=4,'z'=16,'c'=2,'tp'=4] {'z'}, dimensions={0}, use_global_device_ids=true | all-gather | bytes 626688 | tf_op jit(solution)/shard_map/all_gather | solution.py:49
  47.3 1.9 %collective-permute-start = (bf16[16,16,1152]{2,1,0:T(8,128)(2,1)S(1)}, bf16[16,16,1152]{2,1,0:T(8,128)(2,1)S(1)}, u32[]{:S(2)}, u32[]{:S(2)}) collective-permute-start(bf16[16,16,1152]{2,1,0:T(8,128)(2,1)S(1)} %all_gather.3), channel_id=1, source_target_pairs={{0,4},{4,0},{1,5},{5,1},{2,6},{6,2},{3,7},{7,3},{8,12},{12,8},{9,1... | collective-permute-start | bytes 1769480 | tf_op jit(solution)/shard_map/ppermute | solution.py:54
  49.2 0.5 broadcast.294
  49.7 0.7 reduce.3
  50.4 0.1 reshape.258
  50.5 0.6 collective-permute-done
  51.2 1.2 %pad_maximum_fusion = bf16[2,16,16,1152]{3,2,1,0:T(8,128)(2,1)} fusion(bf16[1,16,16,1152]{3,2,1,0:T(8,128)(2,1)S(1)} %bitcast.36, bf16[1,16,16,1152]{3,2,1,0:T(8,128)(2,1)S(1)} %bitcast.35), kind=kLoop, calls=%fused_computation.3 | loop fusion | flops 589824 | bytes 2359296 | tf_op jit(solution)/shard_map/stack | solution.py:51
  52.4 14.5 %all-to-all-done = f32[4,1024,256]{1,2,0:T(8,128)} async-done(((f32[4,1024,256]{1,2,0:T(8,128)}), f32[4,1024,256]{1,2,0:T(8,128)}, u32[]{:S(2)}, u32[]{:S(2)}) %all-to-all-start) | async-done | bytes 4194336 | tf_op jit(solution)/shard_map/all_to_all | solution.py:45
  66.9 2.0 %gather_fusion.1 = bf16[32,16,1152]{2,1,0:T(8,128)(2,1)S(1)} fusion(bf16[2,16,16,1152]{3,2,1,0:T(8,128)(2,1)} %pad_maximum_fusion, s32[32]{0:T(128)S(1)} %fusion.16), kind=kCustom, calls=%fused_computation.1 | custom fusion | bytes 2359552 | tf_op jit(solution)/shard_map/gather | solution.py:16
  68.9 0.2 broadcast_select_fusion
  69.1 19.4 %all_to_all.21 = bf16[4,8,16,1152]{3,2,1,0:T(8,128)(2,1)S(1)} all-to-all(bf16[4,8,16,1152]{3,2,1,0:T(8,128)(2,1)S(1)} %broadcast_select_fusion), channel_id=1, replica_groups=mesh['y'=4,'z'=16,'c'=2,'tp'=4] {'y'}, dimensions={0} | all-to-all | bytes 2359296 | tf_op jit(solution)/shard_map/all_to_all | solution.py:68
  88.5 0.2 reduce_sum.28
  88.7 0.0 copy-start.3
  88.7 0.6 convolution_bitcast_fusion
  89.3 0.7 broadcast_in_dim.49
  90.1 3.4 %all-to-all-start.3 = ((f32[4,1024,16]{1,2,0:T(8,128)}), f32[4,1024,16]{1,2,0:T(8,128)S(1)}, u32[]{:S(2)}, u32[]{:S(2)}) async-start(f32[4,1024,16]{1,2,0:T(8,128)} %broadcast_in_dim.49), calls=%async_computation.3 | async-start | bytes 524288 | tf_op jit(solution)/shard_map/all_to_all | solution.py:80
  93.5 0.0 copy-done.3
  93.5 0.1 fusion.4
  93.6 3.7 %reduce_sum.27 = f32[1024,256]{0,1:T(8,128)} reduce(f32[4,1024,256]{1,2,0:T(8,128)} %all-to-all-done, f32[]{:T(128)} %constant.61.clone.1), dimensions={0}, to_apply=%region_0.0 | reduce | flops 786432 | bytes 5242884 | tf_op jit(solution)/shard_map/reduce_sum | solution.py:63
  97.3 2.9 %all-to-all-done.3 = f32[4,1024,16]{1,2,0:T(8,128)S(1)} async-done(((f32[4,1024,16]{1,2,0:T(8,128)}), f32[4,1024,16]{1,2,0:T(8,128)S(1)}, u32[]{:S(2)}, u32[]{:S(2)}) %all-to-all-start.3) | async-done | bytes 262176 | tf_op jit(solution)/shard_map/all_to_all | solution.py:80
  100.1 1.3 %convolution_multiply_fusion = f32[8,128,256]{2,1,0:T(8,128)} fusion(bf16[8,16,1152]{2,1,0:T(8,128)(2,1)S(1)} %reduce_sum.28, bf16[1024,16]{0,1:T(8,128)(2,1)S(1)} %reduce_sum.29), kind=kOutput, calls=%fused_computation.2 | convolution fusion | flops 8650752 | bytes 1146880 | tf_op jit(solution)/shard_map/bkr,brc->bkc/dot_general | solution.py:88
  101.5 1.6 %copy.13 = f32[1024,256]{0,1:T(8,128)S(1)} copy(f32[1024,256]{1,0:T(8,128)} %bitcast.34) | data formatting | bytes 2097152 | tf_op jit(solution)/shard_map/mul | solution.py:97
  103.0 1.4 %select_convert_fusion = bf16[1024,256]{0,1:T(8,128)(2,1)S(1)} fusion(f32[1024,256]{0,1:T(8,128)} %reduce_sum.27, f32[1024,256]{0,1:T(8,128)S(1)} %copy.13, pred[1024]{0:T(1024)(128)(4,1)S(1)} %fusion.4), kind=kLoop, calls=%fused_computation.6 | loop fusion | flops 786432 | bytes 2622464 | tf_op jit(solution)/shard_map/convert_element_type | solution.py:98
  104.5 1.0 copy.14
  (6 shorter events, 0.1 us)
Async XLA Ops:
  0.0 7.2 %copy-start = (bf16[1024,896]{1,0:T(8,128)(2,1)S(1)}, bf16[1024,896]{1,0:T(8,128)(2,1)}, u32[]{:S(2)}) copy-start(bf16[1024,896]{1,0:T(8,128)(2,1)} %param.7) | copy-start | bytes 5505028
  2.7 10.3 %all-to-all-start.1 = ((s32[4,1,8]{2,1,0:T(1,128)}), s32[4,1,8]{2,1,0:T(1,128)S(1)}, u32[]{:S(2)}, u32[]{:S(2)}) async-start(s32[4,1,8]{2,1,0:T(1,128)} %broadcast_in_dim.45), calls=%async_computation.1 | async-start | bytes 4096 | tf_op jit(solution)/shard_map/all_to_all | solution.py:58
  13.0 5.0 %copy-start.1 = (bf16[1,16,896]{2,1,0:T(8,128)(2,1)S(1)}, bf16[1,16,896]{2,1,0:T(8,128)(2,1)}, u32[]{:S(2)}) copy-start(bf16[1,16,896]{2,1,0:T(8,128)(2,1)} %param.9) | copy-start | bytes 86020
  13.0 5.0 %copy-start.2 = (bf16[1,16,256]{2,1,0:T(8,128)(2,1)S(1)}, bf16[1,16,256]{2,1,0:T(8,128)(2,1)}, u32[]{:S(2)}) copy-start(bf16[1,16,256]{2,1,0:T(8,128)(2,1)} %param.10) | copy-start | bytes 24580
  13.0 53.9 %all-to-all-start = ((f32[4,1024,256]{1,2,0:T(8,128)}), f32[4,1024,256]{1,2,0:T(8,128)}, u32[]{:S(2)}, u32[]{:S(2)}) async-start(f32[4,1024,256]{1,2,0:T(8,128)} %bitcast.33), calls=%async_computation | async-start | bytes 8388608 | tf_op jit(solution)/shard_map/all_to_all | solution.py:45
  47.3 3.9 %collective-permute-start = (bf16[16,16,1152]{2,1,0:T(8,128)(2,1)S(1)}, bf16[16,16,1152]{2,1,0:T(8,128)(2,1)S(1)}, u32[]{:S(2)}, u32[]{:S(2)}) collective-permute-start(bf16[16,16,1152]{2,1,0:T(8,128)(2,1)S(1)} %all_gather.3), channel_id=1, source_target_pairs={{0,4},{4,0},{1,5},{5,1},{2,6},{6,2},{3,7},{7,3},{8,12},{12,8},{9,1... | collective-permute-start | bytes 1769480 | tf_op jit(solution)/shard_map/ppermute | solution.py:54
  88.7 4.8 %copy-start.3 = (s32[8]{0:T(128)S(1)}, s32[8]{0:T(128)}, u32[]{:S(2)}) copy-start(s32[8]{0:T(128)} %param.12) | copy-start | bytes 100
  90.1 10.1 %all-to-all-start.3 = ((f32[4,1024,16]{1,2,0:T(8,128)}), f32[4,1024,16]{1,2,0:T(8,128)S(1)}, u32[]{:S(2)}, u32[]{:S(2)}) async-start(f32[4,1024,16]{1,2,0:T(8,128)} %broadcast_in_dim.49), calls=%async_computation.3 | async-start | bytes 524288 | tf_op jit(solution)/shard_map/all_to_all | solution.py:80

commit v11 on v10

--- a/solution.py
+++ b/solution.py
@@ -3,6 +3,7 @@
 import jax
 import jax.numpy as jnp
 from jax import lax
+from jax.experimental.layout import Layout, with_layout_constraint
 from jax.sharding import Mesh
 from jax.sharding import PartitionSpec as P
 
@@ -60,7 +61,7 @@
     )
     row_table, incoming = lax.optimization_barrier((row_table, incoming))
 
-    base_result = jnp.sum(incoming, axis=0)
+    base_result = with_layout_constraint(jnp.sum(incoming, axis=0), Layout((0, 1)))
 
     sent = pick_entries(
         row_table, row_ids.reshape(-1), my_row, lax.axis_index("c"), per_row, per_column

time: 106 us -> 104 us (0.981)
  the two profiles are of different devices: /device:TPU:480 before, /device:TPU:192 now
where the time goes in v11:
time: 104 us; the launch traced here: 103 us
  blocking collectives  50.5 us (49%)
  starting transfers between devices  15.4 us (15%)
  waiting for transfers between devices  14.7 us (14%)
  other arithmetic  8.86 us (9%)
  matrix products  6.84 us (7%)
  local copies, waits for them, and re-layouts  6.8 us (7%)
    all_gather x1, blocking collectives, shards(): column = lax.all_gather(both_maps, 'z', axis=0, tiled=True)  31.1 us
    all_to_all x1, blocking collectives, shards(): lax.all_to_all(sent.reshape((y_size, blocks_dev) + sent.shape[1:]), 'y',...  19.4 us
    all_to_all x1, waiting for transfers between devices, shards(): incoming = lax.all_to_all(outgoing, 'tp', 0, 0, tiled=False)  12.7 us
    dot_general x1, matrix products, shards(): jnp.dot(tokens, key_value_weight, preferred_element_type=jnp.float32)  5.85 us
    all_to_all x1, starting transfers between devices, shards(): incoming = lax.all_to_all(outgoing, 'tp', 0, 0, tiled=False)  5 us
    all_to_all x1, starting transfers between devices, shards(): lax.all_to_all(jnp.broadcast_to(slot_ids[None], (y_size, blocks_dev)), 'y...  4.46 us
    all_to_all x1, starting transfers between devices, shards(): lax.all_to_all(jnp.broadcast_to(shrunk_partial[None], (tp_size,) + shrunk...  4.04 us
    reduce_sum x1, other arithmetic, shards(): jnp.sum(incoming, axis=0)  3.69 us
  transfers between devices with their start and end apart: 4, of which 3 were waited for; matrix products, arithmetic and copies ran while one was open for 13% of the time, Pallas kernels for 0%

profile of v11, /device:TPU:192, one launch (start us, length us, event | category | flops | bytes accessed | tf_op | source)
XLA Modules:
  0.0 103.2 jit_solution(1624782707772255330)
XLA Ops:
  0.0 0.0 copy-start
  0.0 0.8 compare_select_fusion.2
  0.8 1.3 %gather_fusion = s32[8]{0:T(128)S(1)} fusion(s32[128]{0:T(128)} %param.13, s32[1024]{0:T(1024)S(1)} %pad_clamp_fusion), kind=kCustom, calls=%fused_computation | custom fusion | bytes 96 | tf_op jit(solution)/shard_map/gather | solution.py:41
  2.1 0.6 broadcast_in_dim.45
  2.7 4.5 %all-to-all-start.1 = ((s32[4,1,8]{2,1,0:T(1,128)}), s32[4,1,8]{2,1,0:T(1,128)S(1)}, u32[]{:S(2)}, u32[]{:S(2)}) async-start(s32[4,1,8]{2,1,0:T(1,128)} %broadcast_in_dim.45), calls=%async_computation.1 | async-start | bytes 4096 | tf_op jit(solution)/shard_map/all_to_all | solution.py:59
  7.2 0.0 copy-done
  7.2 5.9 %fusion.19 = f32[1024,1024]{0,1:T(8,128)} fusion(bf16[1024,896]{1,0:T(8,128)(2,1)S(1)} %copy-done, bf16[896,1024]{1,0:T(8,128)(2,1)} %param.8), kind=kOutput, calls=%fused_computation.50 | convolution fusion | flops 1879048192 | bytes 7864320 | tf_op jit(solution)/shard_map/dot_general | solution.py:44
  13.0 0.0 all-to-all-done.1
  13.0 0.0 copy-start.1
  13.0 0.0 copy-start.2
  13.0 5.0 %all-to-all-start = ((f32[4,1024,256]{1,2,0:T(8,128)}), f32[4,1024,256]{1,2,0:T(8,128)}, u32[]{:S(2)}, u32[]{:S(2)}) async-start(f32[4,1024,256]{1,2,0:T(8,128)} %bitcast.38), calls=%async_computation | async-start | bytes 8388608 | tf_op jit(solution)/shard_map/all_to_all | solution.py:46
  18.0 0.0 copy-done.1
  18.0 0.0 copy-done.2
  18.1 31.1 %all_gather.3 = bf16[16,16,1152]{2,1,0:T(8,128)(2,1)S(1)} all-gather(bf16[1,16,1152]{2,1,0:T(8,128)(2,1)S(1)} %pad_maximum_fusion.1), channel_id=1, replica_groups=mesh['y'=4,'z'=16,'c'=2,'tp'=4] {'z'}, dimensions={0}, use_global_device_ids=true | all-gather | bytes 626688 | tf_op jit(solution)/shard_map/all_gather | solution.py:50
  49.1 1.9 %collective-permute-start = (bf16[16,16,1152]{2,1,0:T(8,128)(2,1)S(1)}, bf16[16,16,1152]{2,1,0:T(8,128)(2,1)S(1)}, u32[]{:S(2)}, u32[]{:S(2)}) collective-permute-start(bf16[16,16,1152]{2,1,0:T(8,128)(2,1)S(1)} %all_gather.3), channel_id=1, source_target_pairs={{0,4},{4,0},{1,5},{5,1},{2,6},{6,2},{3,7},{7,3},{8,12},{12,8},{9,1... | collective-permute-start | bytes 1769480 | tf_op jit(solution)/shard_map/ppermute | solution.py:55
  51.0 0.5 broadcast.294
  51.5 0.7 reduce.3
  52.2 0.1 reshape.258
  52.4 0.6 collective-permute-done
  53.0 1.2 %pad_maximum_fusion = bf16[2,16,16,1152]{3,2,1,0:T(8,128)(2,1)} fusion(bf16[1,16,16,1152]{3,2,1,0:T(8,128)(2,1)S(1)} %bitcast.40, bf16[1,16,16,1152]{3,2,1,0:T(8,128)(2,1)S(1)} %bitcast.39), kind=kLoop, calls=%fused_computation.3 | loop fusion | flops 589824 | bytes 2359296 | tf_op jit(solution)/shard_map/stack | solution.py:52
  54.2 12.7 %all-to-all-done = f32[4,1024,256]{1,2,0:T(8,128)} async-done(((f32[4,1024,256]{1,2,0:T(8,128)}), f32[4,1024,256]{1,2,0:T(8,128)}, u32[]{:S(2)}, u32[]{:S(2)}) %all-to-all-start) | async-done | bytes 4194336 | tf_op jit(solution)/shard_map/all_to_all | solution.py:46
  66.9 2.0 %gather_fusion.1 = bf16[32,16,1152]{2,1,0:T(8,128)(2,1)S(1)} fusion(bf16[2,16,16,1152]{3,2,1,0:T(8,128)(2,1)} %pad_maximum_fusion, s32[32]{0:T(128)S(1)} %fusion.18), kind=kCustom, calls=%fused_computation.1 | custom fusion | bytes 2359552 | tf_op jit(solution)/shard_map/gather | solution.py:17
  68.9 0.2 broadcast_select_fusion
  69.1 19.4 %all_to_all.21 = bf16[4,8,16,1152]{3,2,1,0:T(8,128)(2,1)S(1)} all-to-all(bf16[4,8,16,1152]{3,2,1,0:T(8,128)(2,1)S(1)} %broadcast_select_fusion), channel_id=1, replica_groups=mesh['y'=4,'z'=16,'c'=2,'tp'=4] {'y'}, dimensions={0} | all-to-all | bytes 2359296 | tf_op jit(solution)/shard_map/all_to_all | solution.py:69
  88.5 0.2 reduce_sum.28
  88.7 0.0 copy-start.3
  88.7 0.6 convolution_bitcast_fusion
  89.3 0.7 broadcast_in_dim.49
  90.1 4.0 %all-to-all-start.3 = ((f32[4,1024,16]{1,2,0:T(8,128)}), f32[4,1024,16]{1,2,0:T(8,128)}, u32[]{:S(2)}, u32[]{:S(2)}) async-start(f32[4,1024,16]{1,2,0:T(8,128)} %broadcast_in_dim.49), calls=%async_computation.3 | async-start | bytes 524288 | tf_op jit(solution)/shard_map/all_to_all | solution.py:81
  94.1 0.0 copy-done.3
  94.1 0.1 fusion.6
  94.2 3.7 %reduce_sum.27 = f32[1024,256]{0,1:T(8,128)} reduce(f32[4,1024,256]{1,2,0:T(8,128)} %all-to-all-done, f32[]{:T(128)} %constant.61.clone.1), dimensions={0}, to_apply=%region_0.0 | reduce | flops 786432 | bytes 5242884 | tf_op jit(solution)/shard_map/reduce_sum | solution.py:64
  97.9 1.6 %copy.11 = f32[1024,256]{1,0:T(8,128)S(1)} copy(f32[1024,256]{0,1:T(8,128)} %reduce_sum.27) | data formatting | bytes 2097152 | tf_op jit(solution)/shard_map/reduce_sum | solution.py:64
  99.5 1.4 %all-to-all-done.3 = f32[4,1024,16]{1,2,0:T(8,128)} async-done(((f32[4,1024,16]{1,2,0:T(8,128)}), f32[4,1024,16]{1,2,0:T(8,128)}, u32[]{:S(2)}, u32[]{:S(2)}) %all-to-all-start.3) | async-done | bytes 262176 | tf_op jit(solution)/shard_map/all_to_all | solution.py:81
  100.9 1.0 reduce_sum.29
  101.8 0.3 convolution_multiply_fusion
  102.2 1.0 fusion.1
  (5 shorter events, 0.1 us)
Async XLA Ops:
  0.0 7.2 %copy-start = (bf16[1024,896]{1,0:T(8,128)(2,1)S(1)}, bf16[1024,896]{1,0:T(8,128)(2,1)}, u32[]{:S(2)}) copy-start(bf16[1024,896]{1,0:T(8,128)(2,1)} %param.7) | copy-start | bytes 5505028
  2.7 10.3 %all-to-all-start.1 = ((s32[4,1,8]{2,1,0:T(1,128)}), s32[4,1,8]{2,1,0:T(1,128)S(1)}, u32[]{:S(2)}, u32[]{:S(2)}) async-start(s32[4,1,8]{2,1,0:T(1,128)} %broadcast_in_dim.45), calls=%async_computation.1 | async-start | bytes 4096 | tf_op jit(solution)/shard_map/all_to_all | solution.py:59
  13.0 5.0 %copy-start.1 = (bf16[1,16,896]{2,1,0:T(8,128)(2,1)S(1)}, bf16[1,16,896]{2,1,0:T(8,128)(2,1)}, u32[]{:S(2)}) copy-start(bf16[1,16,896]{2,1,0:T(8,128)(2,1)} %param.9) | copy-start | bytes 86020
  13.0 5.0 %copy-start.2 = (bf16[1,16,256]{2,1,0:T(8,128)(2,1)S(1)}, bf16[1,16,256]{2,1,0:T(8,128)(2,1)}, u32[]{:S(2)}) copy-start(bf16[1,16,256]{2,1,0:T(8,128)(2,1)} %param.10) | copy-start | bytes 24580
  13.0 53.9 %all-to-all-start = ((f32[4,1024,256]{1,2,0:T(8,128)}), f32[4,1024,256]{1,2,0:T(8,128)}, u32[]{:S(2)}, u32[]{:S(2)}) async-start(f32[4,1024,256]{1,2,0:T(8,128)} %bitcast.38), calls=%async_computation | async-start | bytes 8388608 | tf_op jit(solution)/shard_map/all_to_all | solution.py:46
  49.1 3.9 %collective-permute-start = (bf16[16,16,1152]{2,1,0:T(8,128)(2,1)S(1)}, bf16[16,16,1152]{2,1,0:T(8,128)(2,1)S(1)}, u32[]{:S(2)}, u32[]{:S(2)}) collective-permute-start(bf16[16,16,1152]{2,1,0:T(8,128)(2,1)S(1)} %all_gather.3), channel_id=1, source_target_pairs={{0,4},{4,0},{1,5},{5,1},{2,6},{6,2},{3,7},{7,3},{8,12},{12,8},{9,1... | collective-permute-start | bytes 1769480 | tf_op jit(solution)/shard_map/ppermute | solution.py:55
  88.7 5.5 %copy-start.3 = (s32[8]{0:T(128)S(1)}, s32[8]{0:T(128)}, u32[]{:S(2)}) copy-start(s32[8]{0:T(128)} %param.12) | copy-start | bytes 100
  90.1 10.8 %all-to-all-start.3 = ((f32[4,1024,16]{1,2,0:T(8,128)}), f32[4,1024,16]{1,2,0:T(8,128)}, u32[]{:S(2)}, u32[]{:S(2)}) async-start(f32[4,1024,16]{1,2,0:T(8,128)} %broadcast_in_dim.49), calls=%async_computation.3 | async-start | bytes 524288 | tf_op jit(solution)/shard_map/all_to_all | solution.py:81

commit v12 on v11

--- a/solution.py
+++ b/solution.py
@@ -69,6 +69,7 @@
     received = lax.all_to_all(
         sent.reshape((y_size, blocks_dev) + sent.shape[1:]), "y", 0, 0, tiled=False
     )
+    received, base_result = lax.optimization_barrier((received, base_result))
     chosen_maps = jnp.sum(received, axis=0, dtype=received.dtype)
     chosen_down_maps = chosen_maps[:, :, :width_dev]
     chosen_up_maps = chosen_maps[:, :, width_dev:]

time: 104 us -> 103 us (level)
  the two profiles are of different devices: /device:TPU:192 before, /device:TPU:416 now
where the time goes in v12:
time: 103 us
  blocking collectives  30.4 us (30%)
  waiting for transfers between devices  29.3 us (28%)
  starting transfers between devices  19.3 us (19%)
  other arithmetic  8.97 us (9%)
  local copies, waits for them, and re-layouts  7.78 us (8%)
  matrix products  6.85 us (7%)
    all_gather x1, blocking collectives, shards(): column = lax.all_gather(both_maps, 'z', axis=0, tiled=True)  30.4 us
    all_to_all x1, waiting for transfers between devices, shards(): incoming = lax.all_to_all(outgoing, 'tp', 0, 0, tiled=False)  13.3 us
    all_to_all x1, waiting for transfers between devices, shards(): lax.all_to_all(sent.reshape((y_size, blocks_dev) + sent.shape[1:]), 'y',...  8.83 us
    all_to_all x1, waiting for transfers between devices, shards(): lax.all_to_all(jnp.broadcast_to(shrunk_partial[None], (tp_size,) + shrunk...  6.56 us
    dot_general x1, matrix products, shards(): jnp.dot(tokens, key_value_weight, preferred_element_type=jnp.float32)  5.86 us
    all_to_all x1, starting transfers between devices, shards(): incoming = lax.all_to_all(outgoing, 'tp', 0, 0, tiled=False)  4.98 us
    all_to_all x1, starting transfers between devices, shards(): lax.all_to_all(sent.reshape((y_size, blocks_dev) + sent.shape[1:]), 'y',...  4.52 us
    all_to_all x1, starting transfers between devices, shards(): lax.all_to_all(jnp.broadcast_to(slot_ids[None], (y_size, blocks_dev)), 'y...  4.46 us
  transfers between devices with their start and end apart: 5, of which 4 were waited for; matrix products, arithmetic and copies ran while one was open for 14% of the time, Pallas kernels for 0%

profile of v12, /device:TPU:416, one launch (start us, length us, event | category | flops | bytes accessed | tf_op | source)
XLA Modules:
  0.0 102.7 jit_solution(1394720287949011068)
XLA Ops:
  0.0 0.0 copy-start
  0.0 0.8 compare_select_fusion.2
  0.8 1.3 %gather_fusion = s32[8]{0:T(128)S(1)} fusion(s32[128]{0:T(128)} %param.13, s32[1024]{0:T(1024)S(1)} %pad_clamp_fusion), kind=kCustom, calls=%fused_computation | custom fusion | bytes 96 | tf_op jit(solution)/shard_map/gather | solution.py:41
  2.1 0.6 broadcast_in_dim.45
  2.7 4.5 %all-to-all-start = ((s32[4,1,8]{2,1,0:T(1,128)}), s32[4,1,8]{2,1,0:T(1,128)S(1)}, u32[]{:S(2)}, u32[]{:S(2)}) async-start(s32[4,1,8]{2,1,0:T(1,128)} %broadcast_in_dim.45), calls=%async_computation | async-start | bytes 4096 | tf_op jit(solution)/shard_map/all_to_all | solution.py:59
  7.2 0.0 copy-done
  7.2 5.9 %fusion.19 = f32[1024,1024]{0,1:T(8,128)} fusion(bf16[1024,896]{1,0:T(8,128)(2,1)S(1)} %copy-done, bf16[896,1024]{1,0:T(8,128)(2,1)} %param.8), kind=kOutput, calls=%fused_computation.50 | convolution fusion | flops 1879048192 | bytes 7864320 | tf_op jit(solution)/shard_map/dot_general | solution.py:44
  13.0 0.0 all-to-all-done
  13.0 0.0 copy-start.2
  13.0 0.0 copy-start.3
  13.0 5.0 %all-to-all-start.1 = ((f32[4,1024,256]{1,2,0:T(8,128)}), f32[4,1024,256]{1,2,0:T(8,128)}, u32[]{:S(2)}, u32[]{:S(2)}) async-start(f32[4,1024,256]{1,2,0:T(8,128)} %bitcast.38), calls=%async_computation.1 | async-start | bytes 8388608 | tf_op jit(solution)/shard_map/all_to_all | solution.py:46
  18.0 0.0 copy-done.2
  18.0 0.0 copy-done.3
  18.0 30.4 %all_gather.3 = bf16[16,16,1152]{2,1,0:T(8,128)(2,1)S(1)} all-gather(bf16[1,16,1152]{2,1,0:T(8,128)(2,1)S(1)} %pad_maximum_fusion.1), channel_id=1, replica_groups=mesh['y'=4,'z'=16,'c'=2,'tp'=4] {'z'}, dimensions={0}, use_global_device_ids=true | all-gather | bytes 626688 | tf_op jit(solution)/shard_map/all_gather | solution.py:50
  48.5 1.9 %collective-permute-start = (bf16[16,16,1152]{2,1,0:T(8,128)(2,1)S(1)}, bf16[16,16,1152]{2,1,0:T(8,128)(2,1)S(1)}, u32[]{:S(2)}, u32[]{:S(2)}) collective-permute-start(bf16[16,16,1152]{2,1,0:T(8,128)(2,1)S(1)} %all_gather.3), channel_id=1, source_target_pairs={{0,4},{4,0},{1,5},{5,1},{2,6},{6,2},{3,7},{7,3},{8,12},{12,8},{9,1... | collective-permute-start | bytes 1769480 | tf_op jit(solution)/shard_map/ppermute | solution.py:55
  50.4 0.5 broadcast.294
  50.9 0.7 reduce.3
  51.6 0.1 reshape.258
  51.7 0.6 collective-permute-done
  52.4 1.2 %pad_maximum_fusion = bf16[2,16,16,1152]{3,2,1,0:T(8,128)(2,1)} fusion(bf16[1,16,16,1152]{3,2,1,0:T(8,128)(2,1)S(1)} %bitcast.40, bf16[1,16,16,1152]{3,2,1,0:T(8,128)(2,1)S(1)} %bitcast.39), kind=kLoop, calls=%fused_computation.3 | loop fusion | flops 589824 | bytes 2359296 | tf_op jit(solution)/shard_map/stack | solution.py:52
  53.6 13.3 %all-to-all-done.1 = f32[4,1024,256]{1,2,0:T(8,128)} async-done(((f32[4,1024,256]{1,2,0:T(8,128)}), f32[4,1024,256]{1,2,0:T(8,128)}, u32[]{:S(2)}, u32[]{:S(2)}) %all-to-all-start.1) | async-done | bytes 4194336 | tf_op jit(solution)/shard_map/all_to_all | solution.py:46
  66.9 2.0 %gather_fusion.1 = bf16[32,16,1152]{2,1,0:T(8,128)(2,1)S(1)} fusion(bf16[2,16,16,1152]{3,2,1,0:T(8,128)(2,1)} %pad_maximum_fusion, s32[32]{0:T(128)S(1)} %fusion.18), kind=kCustom, calls=%fused_computation.1 | custom fusion | bytes 2359552 | tf_op jit(solution)/shard_map/gather | solution.py:17
  68.9 1.2 %broadcast_select_fusion = bf16[4,8,16,1152]{3,2,1,0:T(8,128)(2,1)} fusion(bf16[4,8,16,1152]{3,2,1,0:T(8,128)(2,1)S(1)} %bitcast.37, pred[4,8]{1,0:T(4,128)(4,1)S(1)} %fusion.8), kind=kLoop, calls=%fused_computation.4 | loop fusion | flops 589824 | bytes 2359328 | tf_op jit(solution)/shard_map/jit(_where)/select_n | solution.py:19
  70.1 4.5 %all-to-all-start.2 = ((bf16[4,8,16,1152]{3,2,1,0:T(8,128)(2,1)}), bf16[4,8,16,1152]{3,2,1,0:T(8,128)(2,1)S(1)}, u32[]{:S(2)}, u32[]{:S(2)}) async-start(bf16[4,8,16,1152]{3,2,1,0:T(8,128)(2,1)} %broadcast_select_fusion), calls=%async_computation.2 | async-start | bytes 2359296 | tf_op jit(solution)/shard_map/all_to_all | solution.py:69
  74.6 3.7 %reduce_sum.27 = f32[1024,256]{0,1:T(8,128)} reduce(f32[4,1024,256]{1,2,0:T(8,128)} %all-to-all-done.1, f32[]{:T(128)} %constant.75.clone.1), dimensions={0}, to_apply=%region_0.0 | reduce | flops 786432 | bytes 5242884 | tf_op jit(solution)/shard_map/reduce_sum | solution.py:64
  78.3 2.5 %copy.11 = f32[1024,256]{1,0:T(8,128)} copy(f32[1024,256]{0,1:T(8,128)} %reduce_sum.27) | data formatting | bytes 2097152 | tf_op jit(solution)/shard_map/reduce_sum | solution.py:64
  80.8 8.8 %all-to-all-done.2 = bf16[4,8,16,1152]{3,2,1,0:T(8,128)(2,1)S(1)} async-done(((bf16[4,8,16,1152]{3,2,1,0:T(8,128)(2,1)}), bf16[4,8,16,1152]{3,2,1,0:T(8,128)(2,1)S(1)}, u32[]{:S(2)}, u32[]{:S(2)}) %all-to-all-start.2) | async-done | bytes 1179680 | tf_op jit(solution)/shard_map/all_to_all | solution.py:69
  89.7 0.2 reduce_sum.28
  89.9 0.0 copy-start.4
  89.9 0.0 copy-start.1
  89.9 0.6 convolution_bitcast_fusion
  90.5 0.7 broadcast_in_dim.49
  91.3 3.4 %all-to-all-start.3 = ((f32[4,1024,16]{1,2,0:T(8,128)}), f32[4,1024,16]{1,2,0:T(8,128)S(1)}, u32[]{:S(2)}, u32[]{:S(2)}) async-start(f32[4,1024,16]{1,2,0:T(8,128)} %broadcast_in_dim.49), calls=%async_computation.3 | async-start | bytes 524288 | tf_op jit(solution)/shard_map/all_to_all | solution.py:82
  94.7 0.0 copy-done.4
  94.7 0.1 fusion.6
  94.8 6.6 %all-to-all-done.3 = f32[4,1024,16]{1,2,0:T(8,128)S(1)} async-done(((f32[4,1024,16]{1,2,0:T(8,128)}), f32[4,1024,16]{1,2,0:T(8,128)S(1)}, u32[]{:S(2)}, u32[]{:S(2)}) %all-to-all-start.3) | async-done | bytes 262176 | tf_op jit(solution)/shard_map/all_to_all | solution.py:82
  101.3 0.3 convolution_multiply_fusion
  101.7 0.0 copy-done.1
  101.7 1.0 %fusion.1 = bf16[1024,256]{1,0:T(8,128)(2,1)} fusion(f32[1024,256]{1,0:T(8,128)S(1)} %copy-done.1, f32[8,128,256]{2,1,0:T(8,128)S(1)} %convolution_multiply_fusion, pred[1024]{0:T(1024)(128)(4,1)S(1)} %fusion.6), kind=kLoop, calls=%fused_computation.8 | loop fusion | flops 786432 | bytes 2622464 | tf_op jit(solution)/shard_map/convert_element_type | solution.py:100
  (6 shorter events, 0.1 us)
Async XLA Ops:
  0.0 7.2 %copy-start = (bf16[1024,896]{1,0:T(8,128)(2,1)S(1)}, bf16[1024,896]{1,0:T(8,128)(2,1)}, u32[]{:S(2)}) copy-start(bf16[1024,896]{1,0:T(8,128)(2,1)} %param.7) | copy-start | bytes 5505028
  2.7 10.3 %all-to-all-start = ((s32[4,1,8]{2,1,0:T(1,128)}), s32[4,1,8]{2,1,0:T(1,128)S(1)}, u32[]{:S(2)}, u32[]{:S(2)}) async-start(s32[4,1,8]{2,1,0:T(1,128)} %broadcast_in_dim.45), calls=%async_computation | async-start | bytes 4096 | tf_op jit(solution)/shard_map/all_to_all | solution.py:59
  13.0 5.0 %copy-start.2 = (bf16[1,16,896]{2,1,0:T(8,128)(2,1)S(1)}, bf16[1,16,896]{2,1,0:T(8,128)(2,1)}, u32[]{:S(2)}) copy-start(bf16[1,16,896]{2,1,0:T(8,128)(2,1)} %param.9) | copy-start | bytes 86020
  13.0 5.0 %copy-start.3 = (bf16[1,16,256]{2,1,0:T(8,128)(2,1)S(1)}, bf16[1,16,256]{2,1,0:T(8,128)(2,1)}, u32[]{:S(2)}) copy-start(bf16[1,16,256]{2,1,0:T(8,128)(2,1)} %param.10) | copy-start | bytes 24580
  13.0 53.8 %all-to-all-start.1 = ((f32[4,1024,256]{1,2,0:T(8,128)}), f32[4,1024,256]{1,2,0:T(8,128)}, u32[]{:S(2)}, u32[]{:S(2)}) async-start(f32[4,1024,256]{1,2,0:T(8,128)} %bitcast.38), calls=%async_computation.1 | async-start | bytes 8388608 | tf_op jit(solution)/shard_map/all_to_all | solution.py:46
  48.5 3.9 %collective-permute-start = (bf16[16,16,1152]{2,1,0:T(8,128)(2,1)S(1)}, bf16[16,16,1152]{2,1,0:T(8,128)(2,1)S(1)}, u32[]{:S(2)}, u32[]{:S(2)}) collective-permute-start(bf16[16,16,1152]{2,1,0:T(8,128)(2,1)S(1)} %all_gather.3), channel_id=1, source_target_pairs={{0,4},{4,0},{1,5},{5,1},{2,6},{6,2},{3,7},{7,3},{8,12},{12,8},{9,1... | collective-permute-start | bytes 1769480 | tf_op jit(solution)/shard_map/ppermute | solution.py:55
  70.1 19.6 %all-to-all-start.2 = ((bf16[4,8,16,1152]{3,2,1,0:T(8,128)(2,1)}), bf16[4,8,16,1152]{3,2,1,0:T(8,128)(2,1)S(1)}, u32[]{:S(2)}, u32[]{:S(2)}) async-start(bf16[4,8,16,1152]{3,2,1,0:T(8,128)(2,1)} %broadcast_select_fusion), calls=%async_computation.2 | async-start | bytes 2359296 | tf_op jit(solution)/shard_map/all_to_all | solution.py:69
  89.9 4.8 %copy-start.4 = (s32[8]{0:T(128)S(1)}, s32[8]{0:T(128)}, u32[]{:S(2)}) copy-start(s32[8]{0:T(128)} %param.12) | copy-start | bytes 100
  89.9 11.8 %copy-start.1 = (f32[1024,256]{1,0:T(8,128)S(1)}, f32[1024,256]{1,0:T(8,128)}, u32[]{:S(2)}) copy-start(f32[1024,256]{1,0:T(8,128)} %copy.11) | copy-start | bytes 3145732
  91.3 10.1 %all-to-all-start.3 = ((f32[4,1024,16]{1,2,0:T(8,128)}), f32[4,1024,16]{1,2,0:T(8,128)S(1)}, u32[]{:S(2)}, u32[]{:S(2)}) async-start(f32[4,1024,16]{1,2,0:T(8,128)} %broadcast_in_dim.49), calls=%async_computation.3 | async-start | bytes 524288 | tf_op jit(solution)/shard_map/all_to_all | solution.py:82
